TPU v7x, 128 devices: a whole 4x4x4 slice. The times are simulated.
128 devices in a mesh: dom: 32 (over y, x, core), ref: 4 (over z).
Axes of the slice: x: 4, y: 4, z: 4, core: 2. Of those that a mesh axis runs over, the one named last changes fastest.
Arguments:
- particles: bfloat16 [32768, 16384], P(('dom', 'ref')), may hold values from -12 to 12
- noise_prec: bfloat16 [32768], P(('dom', 'ref')), may hold values from 0.25 to 2
- prior_pose: int32 [32768], P(('dom', 'ref')), may hold values from 0 to 4607
- owners: int32 [32768], P(('dom', 'ref')), may hold values from 0 to 31, as said below
- projections: bfloat16 [32, 64, 16384], P('ref', 'dom'), may hold values from -4 to 4
- pose_index: int32 [64], P('dom'), may hold values from 0 to 4607
Outputs:
- class_prob: float32 [32768, 32], P(('dom', 'ref'))
- log_like: float32 [32768], P(('dom', 'ref'))
- class_sums: bfloat16 [32, 64, 16384], P('ref', 'dom')
- weight_totals: float32 [32, 64], P('ref', 'dom')
Inputs may be any that keep to these rules, and one draw needn't show every extreme that they name: `owners`: the particles of one device name each owner at most 10 times; in every ref row some owner is named exactly 10 times by every device of that row.
All inputs are finite; a program needn't handle non-finite values.
Results may differ from a plain program's by a relative error of at most 0.015.
Values may be sent and summed in bfloat16 or wider, within the bound.
No kernel may reach another device: no remote copies, remote signals or barrier semaphores. Data moves between devices by JAX's collectives and lax.ppermute only.
A program may use at most 128 MiB of HBM per device.

v0:
```python
import jax
import jax.numpy as jnp
from jax import lax
from jax.sharding import PartitionSpec as P

IMG = 128
SHIFTS = 3
PRIOR_WIDTH = 576


def from_behind(block, axis, distance):
    devices = range(lax.axis_size(axis))
    route = [((i - distance) % len(devices), i) for i in devices]
    return lax.ppermute(block, axis, route)


def translate(images, offset):
    full_shape = images.shape
    squares = images.reshape(full_shape[:-1] + (IMG, IMG))
    return jnp.roll(squares, offset, axis=-1).reshape(full_shape)


def shards(particles, noise_prec, prior_pose, owners, projections, pose_index):
    count_dom = lax.axis_size("dom")
    count_ref = lax.axis_size("ref")
    ref_here = lax.axis_index("ref")
    arrived = particles.shape[0]
    pixels = particles.shape[1]
    capacity = (5 * arrived + 4 * count_dom - 1) // (4 * count_dom)
    slot_count = count_dom * capacity
    earlier = jnp.arange(arrived)[:, None] > jnp.arange(arrived)[None, :]
    same_owner = owners[:, None] == owners[None, :]
    slot_rank = jnp.sum(same_owner & earlier, axis=1)
    slot_of = owners * capacity + slot_rank
    source = (
        jnp.full((slot_count,), arrived, jnp.int32)
        .at[slot_of]
        .set(jnp.arange(arrived, dtype=jnp.int32))
    )
    filled = source < arrived
    safe_source = jnp.minimum(source, arrived - 1)
    send_img = jnp.where(
        filled[:, None], particles[safe_source], jnp.zeros((), particles.dtype)
    ).reshape(count_dom, capacity, pixels)
    send_prec = jnp.where(filled, noise_prec[safe_source], jnp.zeros((), noise_prec.dtype)).reshape(
        count_dom, capacity
    )
    send_prior = jnp.where(filled, prior_pose[safe_source], -1).reshape(count_dom, capacity)
    got_img, got_prec, got_prior = (
        lax.all_to_all(send_img, "dom", split_axis=0, concat_axis=0, tiled=True),
        lax.all_to_all(send_prec, "dom", split_axis=0, concat_axis=0, tiled=True),
        lax.all_to_all(send_prior, "dom", split_axis=0, concat_axis=0, tiled=True),
    )
    images = got_img.reshape(slot_count, pixels)
    precision = got_prec.reshape(slot_count).astype(jnp.float32)
    prior_ids = got_prior.reshape(slot_count)
    live_slot = (prior_ids >= 0).astype(jnp.float32)
    offsets = [u - SHIFTS // 2 for u in range(SHIFTS)]
    own_proj = projections.reshape(-1, pixels)
    block_rows = own_proj.shape[0]
    per_class = projections.shape[1]
    log_prior = -jnp.abs(pose_index[None, :] - prior_ids[:, None]).astype(jnp.float32) / PRIOR_WIDTH
    prior_rows = jnp.tile(log_prior, (1, block_rows // per_class))

    def block_scores(proj_block):
        shifted = jnp.stack([translate(proj_block, -t) for t in offsets]).reshape(
            SHIFTS * block_rows, pixels
        )
        correlation = lax.dot_general(
            images, shifted, (((1,), (1,)), ((), ())), preferred_element_type=jnp.float32
        )
        correlation = correlation.reshape(slot_count, SHIFTS, block_rows)
        norms = jnp.sum(jnp.square(proj_block.astype(jnp.float32)), axis=1)
        scaled = correlation / IMG - norms[None, None, :] / (2.0 * IMG * IMG)
        return precision[:, None, None] * scaled + prior_rows[:, None, :]

    scores = jnp.zeros((count_ref, slot_count, SHIFTS, block_rows), jnp.float32)
    scores = lax.dynamic_update_index_in_dim(scores, block_scores(own_proj), ref_here, 0)
    moving = own_proj
    for k in range(1, count_ref):
        moving = from_behind(moving, "ref", 1)
        scores = lax.dynamic_update_index_in_dim(
            scores, block_scores(moving), (ref_here - k) % count_ref, 0
        )
    highest = jnp.max(scores, axis=(0, 2, 3))
    loglike = highest + jnp.log(
        jnp.sum(jnp.exp(scores - highest[None, :, None, None]), axis=(0, 2, 3))
    )
    weights = jnp.exp(scores - loglike[None, :, None, None]) * live_slot[None, :, None, None]
    class_post = jnp.sum(
        weights.reshape(count_ref, slot_count, SHIFTS, block_rows // per_class, per_class),
        axis=(2, 4),
    )
    class_post = jnp.transpose(class_post, (1, 0, 2)).reshape(slot_count, -1)
    low_weights = jnp.transpose(weights, (0, 2, 1, 3)).astype(jnp.bfloat16)
    block_totals = jnp.sum(weights, axis=(1, 2))
    for k in range(count_ref):
        target = (ref_here - k - 1) % count_ref
        per_shift = jnp.einsum(
            "nusr,sp->unrp",
            lax.dynamic_index_in_dim(low_weights, target, 0, keepdims=True),
            images,
            preferred_element_type=jnp.float32,
        )
        summed = translate(per_shift[0], offsets[0])
        for block_u in range(1, SHIFTS):
            summed = summed + translate(per_shift[block_u], offsets[block_u])
        partial_value = summed.reshape(-1, pixels)
        partial_value = lax.optimization_barrier(partial_value.astype(jnp.bfloat16)).astype(
            jnp.float32
        )
        partial_total = lax.dynamic_index_in_dim(block_totals, target, 0, keepdims=False)
        if k == 0:
            carried = partial_value
            carried_total = partial_total
        else:
            carried = carried + partial_value
            carried_total = carried_total + partial_total
        if k < count_ref - 1:
            carried, carried_total = (
                from_behind(carried.astype(jnp.bfloat16), "ref", 1).astype(carried.dtype),
                from_behind(carried_total.astype(jnp.bfloat16), "ref", 1).astype(
                    carried_total.dtype
                ),
            )
    class_sums = carried.astype(jnp.bfloat16).reshape(projections.shape)
    weight_totals = carried_total.reshape(projections.shape[0], projections.shape[1])
    back_prob, back_like = (
        lax.all_to_all(
            class_post.reshape(count_dom, capacity, -1).astype(jnp.bfloat16),
            "dom",
            split_axis=0,
            concat_axis=0,
            tiled=True,
        ).astype(jnp.float32),
        lax.all_to_all(
            loglike.reshape(count_dom, capacity).astype(jnp.bfloat16),
            "dom",
            split_axis=0,
            concat_axis=0,
            tiled=True,
        ).astype(jnp.float32),
    )
    class_prob = back_prob[owners, slot_rank]
    log_like = back_like[owners, slot_rank]
    return (class_prob, log_like, class_sums, weight_totals)


def solution(mesh):
    in_specs = (
        P(("dom", "ref"), None),
        P(("dom", "ref")),
        P(("dom", "ref")),
        P(("dom", "ref")),
        P("ref", "dom", None),
        P("dom"),
    )
    out_specs = (P(("dom", "ref"), None), P(("dom", "ref")), P("ref", "dom", None), P("ref", "dom"))
    return jax.shard_map(shards, mesh=mesh, in_specs=in_specs, out_specs=out_specs, check_vma=False)
```

profile of v0, /device:TPU:0, one launch (start us, length us, event | category | flops | bytes accessed | tf_op | source)
XLA Modules:
  0.0 415.6 jit_solution(1094140482144887348)
XLA Ops:
  2.3 1.4 scatter_custom_fusion
  3.7 3.5 gather_fusion
  7.9 7.4 %all-to-all-start = ((bf16[32,1,10]{2,1,0:T(2,128)(2,1)}), bf16[32,1,10]{2,1,0:T(2,128)(2,1)S(1)}, u32[]{:S(2)}, u32[]{:S(2)}) async-start(bf16[32,1,10]{2,1,0:T(2,128)(2,1)} %all_to_all.29), calls=%async_computation | async-start | bytes 32768 | tf_op jit(solution)/shard_map/all_to_all | solution.py:51
  15.3 2.5 gather_fusion.2
  17.9 32.3 %gather_fusion.1 = bf16[320,16384]{1,0:T(8,128)(2,1)} fusion(bf16[256,16384]{1,0:T(8,128)(2,1)} %param.6, s32[1024]{0:T(1024)S(1)} %pad_clamp_fusion), kind=kCustom, calls=%fused_computation.1 | custom fusion | bytes 20972800 | tf_op jit(solution)/shard_map/gather | solution.py:43
  50.2 12.7 %gather.19 = bf16[32,10,16384]{2,1,0:T(8,128)(2,1)} reshape(bf16[320,16384]{1,0:T(8,128)(2,1)} %gather_fusion.1) | data formatting | bytes 20971520 | tf_op jit(solution)/shard_map/gather | solution.py:43
  63.6 7.4 %all-to-all-start.2 = ((s32[32,1,10]{2,1,0:T(1,128)}), s32[32,1,10]{2,1,0:T(1,128)S(1)}, u32[]{:S(2)}, u32[]{:S(2)}) async-start(s32[32,1,10]{2,1,0:T(1,128)} %bitcast), calls=%async_computation.2 | async-start | bytes 32768 | tf_op jit(solution)/shard_map/all_to_all | solution.py:52
  71.0 14.0 %broadcast_select_fusion = bf16[32,10,16384]{2,1,0:T(8,128)(2,1)} fusion(bf16[32,10,16384]{2,1,0:T(8,128)(2,1)} %gather.19, pred[32,10]{1,0:T(8,128)(4,1)S(1)} %broadcast_in_dim.73), kind=kLoop, calls=%fused_computation.6 | loop fusion | flops 5242880 | bytes 20971840 | tf_op jit(solution)/shard_map/jit(_where)/select_n | solution.py:42
  85.0 7.6 %all-to-all-start.1 = ((bf16[32,10,16384]{2,1,0:T(8,128)(2,1)}), bf16[32,10,16384]{2,1,0:T(8,128)(2,1)}, u32[]{:S(2)}, u32[]{:S(2)}) async-start(bf16[32,10,16384]{2,1,0:T(8,128)(2,1)} %broadcast_select_fusion), calls=%async_computation.1 | async-start | bytes 33554432 | tf_op jit(solution)/shard_map/all_to_all | solution.py:50
  92.9 2.0 collective-permute-start
  95.2 1.0 stack_reshape.37
  97.4 1.0 stack_reshape.36
  98.4 1.0 stack_reshape.38
  101.8 7.5 %collective-permute-done = bf16[16,16384]{1,0:T(8,128)(2,1)S(1)} collective-permute-done((bf16[16,16384]{1,0:T(8,128)(2,1)S(1)}, bf16[16,16384]{1,0:T(8,128)(2,1)S(1)}, u32[]{:S(2)}, u32[]{:S(2)}) %collective-permute-start) | collective-permute-done | bytes 524320 | tf_op jit(solution)/shard_map/ppermute | solution.py:14
  110.5 1.0 stack_reshape.39
  111.5 1.0 stack_reshape.41
  112.8 11.5 %collective-permute-done.1 = bf16[16,16384]{1,0:T(8,128)(2,1)S(1)} collective-permute-done((bf16[16,16384]{1,0:T(8,128)(2,1)S(1)}, bf16[16,16384]{1,0:T(8,128)(2,1)S(1)}, u32[]{:S(2)}, u32[]{:S(2)}) %collective-permute-start.1) | collective-permute-done | bytes 524320 | tf_op jit(solution)/shard_map/ppermute | solution.py:14
  125.5 1.0 stack_reshape.42
  126.6 1.0 stack_reshape.44
  127.9 10.6 %collective-permute-done.2 = bf16[16,16384]{1,0:T(8,128)(2,1)S(1)} collective-permute-done((bf16[16,16384]{1,0:T(8,128)(2,1)S(1)}, bf16[16,16384]{1,0:T(8,128)(2,1)S(1)}, u32[]{:S(2)}, u32[]{:S(2)}) %collective-permute-start.2) | collective-permute-done | bytes 524320 | tf_op jit(solution)/shard_map/ppermute | solution.py:14
  139.7 1.0 stack_reshape.45
  140.7 1.0 stack_reshape.47
  142.0 163.9 %all-to-all-done.1 = bf16[32,10,16384]{2,1,0:T(8,128)(2,1)} async-done(((bf16[32,10,16384]{2,1,0:T(8,128)(2,1)}), bf16[32,10,16384]{2,1,0:T(8,128)(2,1)}, u32[]{:S(2)}, u32[]{:S(2)}) %all-to-all-start.1) | async-done | bytes 10485792 | tf_op jit(solution)/shard_map/all_to_all | solution.py:50
  305.9 13.2 %reshape.390 = bf16[320,16384,1]{1,0,2:T(8,128)(2,1)} reshape(bf16[32,10,16384]{2,1,0:T(8,128)(2,1)} %all-to-all-done.1) | data formatting | bytes 20971520 | tf_op jit(solution)/shard_map/reshape | solution.py:54
  319.1 7.3 %fusion.93 = f32[4,320,3,16]{1,3,2,0:T(8,128)S(1)} fusion(f32[4,320,3,16]{1,3,2,0:T(8,128)S(1)} %broadcast_in_dim.69, s32[]{:T(128)S(6)} %select_n.91, bf16[320,16384,1]{1,0,2:T(8,128)(2,1)} %reshape.390, bf16[1,16,16384]{2,1,0:T(8,128)(2,1)} %stack_reshape.38, bf16[1,16,16384]{2,1,0:T(8,128)(2,1)S(1)} %copy-done.3, ...), kind=kOutput, calls=%fused_computation.54 | convolution fusion | flops 508096512 | bytes 12159492 | tf_op jit(solution)/shard_map/dot_general | solution.py:69
  326.5 3.1 fusion.75
  329.7 3.2 fusion.57
  332.9 3.1 fusion.39
  336.3 2.0 collective-permute-start.6
  338.3 13.1 %reshape.312 = bf16[320,16384]{1,0:T(8,128)(2,1)} reshape(bf16[32,10,16384]{2,1,0:T(8,128)(2,1)} %all-to-all-done.1) | data formatting | bytes 20971520 | tf_op jit(solution)/shard_map/reshape | solution.py:54
  351.4 6.0 %fusion.134 = f32[16384,48]{0,1:S(1)} fusion(bf16[320,48]{0,1:T(8,128)(2,1)S(1)} %bitcast.292, bf16[320,16384]{1,0:T(8,128)(2,1)} %reshape.312), kind=kOutput, calls=%fused_computation.168 | convolution fusion | flops 503316480 | bytes 13662208
  359.3 1.2 fusion.99
  360.6 2.2 collective-permute-start.3
  362.8 2.0 fusion.135
  366.0 2.0 fusion.136
  369.3 2.0 fusion.137
  373.2 1.2 fusion.98
  375.1 1.2 fusion.97
  377.2 1.2 fusion.96
  378.5 1.7 collective-permute-start.4
  382.2 3.8 all-to-all-start.4
  386.9 3.9 collective-permute-done.7
  391.1 4.6 %collective-permute-done.8 = bf16[16]{0:T(256)(128)(2,1)S(1)} collective-permute-done((bf16[16]{0:T(256)(128)(2,1)S(1)}, bf16[16]{0:T(256)(128)(2,1)S(1)}, u32[]{:S(2)}, u32[]{:S(2)}) %collective-permute-start.8) | collective-permute-done | bytes 64 | tf_op jit(solution)/shard_map/ppermute | solution.py:14
  396.4 7.4 %all-to-all-start.3 = ((bf16[32,2,160]{2,1,0:T(2,128)(2,1)}), bf16[32,2,160]{2,1,0:T(2,128)(2,1)S(1)}, u32[]{:S(2)}, u32[]{:S(2)}) async-start(bf16[32,2,160]{2,1,0:T(2,128)(2,1)} %reshape.419), calls=%async_computation.3 | async-start | bytes 65536 | tf_op jit(solution)/shard_map/all_to_all | solution.py:129
  403.8 2.5 gather_fusion.4
  406.4 4.9 %all-to-all-done.3 = bf16[32,2,160]{2,1,0:T(2,128)(2,1)S(1)} async-done(((bf16[32,2,160]{2,1,0:T(2,128)(2,1)}), bf16[32,2,160]{2,1,0:T(2,128)(2,1)S(1)}, u32[]{:S(2)}, u32[]{:S(2)}) %all-to-all-start.3) | async-done | bytes 20512 | tf_op jit(solution)/shard_map/all_to_all | solution.py:129
  411.4 1.8 gather_fusion.3
  414.1 1.1 reshape.333
  (148 shorter events, 24.7 us)
Async XLA Ops:
  0.6 14.7 %copy-start = (s32[256]{0:T(256)S(1)}, s32[256]{0:T(256)}, u32[]{:S(2)}) copy-start(s32[256]{0:T(256)} %param.8) | copy-start | bytes 3076
  7.9 55.7 %all-to-all-start = ((bf16[32,1,10]{2,1,0:T(2,128)(2,1)}), bf16[32,1,10]{2,1,0:T(2,128)(2,1)S(1)}, u32[]{:S(2)}, u32[]{:S(2)}) async-start(bf16[32,1,10]{2,1,0:T(2,128)(2,1)} %all_to_all.29), calls=%async_computation | async-start | bytes 32768 | tf_op jit(solution)/shard_map/all_to_all | solution.py:51
  63.6 21.4 %all-to-all-start.2 = ((s32[32,1,10]{2,1,0:T(1,128)}), s32[32,1,10]{2,1,0:T(1,128)S(1)}, u32[]{:S(2)}, u32[]{:S(2)}) async-start(s32[32,1,10]{2,1,0:T(1,128)} %bitcast), calls=%async_computation.2 | async-start | bytes 32768 | tf_op jit(solution)/shard_map/all_to_all | solution.py:52
  85.0 7.7 %copy-start.2 = (bf16[8,2,16384]{2,1,0:T(2,128)(2,1)S(1)}, bf16[8,2,16384]{2,1,0:T(2,128)(2,1)}, u32[]{:S(2)}) copy-start(bf16[8,2,16384]{2,1,0:T(2,128)(2,1)} %param.10) | copy-start | bytes 1572868
  85.0 220.9 %all-to-all-start.1 = ((bf16[32,10,16384]{2,1,0:T(8,128)(2,1)}), bf16[32,10,16384]{2,1,0:T(8,128)(2,1)}, u32[]{:S(2)}, u32[]{:S(2)}) async-start(bf16[32,10,16384]{2,1,0:T(8,128)(2,1)} %broadcast_select_fusion), calls=%async_computation.1 | async-start | bytes 33554432 | tf_op jit(solution)/shard_map/all_to_all | solution.py:50
  92.9 16.4 %collective-permute-start = (bf16[16,16384]{1,0:T(8,128)(2,1)S(1)}, bf16[16,16384]{1,0:T(8,128)(2,1)S(1)}, u32[]{:S(2)}, u32[]{:S(2)}) collective-permute-start(bf16[16,16384]{1,0:T(8,128)(2,1)S(1)} %reshape.313), channel_id=1, source_target_pairs={{3,0},{0,1},{1,2},{2,3},{7,4},{4,5},{5,6},{6,7},{11,8},{8,9},{9,10... | collective-permute-start | bytes 1572872 | tf_op jit(solution)/shard_map/ppermute | solution.py:14
  96.8 4.9 %copy-start.11 = (s32[2]{0:T(128)S(1)}, s32[2]{0:T(128)}, u32[]{:S(2)}) copy-start(s32[2]{0:T(128)} %param.11) | copy-start | bytes 28
  109.3 14.9 %collective-permute-start.1 = (bf16[16,16384]{1,0:T(8,128)(2,1)S(1)}, bf16[16,16384]{1,0:T(8,128)(2,1)S(1)}, u32[]{:S(2)}, u32[]{:S(2)}) collective-permute-start(bf16[16,16384]{1,0:T(8,128)(2,1)S(1)} %collective-permute-done), channel_id=1, source_target_pairs={{3,0},{0,1},{1,2},{2,3},{7,4},{4,5},{5,6},{6,7},{11,8},{8,9},{9,10... | collective-permute-start | bytes 1572872 | tf_op jit(solution)/shard_map/ppermute | solution.py:14
  124.4 14.1 %collective-permute-start.2 = (bf16[16,16384]{1,0:T(8,128)(2,1)S(1)}, bf16[16,16384]{1,0:T(8,128)(2,1)S(1)}, u32[]{:S(2)}, u32[]{:S(2)}) collective-permute-start(bf16[16,16384]{1,0:T(8,128)(2,1)S(1)} %collective-permute-done.1), channel_id=1, source_target_pairs={{3,0},{0,1},{1,2},{2,3},{7,4},{4,5},{5,6},{6,7},{11,8},{8,9},{9,10... | collective-permute-start | bytes 1572872 | tf_op jit(solution)/shard_map/ppermute | solution.py:14
  142.0 177.1 %copy-start.3 = (bf16[1,16,16384]{2,1,0:T(8,128)(2,1)S(1)}, bf16[1,16,16384]{2,1,0:T(8,128)(2,1)}, u32[]{:S(2)}) copy-start(bf16[1,16,16384]{2,1,0:T(8,128)(2,1)} %stack_reshape.37) | copy-start | bytes 1572868
  142.0 177.1 %copy-start.4 = (bf16[1,16,16384]{2,1,0:T(8,128)(2,1)S(1)}, bf16[1,16,16384]{2,1,0:T(8,128)(2,1)}, u32[]{:S(2)}) copy-start(bf16[1,16,16384]{2,1,0:T(8,128)(2,1)} %stack_reshape.36) | copy-start | bytes 1572868
  319.1 7.4 %slice-start.3 = ((s8[10485760]{0:T(1024)(128)(4,1)}), s8[4194304]{0:T(1024)(128)(4,1)S(1)}, s32[]{:S(2)}) async-start(s8[10485760]{0:T(1024)(128)(4,1)} %bitcast.257), calls=%async_computation.8 | async-start | bytes 8388608
  319.1 7.4 %slice-start.4 = ((s8[10485760]{0:T(1024)(128)(4,1)}), s8[4194304]{0:T(1024)(128)(4,1)S(1)}, s32[]{:S(2)}) async-start(s8[10485760]{0:T(1024)(128)(4,1)} %bitcast.257), calls=%async_computation.9 | async-start | bytes 8388608
  319.1 7.4 %slice-start.5 = ((s8[10485760]{0:T(1024)(128)(4,1)}), s8[2097152]{0:T(1024)(128)(4,1)S(1)}, s32[]{:S(2)}) async-start(s8[10485760]{0:T(1024)(128)(4,1)} %bitcast.257), calls=%async_computation.10 | async-start | bytes 4194304
  319.1 7.4 %copy-start.5 = (bf16[1,16,16384]{2,1,0:T(8,128)(2,1)S(1)}, bf16[1,16,16384]{2,1,0:T(8,128)(2,1)}, u32[]{:S(2)}) copy-start(bf16[1,16,16384]{2,1,0:T(8,128)(2,1)} %stack_reshape.39) | copy-start | bytes 1572868
  319.1 7.4 %copy-start.6 = (bf16[1,16,16384]{2,1,0:T(8,128)(2,1)S(1)}, bf16[1,16,16384]{2,1,0:T(8,128)(2,1)}, u32[]{:S(2)}) copy-start(bf16[1,16,16384]{2,1,0:T(8,128)(2,1)} %stack_reshape.41) | copy-start | bytes 1572868
  326.5 3.2 copy-start.7
  326.5 3.2 copy-start.8
  329.7 3.2 copy-start.9
  329.7 3.2 copy-start.10
  336.3 49.7 %collective-permute-start.6 = (bf16[16]{0:T(256)(128)(2,1)S(1)}, bf16[16]{0:T(256)(128)(2,1)S(1)}, u32[]{:S(2)}, u32[]{:S(2)}) collective-permute-start(bf16[16]{0:T(256)(128)(2,1)S(1)} %fusion.112), channel_id=1, source_target_pairs={{3,0},{0,1},{1,2},{2,3},{7,4},{4,5},{5,6},{6,7},{11,8},{8,9},{9,10... | collective-permute-start | bytes 104 | tf_op jit(solution)/shard_map/ppermute | solution.py:14
  357.4 5.4 %slice-start = ((s8[10485760]{0:T(1024)(128)(4,1)}), s8[4194304]{0:T(1024)(128)(4,1)S(1)}, s32[]{:S(2)}) async-start(s8[10485760]{0:T(1024)(128)(4,1)} %bitcast.239), calls=%async_computation.5 | async-start | bytes 8388608
  357.8 5.0 %slice-start.1 = ((s8[10485760]{0:T(1024)(128)(4,1)}), s8[4194304]{0:T(1024)(128)(4,1)S(1)}, s32[]{:S(2)}) async-start(s8[10485760]{0:T(1024)(128)(4,1)} %bitcast.239), calls=%async_computation.6 | async-start | bytes 8388608
  358.7 4.1 slice-start.2
  360.6 17.8 %collective-permute-start.3 = (bf16[16,16384]{1,0:T(8,128)(2,1)S(1)}, bf16[16,16384]{1,0:T(8,128)(2,1)S(1)}, u32[]{:S(2)}, u32[]{:S(2)}) collective-permute-start(bf16[16,16384]{1,0:T(8,128)(2,1)S(1)} %fusion.99), channel_id=1, source_target_pairs={{3,0},{0,1},{1,2},{2,3},{7,4},{4,5},{5,6},{6,7},{11,8},{8,9},{9,10... | collective-permute-start | bytes 1572872 | tf_op jit(solution)/shard_map/ppermute | solution.py:14
  378.5 12.4 %collective-permute-start.4 = (bf16[16,16384]{1,0:T(8,128)(2,1)S(1)}, bf16[16,16384]{1,0:T(8,128)(2,1)S(1)}, u32[]{:S(2)}, u32[]{:S(2)}) collective-permute-start(bf16[16,16384]{1,0:T(8,128)(2,1)S(1)} %add_convert_fusion.2), channel_id=1, source_target_pairs={{3,0},{0,1},{1,2},{2,3},{7,4},{4,5},{5,6},{6,7},{11,8},{8,9},{9,10... | collective-permute-start | bytes 1572872 | tf_op jit(solution)/shard_map/ppermute | solution.py:14
  382.2 14.2 %all-to-all-start.4 = ((bf16[32,1,10]{2,1,0:T(2,128)(2,1)}), bf16[32,1,10]{2,1,0:T(2,128)(2,1)S(1)}, u32[]{:S(2)}, u32[]{:S(2)}) async-start(bf16[32,1,10]{2,1,0:T(2,128)(2,1)} %convert_element_type.177), calls=%async_computation.4 | async-start | bytes 32768 | tf_op jit(solution)/shard_map/all_to_all | solution.py:136
  386.1 4.8 %collective-permute-start.7 = (bf16[16]{0:T(256)(128)(2,1)S(1)}, bf16[16]{0:T(256)(128)(2,1)S(1)}, u32[]{:S(2)}, u32[]{:S(2)}) collective-permute-start(bf16[16]{0:T(256)(128)(2,1)S(1)} %fusion.115), channel_id=1, source_target_pairs={{3,0},{0,1},{1,2},{2,3},{7,4},{4,5},{5,6},{6,7},{11,8},{8,9},{9,10... | collective-permute-start | bytes 104 | tf_op jit(solution)/shard_map/ppermute | solution.py:14
  390.9 4.8 %collective-permute-start.8 = (bf16[16]{0:T(256)(128)(2,1)S(1)}, bf16[16]{0:T(256)(128)(2,1)S(1)}, u32[]{:S(2)}, u32[]{:S(2)}) collective-permute-start(bf16[16]{0:T(256)(128)(2,1)S(1)} %fusion.118), channel_id=1, source_target_pairs={{3,0},{0,1},{1,2},{2,3},{7,4},{4,5},{5,6},{6,7},{11,8},{8,9},{9,10... | collective-permute-start | bytes 104 | tf_op jit(solution)/shard_map/ppermute | solution.py:14
  390.9 24.3 %copy-start.1 = (s32[256]{0:T(256)S(1)}, s32[256]{0:T(256)}, u32[]{:S(2)}) copy-start(s32[256]{0:T(256)} %param.8) | copy-start | bytes 3076
  391.0 22.9 %collective-permute-start.5 = (bf16[16,16384]{1,0:T(8,128)(2,1)S(1)}, bf16[16,16384]{1,0:T(8,128)(2,1)S(1)}, u32[]{:S(2)}, u32[]{:S(2)}) collective-permute-start(bf16[16,16384]{1,0:T(8,128)(2,1)S(1)} %add_convert_fusion.1), channel_id=1, source_target_pairs={{3,0},{0,1},{1,2},{2,3},{7,4},{4,5},{5,6},{6,7},{11,8},{8,9},{9,10... | collective-permute-start | bytes 1572872 | tf_op jit(solution)/shard_map/ppermute | solution.py:14
  396.4 14.8 %all-to-all-start.3 = ((bf16[32,2,160]{2,1,0:T(2,128)(2,1)}), bf16[32,2,160]{2,1,0:T(2,128)(2,1)S(1)}, u32[]{:S(2)}, u32[]{:S(2)}) async-start(bf16[32,2,160]{2,1,0:T(2,128)(2,1)} %reshape.419), calls=%async_computation.3 | async-start | bytes 65536 | tf_op jit(solution)/shard_map/all_to_all | solution.py:129
where the time goes:
time: 421 us; the launch traced here: 416 us
  waiting for transfers between devices  207 us (49%)
  local copies, waits for them, and re-layouts  107 us (25%)
  starting transfers between devices  42.6 us (10%)
  matrix products  28.8 us (7%)
  other arithmetic  28.7 us (7%)
    all_to_all x1, waiting for transfers between devices, shards(): lax.all_to_all(send_img, 'dom', split_axis=0, concat_axis=0, tiled=True)  164 us
    gather x2, local copies, waits for them, and re-layouts, shards(): particles[safe_source]  44.9 us
    ppermute x9, waiting for transfers between devices, from_behind(): return lax.ppermute(block, axis, route)  38 us
    reshape x2, local copies, waits for them, and re-layouts, shards(): images = got_img.reshape(slot_count, pixels)  26.3 us
    dot_general x4, matrix products, block_scores(): lax.dot_general(images, shifted, (((1,), (1,)), ((), ())), preferred_elem...  16.7 us
    select_n x1, other arithmetic, shards(): jnp.where(filled[:, None], particles[safe_source], jnp.zeros((), particle...  14 us
    unnamed x4, matrix products  12.1 us
    another operation x9, local copies, waits for them, and re-layouts, block_scores(): jnp.stack([translate(proj_block, -t) for t in offsets])  9.25 us
  transfers between devices with their start and end apart: 14, of which 7 were waited for; matrix products, arithmetic and copies ran while one was open for 30% of the time, Pallas kernels for 0%

commit v1 on v0

v1 whole, which is shorter than its diff:
```python
import jax
import jax.numpy as jnp
from jax import lax
from jax.sharding import PartitionSpec as P

IMG = 128
SHIFTS = 3
PRIOR_WIDTH = 576
FIRST_ROWS = 8


def translate(images, offset):
    if offset == 0:
        return images
    pixels = images.shape[-1]
    lane = lax.broadcasted_iota(jnp.int32, images.shape, images.ndim - 1) % IMG
    near = jnp.roll(images, offset, axis=-1)
    if offset > 0:
        far = jnp.roll(images, offset - IMG, axis=-1)
        keep = lane >= offset
    else:
        far = jnp.roll(images, offset + IMG, axis=-1)
        keep = lane < IMG + offset
    del pixels
    return jnp.where(keep, near, far)


def shards(particles, noise_prec, prior_pose, owners, projections, pose_index):
    f32 = jnp.float32
    count_dom = lax.axis_size("dom")
    count_ref = lax.axis_size("ref")
    arrived, pixels = particles.shape
    capacity = (5 * arrived + 4 * count_dom - 1) // (4 * count_dom)
    rows_a = min(FIRST_ROWS, capacity)
    rows_b = capacity - rows_a

    earlier = jnp.arange(arrived)[:, None] > jnp.arange(arrived)[None, :]
    same_owner = owners[:, None] == owners[None, :]
    slot_rank = jnp.sum(same_owner & earlier, axis=1).astype(jnp.int32)
    in_a = slot_rank < rows_a

    def pick(slot_of, count):
        return slot_of[None, :] == jnp.arange(count, dtype=jnp.int32)[:, None]

    pick_a = pick(jnp.where(in_a, owners * rows_a + slot_rank, -1), count_dom * rows_a)
    send_a = jnp.dot(pick_a.astype(particles.dtype), particles, preferred_element_type=f32)
    send_a = send_a.astype(particles.dtype).reshape(count_dom, rows_a, pixels)
    pick_all = pick(owners * capacity + slot_rank, count_dom * capacity)
    send_prec = jnp.sum(jnp.where(pick_all, noise_prec.astype(f32)[None, :], 0.0), axis=1)
    send_prior = jnp.sum(jnp.where(pick_all, prior_pose.astype(f32)[None, :] + 1.0, 0.0), axis=1) - 1.0
    meta = jnp.stack(
        [send_prec.reshape(count_dom, capacity), send_prior.reshape(count_dom, capacity)], axis=1
    )
    got_meta = lax.all_to_all(meta, "dom", 0, 0, tiled=True)
    got_a = lax.all_to_all(send_a, "dom", 0, 0, tiled=True).reshape(count_dom * rows_a, pixels)
    if rows_b:
        pick_b = pick(jnp.where(in_a, -1, owners * rows_b + slot_rank - rows_a), count_dom * rows_b)
        send_b = jnp.dot(pick_b.astype(particles.dtype), particles, preferred_element_type=f32)
        send_b = send_b.astype(particles.dtype).reshape(count_dom, rows_b, pixels)
        got_a, send_b = lax.optimization_barrier((got_a, send_b))
        got_b = lax.all_to_all(send_b, "dom", 0, 0, tiled=True).reshape(count_dom * rows_b, pixels)

    own_proj = projections.reshape(-1, pixels)
    all_proj = lax.all_gather(own_proj, "ref", axis=0, tiled=True)
    rows = all_proj.shape[0]
    offsets = [u - SHIFTS // 2 for u in range(SHIFTS)]
    shifted = jnp.concatenate([translate(all_proj, -t) for t in offsets], axis=0)
    norms = jnp.sum(jnp.square(all_proj.astype(f32)), axis=1)
    per_class = projections.shape[1]
    pose_f = pose_index.astype(f32)

    def part(images, precision, prior_ids):
        n = images.shape[0]
        live = (prior_ids >= 0).astype(f32)
        corr = lax.dot_general(
            images, shifted, (((1,), (1,)), ((), ())), preferred_element_type=f32
        ).reshape(n, SHIFTS, rows)
        log_prior = -jnp.abs(pose_f[None, :] - prior_ids[:, None]) / PRIOR_WIDTH
        prior_rows = jnp.tile(log_prior, (1, rows // per_class))
        scaled = corr / IMG - norms[None, None, :] / (2.0 * IMG * IMG)
        scores = precision[:, None, None] * scaled + prior_rows[:, None, :]
        highest = jnp.max(scores, axis=(1, 2))
        loglike = highest + jnp.log(jnp.sum(jnp.exp(scores - highest[:, None, None]), axis=(1, 2)))
        weights = jnp.exp(scores - loglike[:, None, None]) * live[:, None, None]
        class_post = jnp.sum(weights.reshape(n, SHIFTS, rows // per_class, per_class), axis=(1, 3))
        totals = jnp.sum(weights, axis=(0, 1))
        low = weights.astype(jnp.bfloat16).reshape(n, SHIFTS * rows)
        summed = lax.dot_general(low, images, (((0,), (0,)), ((), ())), preferred_element_type=f32)
        post = jnp.concatenate([class_post, loglike[:, None]], axis=1)
        return summed, totals, post

    meta_prec = got_meta[:, 0, :]
    meta_prior = got_meta[:, 1, :]
    sum_a, tot_a, post_a = part(
        got_a, meta_prec[:, :rows_a].reshape(-1), meta_prior[:, :rows_a].reshape(-1)
    )
    post_width = post_a.shape[1]
    back = [post_a.reshape(count_dom, rows_a, post_width)]
    if rows_b:
        sum_b, tot_b, post_b = part(
            got_b, meta_prec[:, rows_a:].reshape(-1), meta_prior[:, rows_a:].reshape(-1)
        )
        sum_a = sum_a + sum_b
        tot_a = tot_a + tot_b
        back.append(post_b.reshape(count_dom, rows_b, post_width))
    back = jnp.concatenate(back, axis=1)
    got_back = lax.all_to_all(back, "dom", 0, 0, tiled=True).reshape(count_dom * capacity, post_width)

    per_shift = sum_a.reshape(SHIFTS, rows, pixels)
    image_sums = translate(per_shift[0], offsets[0])
    for u in range(1, SHIFTS):
        image_sums = image_sums + translate(per_shift[u], offsets[u])
    partial = image_sums.astype(jnp.bfloat16).reshape(count_ref, rows // count_ref, pixels)
    got_partial = lax.all_to_all(partial, "ref", 0, 0, tiled=True)
    class_sums = jnp.sum(got_partial.astype(f32), axis=0).astype(jnp.bfloat16)
    class_sums = class_sums.reshape(projections.shape)
    got_tot = lax.all_to_all(tot_a.reshape(count_ref, rows // count_ref), "ref", 0, 0, tiled=True)
    weight_totals = jnp.sum(got_tot, axis=0).reshape(projections.shape[0], projections.shape[1])

    mine = got_back[owners * capacity + slot_rank]
    class_prob = mine[:, : post_width - 1]
    log_like = mine[:, post_width - 1]
    return (class_prob, log_like, class_sums, weight_totals)


def solution(mesh):
    in_specs = (
        P(("dom", "ref"), None),
        P(("dom", "ref")),
        P(("dom", "ref")),
        P(("dom", "ref")),
        P("ref", "dom", None),
        P("dom"),
    )
    out_specs = (P(("dom", "ref"), None), P(("dom", "ref")), P("ref", "dom", None), P("ref", "dom"))
    return jax.shard_map(shards, mesh=mesh, in_specs=in_specs, out_specs=out_specs, check_vma=False)
```

time: 421 us -> 279 us (0.66)
  waiting for transfers between devices: 207 us -> 123 us
  local copies, waits for them, and re-layouts: 107 us -> 42.9 us
  between operations: 1.91 us -> 14.4 us
  matrix products: 28.8 us -> 39.4 us
  starting transfers between devices: 42.6 us -> 33.7 us
  other arithmetic: 28.7 us -> 24.3 us
    gather x6 -> x1, local copies, waits for them, and re-layouts: 55.2 us -> 0.73 us  [shards(): mine = got_back[owners * capacity + slot_rank]]
    all_to_all x5 -> x6, waiting for transfers between devices: 169 us -> 123 us  [the longest x1 89.7 us: shards(): lax.all_to_all(send_a, 'dom', 0, 0, tiled=True)]
    ppermute x9 -> x0, waiting for transfers between devices: 38 us -> none  [from_behind(): return lax.ppermute(block, axis, route)]
    dot_general x4 -> x6, matrix products: 16.7 us -> 39.4 us  [the longest x2 16.1 us: part(): lax.dot_general(low, images, (((0,), (0,)), ((), ())), preferred_element_...]
    reshape x4 -> x6, local copies, waits for them, and re-layouts: 27.5 us -> 9.4 us  [the longest x2 5.49 us: shards(): lax.all_to_all(send_b, 'dom', 0, 0, tiled=True)]
    slice x16 -> x13, local copies, waits for them, and re-layouts: 4.61 us -> 20.5 us  [the longest x4 8.98 us: translate(): far = jnp.roll(images, offset - IMG, axis=-1)]
    unnamed x4 -> x0, matrix products: 12.1 us -> none
    ppermute x9 -> x0, starting transfers between devices: 8.99 us -> none  [from_behind(): return lax.ppermute(block, axis, route)]
  transfers between devices with their start and end apart: 14 -> 7, of which waited for: 7 -> 4; matrix products, arithmetic and copies ran while one was open for 30% -> 26% of each run, Pallas kernels for 0% -> 0%
where the time goes in v1:
time: 279 us; the launch traced here: 277 us
  waiting for transfers between devices  123 us (44%)
  local copies, waits for them, and re-layouts  42.9 us (15%)
  matrix products  39.4 us (14%)
  starting transfers between devices  33.7 us (12%)
  other arithmetic  24.3 us (9%)
  between operations  14.4 us (5%)
    all_to_all x1, waiting for transfers between devices, shards(): lax.all_to_all(send_a, 'dom', 0, 0, tiled=True)  89.7 us
    all_to_all x1, waiting for transfers between devices, shards(): got_partial = lax.all_to_all(partial, 'ref', 0, 0, tiled=True)  22.3 us
    dot_general x2, matrix products, part(): lax.dot_general(low, images, (((0,), (0,)), ((), ())), preferred_element_...  16.1 us
    dot_general x2, matrix products, part(): lax.dot_general(images, shifted, (((1,), (1,)), ((), ())), preferred_elem...  12.1 us
    all_to_all x1, waiting for transfers between devices, shards(): lax.all_to_all(send_b, 'dom', 0, 0, tiled=True)  10.7 us
    convert_element_type x1, other arithmetic, shards(): image_sums.astype(jnp.bfloat16)  10.4 us
    slice x4, local copies, waits for them, and re-layouts, translate(): far = jnp.roll(images, offset - IMG, axis=-1)  8.98 us
    all_to_all x1, starting transfers between devices, shards(): lax.all_to_all(send_a, 'dom', 0, 0, tiled=True)  7.48 us
  transfers between devices with their start and end apart: 7, of which 4 were waited for; matrix products, arithmetic and copies ran while one was open for 26% of the time, Pallas kernels for 0%

profile of v1, /device:TPU:0, one launch (start us, length us, event | category | flops | bytes accessed | tf_op | source)
XLA Modules:
  0.0 277.5 jit_solution(7642997682272354846)
XLA Ops:
  7.2 2.0 reshape.301
  9.3 0.7 convert_element_type.51
  9.9 0.7 convert_add_fusion
  10.6 0.9 convert_reduce_fusion
  11.5 0.7 compare_select_fusion
  12.7 0.6 copy.45
  13.3 7.4 %all-to-all-start = ((f32[32,2,10]{2,1,0:T(2,128)}), f32[32,2,10]{2,1,0:T(2,128)S(1)}, u32[]{:S(2)}, u32[]{:S(2)}) async-start(f32[32,2,10]{2,1,0:T(2,128)} %copy.45), calls=%async_computation | async-start | bytes 65536 | tf_op jit(solution)/shard_map/all_to_all | solution.py:54
  20.8 5.5 %convolution_convert_fusion.1 = bf16[64,16384]{1,0:T(8,128)(2,1)S(1)} fusion(bf16[256,16384]{1,0:T(8,128)(2,1)} %param.6, s32[256]{0:T(256)S(1)} %get-tuple-element.58), kind=kOutput, calls=%fused_computation.4 | convolution fusion | flops 537935872 | bytes 10486784 | tf_op jit(solution)/shard_map/dot_general | solution.py:58
  26.3 0.7 copy-done.2
  27.0 5.7 %fusion = bf16[32,8,16384]{2,1,0:T(8,128)(2,1)} fusion(bf16[256,16384]{1,0:T(8,128)(2,1)S(1)} %copy-done.2, s32[256]{0:T(256)S(1)} %get-tuple-element.57), kind=kOutput, calls=%fused_computation.3 | convolution fusion | flops 2151743488 | bytes 16778240 | tf_op jit(solution)/shard_map/dot_general | solution.py:46
  32.7 2.7 reshape.300
  35.3 7.5 %all-to-all-start.1 = ((bf16[32,8,16384]{2,1,0:T(8,128)(2,1)}), bf16[32,8,16384]{2,1,0:T(8,128)(2,1)}, u32[]{:S(2)}, u32[]{:S(2)}) async-start(bf16[32,8,16384]{2,1,0:T(8,128)(2,1)} %fusion), calls=%async_computation.1 | async-start | bytes 16777216 | tf_op jit(solution)/shard_map/all_to_all | solution.py:55
  43.8 0.8 fusion.31
  44.6 0.8 fusion.32
  45.4 3.1 %fusion.30 = (bf16[64,16257]{1,0:T(8,128)(2,1)S(1)}, bf16[64,16257]{1,0:T(8,128)(2,1)S(1)}) fusion(bf16[64,16384]{1,0:T(8,128)(2,1)} %all-gather.2.cloned.1.call-done), kind=kLoop, calls=%fused_computation.75 | loop fusion | bytes 8323584 | tf_op jit(solution)/shard_map/jit(_roll_static)/slice | solution.py:19
  48.5 0.7 fusion.33
  49.3 4.6 %fusion.4 = (bf16[64,16384]{1,0:T(8,128)(2,1)S(1)}, bf16[64,16384]{1,0:T(8,128)(2,1)S(1)}) fusion(bf16[64,16383]{1,0:T(8,128)(2,1)S(1)} %get-tuple-element.50, bf16[64,1]{1,0:T(8,128)(2,1)S(1)} %get-tuple-element.48, bf16[64,127]{1,0:T(8,128)(2,1)S(1)} %get-tuple-element.46, bf16[64,16257]{1,0:T(8,128)(2,1)S(1)} %get-tuple-element.44, ...), kind=kLoop, calls=%fused_computation.16 | loop fusion | flops 22020096 | bytes 12730368 | tf_op jit(solution)/shard_map/jit(_where)/select_n | solution.py:25
  53.9 1.3 copy-done.3
  55.2 0.7 copy-done.4
  55.9 3.1 %pad_maximum_fusion = bf16[192,16384]{1,0:T(8,128)(2,1)} fusion(bf16[64,16384]{1,0:T(8,128)(2,1)S(1)} %get-tuple-element.53, bf16[64,16384]{1,0:T(8,128)(2,1)S(1)} %copy-done, bf16[64,16384]{1,0:T(8,128)(2,1)S(1)} %get-tuple-element.52), kind=kLoop, calls=%fused_computation.5 | loop fusion | flops 18874368 | bytes 12582912 | tf_op jit(solution)/shard_map/concatenate | solution.py:67
  59.1 89.7 %all-to-all-done.1 = bf16[32,8,16384]{2,1,0:T(8,128)(2,1)} async-done(((bf16[32,8,16384]{2,1,0:T(8,128)(2,1)}), bf16[32,8,16384]{2,1,0:T(8,128)(2,1)}, u32[]{:S(2)}, u32[]{:S(2)}) %all-to-all-start.1) | async-done | bytes 8388640 | tf_op jit(solution)/shard_map/all_to_all | solution.py:55
  148.7 4.9 %all-to-all-start.2 = ((bf16[32,2,16384]{2,1,0:T(2,128)(2,1)}), bf16[32,2,16384]{2,1,0:T(2,128)(2,1)}, u32[]{:S(2)}, u32[]{:S(2)}) async-start(bf16[32,2,16384]{2,1,0:T(2,128)(2,1)} %reshape.300), calls=%async_computation.2 | async-start | bytes 4194304 | tf_op jit(solution)/shard_map/all_to_all | solution.py:61
  154.4 7.5 %fusion.25 = (f32[256]{0:T(256)S(1)}, f32[256,192]{0,1:T(8,128)S(1)}, f32[256,192]{0,1:T(8,128)S(1)}) fusion(f32[256,64]{0,1:T(8,128)S(1)} %tile.17, f32[192]{0:T(256)S(1)} %sub.126, f32[256]{0:T(256)S(1)} %mul.66, bf16[256,16384]{1,0:T(8,128)(2,1)} %bitcast.2, bf16[64,16384]{1,0:T(8,128)(2,1)} %copy-done.4, bf16[64,16384]{1,0:T(8,128)(2,1)S(1)} %copy-done, ...), kind=kOutput, calls=%fused_computation.70 | convolution fusion | flops 1629732608 | bytes 15141632 | tf_op jit(solution)/shard_map/dot_general | solution.py:75
  163.0 9.8 %fusion.13 = f32[192,16384]{1,0:T(8,128)} fusion(bf16[256,16384]{1,0:T(8,128)(2,1)} %bitcast.2, f32[256,192]{0,1:T(8,128)S(1)} %get-tuple-element.35, f32[256]{0:T(256)S(1)} %compare_convert_fusion.1, f32[256]{0:T(256)S(1)} %log_add_fusion), kind=kOutput, calls=%fused_computation.39 | convolution fusion | flops 1610760192 | bytes 21170176 | tf_op jit(solution)/shard_map/dot_general | solution.py:88
  172.7 10.7 %all-to-all-done.2 = bf16[32,2,16384]{2,1,0:T(2,128)(2,1)} async-done(((bf16[32,2,16384]{2,1,0:T(2,128)(2,1)}), bf16[32,2,16384]{2,1,0:T(2,128)(2,1)}, u32[]{:S(2)}, u32[]{:S(2)}) %all-to-all-start.2) | async-done | bytes 2097184 | tf_op jit(solution)/shard_map/all_to_all | solution.py:61
  183.4 2.7 reshape.316
  186.2 4.6 %fusion.35 = (f32[64]{0:T(128)S(1)}, f32[64,3,64]{0,2,1:T(8,128)S(1)}) fusion(f32[64,64]{0,1:T(8,128)S(1)} %bitcast.46, f32[64]{0:T(128)S(1)} %broadcast_multiply_fusion, bf16[64,16384,1]{1,0,2:T(8,128)(2,1)S(1)} %reshape.316, bf16[3,64,16384]{2,1,0:T(8,128)(2,1)} %bitcast.39, f32[64]{0:T(128)S(1)} %mul.76), kind=kOutput, calls=%fused_computation.80 | convolution fusion | flops 402714560 | bytes 8454912 | tf_op jit(solution)/shard_map/dot_general | solution.py:75
  191.2 2.7 reshape.302
  193.9 6.4 %convolution_add_fusion = f32[192,16384]{1,0:T(8,128)S(1)} fusion(f32[192,16384]{1,0:T(8,128)} %fusion.13, bf16[64,192]{0,1:T(8,128)(2,1)S(1)} %bitcast.48, bf16[64,16384]{1,0:T(8,128)(2,1)S(1)} %reshape.302), kind=kOutput, calls=%fused_computation.1 | convolution fusion | flops 405798912 | bytes 27287552 | tf_op jit(solution)/shard_map/dot_general | solution.py:88
  200.4 5.0 %fusion.26 = (f32[64,16257]{1,0:T(8,128)}, f32[64,16257]{1,0:T(8,128)}) fusion(f32[192,16384]{1,0:T(8,128)S(1)} %convolution_add_fusion), kind=kLoop, calls=%fused_computation.71 | loop fusion | bytes 16647168 | tf_op jit(solution)/shard_map/jit(_roll_static)/slice | solution.py:19
  205.4 1.9 copy-done.1
  207.3 4.5 %fusion.29 = (f32[64,16383]{1,0:T(8,128)}, f32[64,16383]{1,0:T(8,128)}) fusion(f32[192,16384]{1,0:T(8,128)S(1)} %convolution_add_fusion), kind=kLoop, calls=%fused_computation.74 | loop fusion | bytes 16776192 | tf_op jit(solution)/shard_map/jit(_roll_static)/slice | solution.py:17
  211.9 0.7 add.163
  212.6 5.1 %all-to-all-start.5 = ((f32[4,1,16]{2,1,0:T(1,128)}), f32[4,1,16]{2,1,0:T(1,128)S(1)}, u32[]{:S(2)}, u32[]{:S(2)}) async-start(f32[4,1,16]{2,1,0:T(1,128)} %bitcast.20), calls=%async_computation.5 | async-start | bytes 4096 | tf_op jit(solution)/shard_map/all_to_all | solution.py:117
  217.9 4.5 %slice.151 = f32[64,16384]{1,0:T(8,128)} slice(f32[192,16384]{1,0:T(8,128)} %copy-done.1), slice={[64:128], [0:16384]} | slice | bytes 8388608 | tf_op jit(solution)/shard_map/slice | solution.py:112
  222.4 0.8 reshape.319
  223.2 3.9 %all-to-all-start.3 = ((f32[32,1,330]{2,1,0:T(1,128)}), f32[32,1,330]{2,1,0:T(1,128)S(1)}, u32[]{:S(2)}, u32[]{:S(2)}) async-start(f32[32,1,330]{2,1,0:T(1,128)} %reshape.319), calls=%async_computation.3 | async-start | bytes 98304 | tf_op jit(solution)/shard_map/all_to_all | solution.py:107
  227.0 10.4 %fusion.3 = bf16[4,16,16384]{2,1,0:T(8,128)(2,1)} fusion(f32[4,16,16384]{2,1,0:T(8,128)} %bitcast.40, f32[4,16,1]{2,1,0:T(8,128)S(1)} %bitcast.56, f32[4,16,16383]{2,1,0:T(8,128)} %bitcast.44, f32[4,16,16257]{2,1,0:T(8,128)} %bitcast.42, f32[4,16,127]{2,1,0:T(8,128)S(1)} %bitcast.54, f32[4,16,16383]{2,1,0:T(8,128)} %bitcast.43, f32[4,16,1]{2,1,0:T(8,128)S(1)} %bitcast.55, ...), kind=kLoop, calls=%fused_computation.13 | loop fusion | flops 12582912 | bytes 23216128 | tf_op jit(solution)/shard_map/convert_element_type | solution.py:113
  237.4 4.8 %all-to-all-start.4 = ((bf16[4,16,16384]{2,1,0:T(8,128)(2,1)}), bf16[4,16,16384]{2,1,0:T(8,128)(2,1)S(1)}, u32[]{:S(2)}, u32[]{:S(2)}) async-start(bf16[4,16,16384]{2,1,0:T(8,128)(2,1)} %fusion.3), calls=%async_computation.4 | async-start | bytes 4194304 | tf_op jit(solution)/shard_map/all_to_all | solution.py:114
  242.3 0.6 copy.54
  243.0 0.5 broadcast.220
  243.5 0.8 reduce.10
  244.4 0.7 gather_fusion
  245.1 0.7 copy.53
  245.8 0.7 slice_reduce_fusion
  246.6 22.3 %all-to-all-done.4 = bf16[4,16,16384]{2,1,0:T(8,128)(2,1)S(1)} async-done(((bf16[4,16,16384]{2,1,0:T(8,128)(2,1)}), bf16[4,16,16384]{2,1,0:T(8,128)(2,1)S(1)}, u32[]{:S(2)}, u32[]{:S(2)}) %all-to-all-start.4) | async-done | bytes 2097184 | tf_op jit(solution)/shard_map/all_to_all | solution.py:114
  268.9 0.6 reduce_sum.135
  269.5 1.1 reshape.305
  (65 shorter events, 4.2 us)
Async XLA Ops:
  7.2 36.6 %all-gather.2.cloned.1.call-start = ((), (), s32[]{:S(2)}) async-start(), calls=%async_computation.6 | async-start | bytes 2621440 | tf_op jit(solution)/shard_map/all_gather | solution.py:64
  13.3 22.0 %all-to-all-start = ((f32[32,2,10]{2,1,0:T(2,128)}), f32[32,2,10]{2,1,0:T(2,128)S(1)}, u32[]{:S(2)}, u32[]{:S(2)}) async-start(f32[32,2,10]{2,1,0:T(2,128)} %copy.45), calls=%async_computation | async-start | bytes 65536 | tf_op jit(solution)/shard_map/all_to_all | solution.py:54
  20.7 6.2 %copy-start.2 = (bf16[256,16384]{1,0:T(8,128)(2,1)S(1)}, bf16[256,16384]{1,0:T(8,128)(2,1)}, u32[]{:S(2)}) copy-start(bf16[256,16384]{1,0:T(8,128)(2,1)} %param.6) | copy-start | bytes 25165828
  27.0 5.7 %copy-start.5 = (s32[2]{0:T(128)S(1)}, s32[2]{0:T(128)}, u32[]{:S(2)}) copy-start(s32[2]{0:T(128)} %param.11) | copy-start | bytes 28
  35.3 113.4 %all-to-all-start.1 = ((bf16[32,8,16384]{2,1,0:T(8,128)(2,1)}), bf16[32,8,16384]{2,1,0:T(8,128)(2,1)}, u32[]{:S(2)}, u32[]{:S(2)}) async-start(bf16[32,8,16384]{2,1,0:T(8,128)(2,1)} %fusion), calls=%async_computation.1 | async-start | bytes 16777216 | tf_op jit(solution)/shard_map/all_to_all | solution.py:55
  45.4 3.1 %copy-start = (bf16[64,16384]{1,0:T(8,128)(2,1)S(1)}, bf16[64,16384]{1,0:T(8,128)(2,1)}, u32[]{:S(2)}) copy-start(bf16[64,16384]{1,0:T(8,128)(2,1)} %all-gather.2.cloned.1.call-done) | copy-start | bytes 6291460
  53.9 1.3 copy-start.3
  53.9 2.0 copy-start.4
  148.7 34.7 %all-to-all-start.2 = ((bf16[32,2,16384]{2,1,0:T(2,128)(2,1)}), bf16[32,2,16384]{2,1,0:T(2,128)(2,1)}, u32[]{:S(2)}, u32[]{:S(2)}) async-start(bf16[32,2,16384]{2,1,0:T(2,128)(2,1)} %reshape.300), calls=%async_computation.2 | async-start | bytes 4194304 | tf_op jit(solution)/shard_map/all_to_all | solution.py:61
  200.3 7.0 %copy-start.1 = (f32[192,16384]{1,0:T(8,128)}, f32[192,16384]{1,0:T(8,128)S(1)}, u32[]{:S(2)}) copy-start(f32[192,16384]{1,0:T(8,128)S(1)} %convolution_add_fusion) | copy-start | bytes 37748740
  212.6 10.6 %all-to-all-start.5 = ((f32[4,1,16]{2,1,0:T(1,128)}), f32[4,1,16]{2,1,0:T(1,128)S(1)}, u32[]{:S(2)}, u32[]{:S(2)}) async-start(f32[4,1,16]{2,1,0:T(1,128)} %bitcast.20), calls=%async_computation.5 | async-start | bytes 4096 | tf_op jit(solution)/shard_map/all_to_all | solution.py:117
  223.2 14.2 %all-to-all-start.3 = ((f32[32,1,330]{2,1,0:T(1,128)}), f32[32,1,330]{2,1,0:T(1,128)S(1)}, u32[]{:S(2)}, u32[]{:S(2)}) async-start(f32[32,1,330]{2,1,0:T(1,128)} %reshape.319), calls=%async_computation.3 | async-start | bytes 98304 | tf_op jit(solution)/shard_map/all_to_all | solution.py:107
  237.4 31.5 %all-to-all-start.4 = ((bf16[4,16,16384]{2,1,0:T(8,128)(2,1)}), bf16[4,16,16384]{2,1,0:T(8,128)(2,1)S(1)}, u32[]{:S(2)}, u32[]{:S(2)}) async-start(bf16[4,16,16384]{2,1,0:T(8,128)(2,1)} %fusion.3), calls=%async_computation.4 | async-start | bytes 4194304 | tf_op jit(solution)/shard_map/all_to_all | solution.py:114
Sparse Core Ops, SparseCore 0:
  10.2 33.5 all-gather.1

commit v2 on v1

--- a/solution.py
+++ b/solution.py
@@ -1,12 +1,17 @@
+import functools
+
 import jax
 import jax.numpy as jnp
 from jax import lax
+from jax.experimental import pallas as pl
+from jax.experimental.pallas import tpu as pltpu
 from jax.sharding import PartitionSpec as P
 
 IMG = 128
 SHIFTS = 3
 PRIOR_WIDTH = 576
 FIRST_ROWS = 8
+CHUNK = 2048
 
 
 def translate(images, offset):
@@ -23,6 +28,40 @@
         keep = lane < IMG + offset
     del pixels
     return jnp.where(keep, near, far)
+
+
+def sums_kernel(offsets, rows, wa_ref, xa_ref, wb_ref, xb_ref, out_ref):
+    y = jnp.dot(wa_ref[...], xa_ref[...], preferred_element_type=jnp.float32)
+    y = y + jnp.dot(wb_ref[...], xb_ref[...], preferred_element_type=jnp.float32)
+    for j in range(out_ref.shape[1] // IMG):
+        acc = None
+        for u, t in enumerate(offsets):
+            blk = y[u * rows:(u + 1) * rows, j * IMG:(j + 1) * IMG]
+            if t % IMG:
+                blk = pltpu.roll(blk, shift=t % IMG, axis=1)
+            acc = blk if acc is None else acc + blk
+        out_ref[:, j * IMG:(j + 1) * IMG] = acc.astype(out_ref.dtype)
+
+
+def class_image_sums(wa, xa, wb, xb, offsets):
+    rows = wa.shape[0] // len(offsets)
+    pixels = xa.shape[1]
+    chunk = min(CHUNK, pixels)
+    flops = 2 * wa.shape[0] * pixels * (xa.shape[0] + xb.shape[0])
+    bytes_accessed = 2 * (xa.size + xb.size + wa.size + wb.size + rows * pixels)
+    return pl.pallas_call(
+        functools.partial(sums_kernel, tuple(offsets), rows),
+        grid=(pixels // chunk,),
+        in_specs=[
+            pl.BlockSpec(wa.shape, lambda k: (0, 0)),
+            pl.BlockSpec((xa.shape[0], chunk), lambda k: (0, k)),
+            pl.BlockSpec(wb.shape, lambda k: (0, 0)),
+            pl.BlockSpec((xb.shape[0], chunk), lambda k: (0, k)),
+        ],
+        out_specs=pl.BlockSpec((rows, chunk), lambda k: (0, k)),
+        out_shape=jax.ShapeDtypeStruct((rows, pixels), jnp.bfloat16),
+        cost_estimate=pl.CostEstimate(flops=flops, transcendentals=0, bytes_accessed=bytes_accessed),
+    )(wa, xa, wb, xb)
 
 
 def shards(particles, noise_prec, prior_pose, owners, projections, pose_index):
@@ -55,6 +94,7 @@
     got_a = lax.all_to_all(send_a, "dom", 0, 0, tiled=True).reshape(count_dom * rows_a, pixels)
     if rows_b:
         pick_b = pick(jnp.where(in_a, -1, owners * rows_b + slot_rank - rows_a), count_dom * rows_b)
+        send_a, pick_b = lax.optimization_barrier((send_a, pick_b))
         send_b = jnp.dot(pick_b.astype(particles.dtype), particles, preferred_element_type=f32)
         send_b = send_b.astype(particles.dtype).reshape(count_dom, rows_b, pixels)
         got_a, send_b = lax.optimization_barrier((got_a, send_b))
@@ -84,33 +124,31 @@
         weights = jnp.exp(scores - loglike[:, None, None]) * live[:, None, None]
         class_post = jnp.sum(weights.reshape(n, SHIFTS, rows // per_class, per_class), axis=(1, 3))
         totals = jnp.sum(weights, axis=(0, 1))
-        low = weights.astype(jnp.bfloat16).reshape(n, SHIFTS * rows)
-        summed = lax.dot_general(low, images, (((0,), (0,)), ((), ())), preferred_element_type=f32)
+        low = weights.astype(jnp.bfloat16).reshape(n, SHIFTS * rows).T
         post = jnp.concatenate([class_post, loglike[:, None]], axis=1)
-        return summed, totals, post
+        return low, totals, post
 
     meta_prec = got_meta[:, 0, :]
     meta_prior = got_meta[:, 1, :]
-    sum_a, tot_a, post_a = part(
+    low_a, tot_a, post_a = part(
         got_a, meta_prec[:, :rows_a].reshape(-1), meta_prior[:, :rows_a].reshape(-1)
     )
     post_width = post_a.shape[1]
     back = [post_a.reshape(count_dom, rows_a, post_width)]
     if rows_b:
-        sum_b, tot_b, post_b = part(
+        low_b, tot_b, post_b = part(
             got_b, meta_prec[:, rows_a:].reshape(-1), meta_prior[:, rows_a:].reshape(-1)
         )
-        sum_a = sum_a + sum_b
         tot_a = tot_a + tot_b
         back.append(post_b.reshape(count_dom, rows_b, post_width))
     back = jnp.concatenate(back, axis=1)
     got_back = lax.all_to_all(back, "dom", 0, 0, tiled=True).reshape(count_dom * capacity, post_width)
 
-    per_shift = sum_a.reshape(SHIFTS, rows, pixels)
-    image_sums = translate(per_shift[0], offsets[0])
-    for u in range(1, SHIFTS):
-        image_sums = image_sums + translate(per_shift[u], offsets[u])
-    partial = image_sums.astype(jnp.bfloat16).reshape(count_ref, rows // count_ref, pixels)
+    if not rows_b:
+        low_b = jnp.zeros((SHIFTS * rows, 8), jnp.bfloat16)
+        got_b = jnp.zeros((8, pixels), particles.dtype)
+    image_sums = class_image_sums(low_a, got_a, low_b, got_b, offsets)
+    partial = image_sums.reshape(count_ref, rows // count_ref, pixels)
     got_partial = lax.all_to_all(partial, "ref", 0, 0, tiled=True)
     class_sums = jnp.sum(got_partial.astype(f32), axis=0).astype(jnp.bfloat16)
     class_sums = class_sums.reshape(projections.shape)

time: 279 us -> 260 us (0.932)
  local copies, waits for them, and re-layouts: 42.9 us -> 27.6 us
  matrix products: 39.4 us -> 24.9 us
  Pallas kernels: 0 us -> 9.9 us
  waiting for transfers between devices: 123 us -> 129 us
  other arithmetic: 24.3 us -> 19.9 us
    dot_general x2 -> x0, matrix products: 16.1 us -> none  [part(): lax.dot_general(low, images, (((0,), (0,)), ((), ())), preferred_element_...]
    convert_element_type x1 -> x0, other arithmetic: 10.4 us -> none  [shards(): image_sums.astype(jnp.bfloat16)]
    pallas_call x0 -> x1, Pallas kernels: none -> 9.9 us  [class_image_sums(): pl.pallas_call(functools.partial(sums_kernel, tuple(offsets), rows), grid...]
    slice x4 -> x2, local copies, waits for them, and re-layouts: 6.14 us -> 0.8 us  [translate(): near = jnp.roll(images, offset, axis=-1)]
    all_to_all x1, waiting for transfers between devices: 10.7 us -> 15.7 us  [shards(): lax.all_to_all(send_b, 'dom', 0, 0, tiled=True)]
    slice x1 -> x0, local copies, waits for them, and re-layouts: 4.45 us -> none  [shards(): image_sums = image_sums + translate(per_shift[u], offsets[u])]
    slice x4 -> x2, local copies, waits for them, and re-layouts: 8.98 us -> 5.11 us  [translate(): far = jnp.roll(images, offset - IMG, axis=-1)]
    dot_general x1, matrix products: 5.66 us -> 9.4 us  [shards(): jnp.dot(pick_a.astype(particles.dtype), particles, preferred_element_type...]
  transfers between devices with their start and end apart: 7 -> 7, of which waited for: 4 -> 3; matrix products, arithmetic and copies ran while one was open for 26% -> 22% of each run, Pallas kernels for 0% -> 4%
where the time goes in v2:
time: 260 us; the launch traced here: 259 us
  waiting for transfers between devices  129 us (50%)
  starting transfers between devices  33.6 us (13%)
  local copies, waits for them, and re-layouts  27.6 us (11%)
  matrix products  24.9 us (10%)
  other arithmetic  19.9 us (8%)
  between operations  14.3 us (6%)
  Pallas kernels  9.9 us (4%)
    all_to_all x1, waiting for transfers between devices, shards(): lax.all_to_all(send_a, 'dom', 0, 0, tiled=True)  91 us
    all_to_all x1, waiting for transfers between devices, shards(): got_partial = lax.all_to_all(partial, 'ref', 0, 0, tiled=True)  22.3 us
    all_to_all x1, waiting for transfers between devices, shards(): lax.all_to_all(send_b, 'dom', 0, 0, tiled=True)  15.7 us
    dot_general x2, matrix products, part(): lax.dot_general(images, shifted, (((1,), (1,)), ((), ())), preferred_elem...  10.5 us
    pallas_call x1, Pallas kernels, class_image_sums(): pl.pallas_call(functools.partial(sums_kernel, tuple(offsets), rows), grid...  9.9 us
    dot_general x1, matrix products, shards(): jnp.dot(pick_a.astype(particles.dtype), particles, preferred_element_type...  9.4 us
    all_to_all x1, starting transfers between devices, shards(): lax.all_to_all(send_a, 'dom', 0, 0, tiled=True)  7.48 us
    all_to_all x1, starting transfers between devices, shards(): got_meta = lax.all_to_all(meta, 'dom', 0, 0, tiled=True)  7.41 us
  transfers between devices with their start and end apart: 7, of which 3 were waited for; matrix products, arithmetic and copies ran while one was open for 22% of the time, Pallas kernels for 4%

profile of v2, /device:TPU:0, one launch (start us, length us, event | category | flops | bytes accessed | tf_op | source)
XLA Modules:
  0.0 259.2 jit_solution(9462692719927340290)
XLA Ops:
  7.2 2.0 reshape.271
  9.3 0.9 convert_reduce_fusion
  10.2 0.7 compare_select_fusion
  10.9 0.7 convert_add_fusion
  11.6 0.7 convert_element_type.47
  12.2 0.2 select_reduce_fusion.1
  12.7 0.6 copy.37
  13.3 7.4 %all-to-all-start = ((f32[32,2,10]{2,1,0:T(2,128)}), f32[32,2,10]{2,1,0:T(2,128)S(1)}, u32[]{:S(2)}, u32[]{:S(2)}) async-start(f32[32,2,10]{2,1,0:T(2,128)} %copy.37), calls=%async_computation | async-start | bytes 65536 | tf_op jit(solution)/shard_map/all_to_all | solution.py:93
  20.7 9.4 %fusion = bf16[32,8,16384]{2,1,0:T(8,128)(2,1)} fusion(bf16[256,16384]{1,0:T(8,128)(2,1)} %param.6, s32[256]{0:T(256)S(1)} %get-tuple-element.53), kind=kOutput, calls=%fused_computation.2 | convolution fusion | flops 2151743488 | bytes 16778240 | tf_op jit(solution)/shard_map/dot_general | solution.py:85
  30.2 5.0 %convolution_convert_fusion.1 = bf16[64,16384]{1,0:T(8,128)(2,1)S(1)} fusion(pred[64,256]{1,0:T(32,128)(4,1)S(1)} %iota_compare_fusion.4, bf16[256,16384]{1,0:T(8,128)(2,1)} %param.6), kind=kOutput, calls=%fused_computation.3 | convolution fusion | flops 537919488 | bytes 10502144 | tf_op jit(solution)/shard_map/dot_general | solution.py:98
  35.2 2.7 %reshape.270 = bf16[32,2,16384]{2,1,0:T(2,128)(2,1)} reshape(bf16[64,16384]{1,0:T(8,128)(2,1)S(1)} %convolution_convert_fusion.1) | data formatting | bytes 4194304 | tf_op jit(solution)/shard_map/reshape | solution.py:99
  37.9 7.5 %all-to-all-start.1 = ((bf16[32,8,16384]{2,1,0:T(8,128)(2,1)}), bf16[32,8,16384]{2,1,0:T(8,128)(2,1)}, u32[]{:S(2)}, u32[]{:S(2)}) async-start(bf16[32,8,16384]{2,1,0:T(8,128)(2,1)} %fusion), calls=%async_computation.1 | async-start | bytes 16777216 | tf_op jit(solution)/shard_map/all_to_all | solution.py:94
  46.2 5.0 %fusion.19 = (bf16[64,16257]{1,0:T(8,128)(2,1)}, bf16[64,16257]{1,0:T(8,128)(2,1)}) fusion(bf16[64,16384]{1,0:T(8,128)(2,1)} %all-gather.2.cloned.1.call-done), kind=kLoop, calls=%fused_computation.60 | loop fusion | bytes 8323584 | tf_op jit(solution)/shard_map/jit(_roll_static)/slice | solution.py:24
  51.3 0.5 multiply_reduce_fusion
  52.1 0.7 fusion.22
  52.9 0.9 copy-done.3
  53.7 0.6 copy-done.4
  54.4 5.9 %fusion.1 = (bf16[64,16384]{1,0:T(8,128)(2,1)}, bf16[64,16384]{1,0:T(8,128)(2,1)}) fusion(bf16[64,16383]{1,0:T(8,128)(2,1)S(1)} %get-tuple-element.44, bf16[64,1]{1,0:T(8,128)(2,1)S(1)} %get-tuple-element.42, bf16[64,127]{1,0:T(8,128)(2,1)S(1)} %get-tuple-element.40, bf16[64,16257]{1,0:T(8,128)(2,1)S(1)} %copy-done.3, s32[16384]{0:T(1024)S(1)} %get-tuple-element.58, ...), kind=kLoop, calls=%fused_computation.8 | loop fusion | flops 22020096 | bytes 12730368 | tf_op jit(solution)/shard_map/jit(_where)/select_n | solution.py:30
  60.3 91.0 %all-to-all-done.1 = bf16[32,8,16384]{2,1,0:T(8,128)(2,1)} async-done(((bf16[32,8,16384]{2,1,0:T(8,128)(2,1)}), bf16[32,8,16384]{2,1,0:T(8,128)(2,1)}, u32[]{:S(2)}, u32[]{:S(2)}) %all-to-all-start.1) | async-done | bytes 8388640 | tf_op jit(solution)/shard_map/all_to_all | solution.py:94
  151.3 4.9 %all-to-all-start.2 = ((bf16[32,2,16384]{2,1,0:T(2,128)(2,1)}), bf16[32,2,16384]{2,1,0:T(2,128)(2,1)}, u32[]{:S(2)}, u32[]{:S(2)}) async-start(bf16[32,2,16384]{2,1,0:T(2,128)(2,1)} %reshape.270), calls=%async_computation.2 | async-start | bytes 4194304 | tf_op jit(solution)/shard_map/all_to_all | solution.py:101
  156.2 6.5 %pad_maximum_fusion = bf16[192,16384]{1,0:T(8,128)(2,1)} fusion(bf16[64,16384]{1,0:T(8,128)(2,1)} %get-tuple-element.49, bf16[64,16384]{1,0:T(8,128)(2,1)S(1)} %copy-done, bf16[64,16384]{1,0:T(8,128)(2,1)} %get-tuple-element.48), kind=kLoop, calls=%fused_computation.4 | loop fusion | flops 18874368 | bytes 12582912 | tf_op jit(solution)/shard_map/concatenate | solution.py:107
  162.7 5.9 %fusion.18 = (f32[256]{0:T(256)S(1)}, f32[256,192]{0,1:T(8,128)S(1)}, f32[256,192]{0,1:T(8,128)S(1)}) fusion(f32[256,64]{0,1:T(8,128)S(1)} %tile.17, f32[192]{0:T(256)S(1)} %sub.126, f32[256]{0:T(256)S(1)} %mul.66, bf16[256,16384]{1,0:T(8,128)(2,1)} %bitcast.2.xa_ref, bf16[64,16384]{1,0:T(8,128)(2,1)S(1)} %copy-done.2, bf16[64,16384]{1,0:T(8,128)(2,1)S(1)} %copy-done, ...), kind=kOutput, calls=%fused_computation.59 | convolution fusion | flops 1629732608 | bytes 15141632 | tf_op jit(solution)/shard_map/dot_general | solution.py:115
  168.7 0.2 add.142
  169.0 0.7 fusion.7
  169.8 0.4 multiply_reduce_fusion.1
  170.3 15.7 %all-to-all-done.2 = bf16[32,2,16384]{2,1,0:T(2,128)(2,1)} async-done(((bf16[32,2,16384]{2,1,0:T(2,128)(2,1)}), bf16[32,2,16384]{2,1,0:T(2,128)(2,1)}, u32[]{:S(2)}, u32[]{:S(2)}) %all-to-all-start.2) | async-done | bytes 2097184 | tf_op jit(solution)/shard_map/all_to_all | solution.py:101
  186.0 2.7 %reshape.287 = bf16[64,16384,1]{1,0,2:T(8,128)(2,1)S(1)} reshape(bf16[32,2,16384]{2,1,0:T(2,128)(2,1)} %all-to-all-done.2) | data formatting | bytes 4194304 | tf_op jit(solution)/shard_map/reshape | solution.py:101
  188.8 4.6 %fusion.24 = (f32[64]{0:T(128)S(1)}, f32[64,3,64]{0,2,1:T(8,128)S(1)}) fusion(f32[64,64]{0,1:T(8,128)S(1)} %bitcast.36, f32[64]{0:T(128)S(1)} %broadcast_multiply_fusion, bf16[64,16384,1]{1,0,2:T(8,128)(2,1)S(1)} %reshape.287, bf16[3,64,16384]{2,1,0:T(8,128)(2,1)} %bitcast.33, f32[64]{0:T(128)S(1)} %mul.76), kind=kOutput, calls=%fused_computation.65 | convolution fusion | flops 402714560 | bytes 8454912 | tf_op jit(solution)/shard_map/dot_general | solution.py:115
  193.4 0.2 add.143
  193.6 0.8 fusion.15
  194.3 0.7 add.141
  195.0 5.1 %all-to-all-start.5 = ((f32[4,1,16]{2,1,0:T(1,128)}), f32[4,1,16]{2,1,0:T(1,128)S(1)}, u32[]{:S(2)}, u32[]{:S(2)}) async-start(f32[4,1,16]{2,1,0:T(1,128)} %bitcast.14), calls=%async_computation.5 | async-start | bytes 4096 | tf_op jit(solution)/shard_map/all_to_all | solution.py:155
  200.3 0.1 maximum_maximum_fusion
  200.4 0.8 reshape.290
  201.2 4.1 %reshape.272.xb_ref = bf16[64,16384]{1,0:T(8,128)(2,1)} reshape(bf16[32,2,16384]{2,1,0:T(2,128)(2,1)} %all-to-all-done.2) | data formatting | bytes 4194304 | tf_op jit(solution)/shard_map/reshape | solution.py:101
  205.3 3.8 %all-to-all-start.3 = ((f32[32,1,330]{2,1,0:T(1,128)}), f32[32,1,330]{2,1,0:T(1,128)S(1)}, u32[]{:S(2)}, u32[]{:S(2)}) async-start(f32[32,1,330]{2,1,0:T(1,128)} %reshape.290), calls=%async_computation.3 | async-start | bytes 98304 | tf_op jit(solution)/shard_map/all_to_all | solution.py:145
  209.2 9.9 %shard_map.93 = bf16[64,16384]{1,0:T(8,128)(2,1)} custom-call(bf16[192,256]{1,0:T(8,128)(2,1)} %get-tuple-element.47.wa_ref, bf16[256,16384]{1,0:T(8,128)(2,1)} %bitcast.2.xa_ref, bf16[192,64]{1,0:T(8,128)(2,1)} %bitcast.38, bf16[64,16384]{1,0:T(8,128)(2,1)} %reshape.272.xb_ref), custom_call_target="tpu_custom_call" | custom-call | flops 2013265920 | bytes 12705792 | tf_op jit(solution)/shard_map/pallas_call | solution.py:52
  219.1 4.8 %all-to-all-start.4 = ((bf16[4,16,16384]{2,1,0:T(8,128)(2,1)}), bf16[4,16,16384]{2,1,0:T(8,128)(2,1)S(1)}, u32[]{:S(2)}, u32[]{:S(2)}) async-start(bf16[4,16,16384]{2,1,0:T(8,128)(2,1)} %bitcast.34), calls=%async_computation.4 | async-start | bytes 4194304 | tf_op jit(solution)/shard_map/all_to_all | solution.py:152
  224.0 0.6 copy.44
  224.6 0.5 broadcast.175
  225.1 0.8 reduce.10
  225.9 0.1 reshape.291
  226.1 0.7 gather_fusion
  226.8 0.7 copy.43
  227.5 0.7 slice_reduce_fusion
  228.2 22.3 %all-to-all-done.4 = bf16[4,16,16384]{2,1,0:T(8,128)(2,1)S(1)} async-done(((bf16[4,16,16384]{2,1,0:T(8,128)(2,1)}), bf16[4,16,16384]{2,1,0:T(8,128)(2,1)S(1)}, u32[]{:S(2)}, u32[]{:S(2)}) %all-to-all-start.4) | async-done | bytes 2097184 | tf_op jit(solution)/shard_map/all_to_all | solution.py:152
  250.5 0.6 reduce_sum.135
  251.2 1.1 reshape.276
  (59 shorter events, 2.2 us)
Async XLA Ops:
  7.2 39.1 %all-gather.2.cloned.1.call-start = ((), (), s32[]{:S(2)}) async-start(), calls=%async_computation.6 | async-start | bytes 2621440 | tf_op jit(solution)/shard_map/all_gather | solution.py:104
  13.3 24.6 %all-to-all-start = ((f32[32,2,10]{2,1,0:T(2,128)}), f32[32,2,10]{2,1,0:T(2,128)S(1)}, u32[]{:S(2)}, u32[]{:S(2)}) async-start(f32[32,2,10]{2,1,0:T(2,128)} %copy.37), calls=%async_computation | async-start | bytes 65536 | tf_op jit(solution)/shard_map/all_to_all | solution.py:93
  35.2 2.7 %copy-start.5 = (s32[2]{0:T(128)S(1)}, s32[2]{0:T(128)}, u32[]{:S(2)}) copy-start(s32[2]{0:T(128)} %param.11) | copy-start | bytes 28
  37.9 113.4 %all-to-all-start.1 = ((bf16[32,8,16384]{2,1,0:T(8,128)(2,1)}), bf16[32,8,16384]{2,1,0:T(8,128)(2,1)}, u32[]{:S(2)}, u32[]{:S(2)}) async-start(bf16[32,8,16384]{2,1,0:T(8,128)(2,1)} %fusion), calls=%async_computation.1 | async-start | bytes 16777216 | tf_op jit(solution)/shard_map/all_to_all | solution.py:94
  46.2 5.0 %copy-start = (bf16[64,16384]{1,0:T(8,128)(2,1)S(1)}, bf16[64,16384]{1,0:T(8,128)(2,1)}, u32[]{:S(2)}) copy-start(bf16[64,16384]{1,0:T(8,128)(2,1)} %all-gather.2.cloned.1.call-done) | copy-start | bytes 6291460
  52.1 1.6 copy-start.3
  52.1 2.2 copy-start.4
  151.3 34.7 %all-to-all-start.2 = ((bf16[32,2,16384]{2,1,0:T(2,128)(2,1)}), bf16[32,2,16384]{2,1,0:T(2,128)(2,1)}, u32[]{:S(2)}, u32[]{:S(2)}) async-start(bf16[32,2,16384]{2,1,0:T(2,128)(2,1)} %reshape.270), calls=%async_computation.2 | async-start | bytes 4194304 | tf_op jit(solution)/shard_map/all_to_all | solution.py:101
  156.2 6.5 %copy-start.1 = (bf16[64,16384]{1,0:T(8,128)(2,1)S(1)}, bf16[64,16384]{1,0:T(8,128)(2,1)}, u32[]{:S(2)}) copy-start(bf16[64,16384]{1,0:T(8,128)(2,1)} %get-tuple-element.48) | copy-start | bytes 6291460
  156.2 6.5 %copy-start.2 = (bf16[64,16384]{1,0:T(8,128)(2,1)S(1)}, bf16[64,16384]{1,0:T(8,128)(2,1)}, u32[]{:S(2)}) copy-start(bf16[64,16384]{1,0:T(8,128)(2,1)} %get-tuple-element.49) | copy-start | bytes 6291460
  195.0 10.3 %all-to-all-start.5 = ((f32[4,1,16]{2,1,0:T(1,128)}), f32[4,1,16]{2,1,0:T(1,128)S(1)}, u32[]{:S(2)}, u32[]{:S(2)}) async-start(f32[4,1,16]{2,1,0:T(1,128)} %bitcast.14), calls=%async_computation.5 | async-start | bytes 4096 | tf_op jit(solution)/shard_map/all_to_all | solution.py:155
  205.3 13.8 %all-to-all-start.3 = ((f32[32,1,330]{2,1,0:T(1,128)}), f32[32,1,330]{2,1,0:T(1,128)S(1)}, u32[]{:S(2)}, u32[]{:S(2)}) async-start(f32[32,1,330]{2,1,0:T(1,128)} %reshape.290), calls=%async_computation.3 | async-start | bytes 98304 | tf_op jit(solution)/shard_map/all_to_all | solution.py:145
  219.1 31.5 %all-to-all-start.4 = ((bf16[4,16,16384]{2,1,0:T(8,128)(2,1)}), bf16[4,16,16384]{2,1,0:T(8,128)(2,1)S(1)}, u32[]{:S(2)}, u32[]{:S(2)}) async-start(bf16[4,16,16384]{2,1,0:T(8,128)(2,1)} %bitcast.34), calls=%async_computation.4 | async-start | bytes 4194304 | tf_op jit(solution)/shard_map/all_to_all | solution.py:152
Sparse Core Ops, SparseCore 0:
  10.2 33.5 all-gather.1

commit v3 on v2

--- a/solution.py
+++ b/solution.py
@@ -30,38 +30,83 @@
     return jnp.where(keep, near, far)
 
 
-def sums_kernel(offsets, rows, wa_ref, xa_ref, wb_ref, xb_ref, out_ref):
-    y = jnp.dot(wa_ref[...], xa_ref[...], preferred_element_type=jnp.float32)
-    y = y + jnp.dot(wb_ref[...], xb_ref[...], preferred_element_type=jnp.float32)
+def rolled_sum(y, rows, offsets, lanes):
+    acc = None
+    for u, t in enumerate(offsets):
+        blk = y[u * rows:(u + 1) * rows, lanes * IMG:(lanes + 1) * IMG]
+        if t % IMG:
+            blk = pltpu.roll(blk, shift=t % IMG, axis=1)
+        acc = blk if acc is None else acc + blk
+    return acc
+
+
+def first_sums_kernel(offsets, rows, w_ref, x_ref, out_ref):
+    y = jnp.dot(w_ref[...], x_ref[...], preferred_element_type=jnp.float32)
     for j in range(out_ref.shape[1] // IMG):
-        acc = None
-        for u, t in enumerate(offsets):
-            blk = y[u * rows:(u + 1) * rows, j * IMG:(j + 1) * IMG]
-            if t % IMG:
-                blk = pltpu.roll(blk, shift=t % IMG, axis=1)
-            acc = blk if acc is None else acc + blk
-        out_ref[:, j * IMG:(j + 1) * IMG] = acc.astype(out_ref.dtype)
-
-
-def class_image_sums(wa, xa, wb, xb, offsets):
-    rows = wa.shape[0] // len(offsets)
-    pixels = xa.shape[1]
+        out_ref[:, j * IMG:(j + 1) * IMG] = rolled_sum(y, rows, offsets, j)
+
+
+def last_sums_kernel(offsets, rows, chunk, w_ref, x_ref, acc_ref, tail_ref, out_ref):
+    k = pl.program_id(0)
+    y = jnp.dot(w_ref[...], x_ref[...], preferred_element_type=jnp.float32)
+    for j in range(chunk // IMG):
+        total = acc_ref[:, j * IMG:(j + 1) * IMG] + rolled_sum(y, rows, offsets, j)
+        out_ref[:, pl.ds(k * chunk + j * IMG, IMG)] = total.astype(out_ref.dtype)
+    pixels = out_ref.shape[1] - tail_ref.shape[1]
+    out_ref[:, pixels:] = tail_ref[...]
+
+
+def first_sums(w, x, offsets):
+    rows = w.shape[0] // len(offsets)
+    pixels = x.shape[1]
     chunk = min(CHUNK, pixels)
-    flops = 2 * wa.shape[0] * pixels * (xa.shape[0] + xb.shape[0])
-    bytes_accessed = 2 * (xa.size + xb.size + wa.size + wb.size + rows * pixels)
     return pl.pallas_call(
-        functools.partial(sums_kernel, tuple(offsets), rows),
+        functools.partial(first_sums_kernel, tuple(offsets), rows),
         grid=(pixels // chunk,),
         in_specs=[
-            pl.BlockSpec(wa.shape, lambda k: (0, 0)),
-            pl.BlockSpec((xa.shape[0], chunk), lambda k: (0, k)),
-            pl.BlockSpec(wb.shape, lambda k: (0, 0)),
-            pl.BlockSpec((xb.shape[0], chunk), lambda k: (0, k)),
+            pl.BlockSpec(w.shape, lambda k: (0, 0)),
+            pl.BlockSpec((x.shape[0], chunk), lambda k: (0, k)),
         ],
         out_specs=pl.BlockSpec((rows, chunk), lambda k: (0, k)),
-        out_shape=jax.ShapeDtypeStruct((rows, pixels), jnp.bfloat16),
-        cost_estimate=pl.CostEstimate(flops=flops, transcendentals=0, bytes_accessed=bytes_accessed),
-    )(wa, xa, wb, xb)
+        out_shape=jax.ShapeDtypeStruct((rows, pixels), jnp.float32),
+        cost_estimate=pl.CostEstimate(
+            flops=2 * w.shape[0] * pixels * x.shape[0],
+            transcendentals=0,
+            bytes_accessed=2 * (x.size + w.size) + 4 * rows * pixels,
+        ),
+    )(w, x)
+
+
+def last_sums(w, x, acc, tail, offsets):
+    rows = w.shape[0] // len(offsets)
+    pixels = x.shape[1]
+    chunk = min(CHUNK, pixels)
+    width = pixels + tail.shape[1]
+    return pl.pallas_call(
+        functools.partial(last_sums_kernel, tuple(offsets), rows, chunk),
+        grid=(pixels // chunk,),
+        in_specs=[
+            pl.BlockSpec(w.shape, lambda k: (0, 0)),
+            pl.BlockSpec((x.shape[0], chunk), lambda k: (0, k)),
+            pl.BlockSpec((rows, chunk), lambda k: (0, k)),
+            pl.BlockSpec(tail.shape, lambda k: (0, 0)),
+        ],
+        out_specs=pl.BlockSpec((rows, width), lambda k: (0, 0)),
+        out_shape=jax.ShapeDtypeStruct((rows, width), jnp.bfloat16),
+        cost_estimate=pl.CostEstimate(
+            flops=2 * w.shape[0] * pixels * x.shape[0],
+            transcendentals=0,
+            bytes_accessed=2 * (x.size + w.size + rows * width) + 4 * rows * pixels,
+        ),
+    )(w, x, acc, tail)
+
+
+def split_bf16(values):
+    hi = values.astype(jnp.bfloat16)
+    rest = values - hi.astype(jnp.float32)
+    mid = rest.astype(jnp.bfloat16)
+    lo = (rest - mid.astype(jnp.float32)).astype(jnp.bfloat16)
+    return [hi, mid, lo]
 
 
 def shards(particles, noise_prec, prior_pose, owners, projections, pose_index):
@@ -101,7 +146,8 @@
         got_b = lax.all_to_all(send_b, "dom", 0, 0, tiled=True).reshape(count_dom * rows_b, pixels)
 
     own_proj = projections.reshape(-1, pixels)
-    all_proj = lax.all_gather(own_proj, "ref", axis=0, tiled=True)
+    spread = jnp.broadcast_to(own_proj[None], (count_ref,) + own_proj.shape)
+    all_proj = lax.all_to_all(spread, "ref", 0, 0, tiled=True).reshape(-1, pixels)
     rows = all_proj.shape[0]
     offsets = [u - SHIFTS // 2 for u in range(SHIFTS)]
     shifted = jnp.concatenate([translate(all_proj, -t) for t in offsets], axis=0)
@@ -133,6 +179,7 @@
     low_a, tot_a, post_a = part(
         got_a, meta_prec[:, :rows_a].reshape(-1), meta_prior[:, :rows_a].reshape(-1)
     )
+    sums_a = first_sums(low_a, got_a, offsets)
     post_width = post_a.shape[1]
     back = [post_a.reshape(count_dom, rows_a, post_width)]
     if rows_b:
@@ -147,12 +194,16 @@
     if not rows_b:
         low_b = jnp.zeros((SHIFTS * rows, 8), jnp.bfloat16)
         got_b = jnp.zeros((8, pixels), particles.dtype)
-    image_sums = class_image_sums(low_a, got_a, low_b, got_b, offsets)
-    partial = image_sums.reshape(count_ref, rows // count_ref, pixels)
-    got_partial = lax.all_to_all(partial, "ref", 0, 0, tiled=True)
-    class_sums = jnp.sum(got_partial.astype(f32), axis=0).astype(jnp.bfloat16)
+    pieces = split_bf16(tot_a)
+    tail = jnp.zeros((rows, IMG), jnp.bfloat16)
+    for q, piece in enumerate(pieces):
+        tail = tail.at[:, q].set(piece)
+    image_sums = last_sums(low_b, got_b, sums_a, tail, offsets)
+    partial = image_sums.reshape(count_ref, rows // count_ref, pixels + IMG)
+    got_partial = lax.all_to_all(partial, "ref", 0, 0, tiled=True).astype(f32)
+    class_sums = jnp.sum(got_partial[:, :, :pixels], axis=0).astype(jnp.bfloat16)
     class_sums = class_sums.reshape(projections.shape)
-    got_tot = lax.all_to_all(tot_a.reshape(count_ref, rows // count_ref), "ref", 0, 0, tiled=True)
+    got_tot = got_partial[:, :, pixels] + got_partial[:, :, pixels + 1] + got_partial[:, :, pixels + 2]
     weight_totals = jnp.sum(got_tot, axis=0).reshape(projections.shape[0], projections.shape[1])
 
     mine = got_back[owners * capacity + slot_rank]

time: 260 us -> 272 us (1.046)
  waiting for transfers between devices: 129 us -> 150 us
  between operations: 14.3 us -> 1.01 us
  Pallas kernels: 9.9 us -> 17.8 us
  other arithmetic: 19.9 us -> 23.9 us
  matrix products: 24.9 us -> 21.1 us
  local copies, waits for them, and re-layouts: 27.6 us -> 24.7 us
    all_to_all x2, waiting for transfers between devices: 22.3 us -> 49.3 us  [the longest x1 25.9 us: shards(): lax.all_to_all(spread, 'ref', 0, 0, tiled=True).reshape(-1, pixels)]
    all_to_all x1, waiting for transfers between devices: 15.7 us -> 6.39 us  [shards(): lax.all_to_all(send_b, 'dom', 0, 0, tiled=True)]
    pallas_call x1 -> x2, Pallas kernels: 9.9 us -> 17.8 us  [the longest x1 9.28 us: first_sums(): pl.pallas_call(functools.partial(first_sums_kernel, tuple(offsets), rows)...]
    another operation x0 -> x5, other arithmetic: none -> 3.93 us
    dot_general x1, matrix products: 5.03 us -> 1.57 us  [shards(): jnp.dot(pick_b.astype(particles.dtype), particles, preferred_element_type...]
    reshape x2 -> x0, local copies, waits for them, and re-layouts: 3.17 us -> none  [the longest x1 2.03 us: shards(): own_proj = projections.reshape(-1, pixels)]
    all_to_all x1, waiting for transfers between devices: 91 us -> 94 us  [shards(): lax.all_to_all(send_a, 'dom', 0, 0, tiled=True)]
  transfers between devices with their start and end apart: 7 -> 6, of which waited for: 3 -> 4; matrix products, arithmetic and copies ran while one was open for 22% -> 19% of each run, Pallas kernels for 4% -> 7%
where the time goes in v3:
time: 272 us; the launch traced here: 271 us
  waiting for transfers between devices  150 us (55%)
  starting transfers between devices  32.5 us (12%)
  local copies, waits for them, and re-layouts  24.7 us (9%)
  other arithmetic  23.9 us (9%)
  matrix products  21.1 us (8%)
  Pallas kernels  17.8 us (7%)
    all_to_all x1, waiting for transfers between devices, shards(): lax.all_to_all(send_a, 'dom', 0, 0, tiled=True)  94 us
    all_to_all x1, waiting for transfers between devices, shards(): lax.all_to_all(spread, 'ref', 0, 0, tiled=True).reshape(-1, pixels)  25.9 us
    all_to_all x1, waiting for transfers between devices, shards(): got_partial = lax.all_to_all(partial, 'ref', 0, 0, tiled=True).astype(f32)  23.4 us
    dot_general x2, matrix products, part(): lax.dot_general(images, shifted, (((1,), (1,)), ((), ())), preferred_elem...  10.5 us
    pallas_call x1, Pallas kernels, first_sums(): pl.pallas_call(functools.partial(first_sums_kernel, tuple(offsets), rows)...  9.28 us
    dot_general x1, matrix products, shards(): jnp.dot(pick_a.astype(particles.dtype), particles, preferred_element_type...  9.08 us
    pallas_call x1, Pallas kernels, last_sums(): pl.pallas_call(functools.partial(last_sums_kernel, tuple(offsets), rows,...  8.53 us
    all_to_all x1, starting transfers between devices, shards(): got_meta = lax.all_to_all(meta, 'dom', 0, 0, tiled=True)  7.4 us
  transfers between devices with their start and end apart: 6, of which 4 were waited for; matrix products, arithmetic and copies ran while one was open for 19% of the time, Pallas kernels for 7%

profile of v3, /device:TPU:0, one launch (start us, length us, event | category | flops | bytes accessed | tf_op | source)
XLA Modules:
  0.0 270.8 jit_solution(3369259014872843909)
XLA Ops:
  0.6 0.9 convert_reduce_fusion
  1.6 0.7 compare_select_fusion
  2.3 0.7 convert_add_fusion
  2.9 0.7 convert_element_type.108
  4.0 0.6 copy.43
  4.7 7.4 %all-to-all-start = ((f32[32,2,10]{2,1,0:T(2,128)}), f32[32,2,10]{2,1,0:T(2,128)S(1)}, u32[]{:S(2)}, u32[]{:S(2)}) async-start(f32[32,2,10]{2,1,0:T(2,128)} %copy.43), calls=%async_computation | async-start | bytes 65536 | tf_op jit(solution)/shard_map/all_to_all | solution.py:138
  12.1 9.1 %fusion = bf16[32,8,16384]{2,1,0:T(8,128)(2,1)} fusion(bf16[256,16384]{1,0:T(8,128)(2,1)} %param.12, s32[256]{0:T(256)S(1)} %get-tuple-element.91), kind=kOutput, calls=%fused_computation.2 | convolution fusion | flops 2151743488 | bytes 16778240 | tf_op jit(solution)/shard_map/dot_general | solution.py:130
  21.2 1.6 convolution_convert_fusion.1
  23.0 2.7 reshape.365
  25.7 0.6 compare_reduce_fusion.1
  26.3 0.6 compare_reduce_fusion.2
  27.0 0.6 compare_reduce_fusion
  27.6 1.5 broadcast_in_dim.35
  29.1 5.3 %all-to-all-start.2 = ((bf16[4,16,16384]{2,1,0:T(8,128)(2,1)}), bf16[4,16,16384]{2,1,0:T(8,128)(2,1)S(1)}, u32[]{:S(2)}, u32[]{:S(2)}) async-start(bf16[4,16,16384]{2,1,0:T(8,128)(2,1)} %broadcast_in_dim.35), calls=%async_computation.2 | async-start | bytes 4194304 | tf_op jit(solution)/shard_map/all_to_all | solution.py:150
  35.3 25.9 %all-to-all-done.2 = bf16[4,16,16384]{2,1,0:T(8,128)(2,1)S(1)} async-done(((bf16[4,16,16384]{2,1,0:T(8,128)(2,1)}), bf16[4,16,16384]{2,1,0:T(8,128)(2,1)S(1)}, u32[]{:S(2)}, u32[]{:S(2)}) %all-to-all-start.2) | async-done | bytes 2097184 | tf_op jit(solution)/shard_map/all_to_all | solution.py:150
  61.2 7.4 %all-to-all-start.1 = ((bf16[32,8,16384]{2,1,0:T(8,128)(2,1)}), bf16[32,8,16384]{2,1,0:T(8,128)(2,1)}, u32[]{:S(2)}, u32[]{:S(2)}) async-start(bf16[32,8,16384]{2,1,0:T(8,128)(2,1)} %fusion), calls=%async_computation.1 | async-start | bytes 16777216 | tf_op jit(solution)/shard_map/all_to_all | solution.py:139
  68.6 2.7 %fusion.23 = (bf16[64,16257]{1,0:T(8,128)(2,1)}, bf16[64,16257]{1,0:T(8,128)(2,1)}) fusion(bf16[64,16384]{1,0:T(8,128)(2,1)S(1)} %bitcast.35), kind=kLoop, calls=%fused_computation.75 | loop fusion | bytes 8323584 | tf_op jit(solution)/shard_map/jit(_roll_static)/slice | solution.py:24
  71.3 0.5 multiply_reduce_fusion
  72.3 0.7 fusion.26
  73.0 0.9 copy-done.3
  73.9 0.6 copy-done.4
  74.5 6.0 %fusion.1 = (bf16[64,16384]{1,0:T(8,128)(2,1)}, bf16[64,16384]{1,0:T(8,128)(2,1)}) fusion(bf16[64,16383]{1,0:T(8,128)(2,1)S(1)} %get-tuple-element.80, bf16[64,1]{1,0:T(8,128)(2,1)S(1)} %get-tuple-element.78, bf16[64,127]{1,0:T(8,128)(2,1)S(1)} %get-tuple-element.76, bf16[64,16257]{1,0:T(8,128)(2,1)S(1)} %copy-done.3, s32[16384]{0:T(1024)S(1)} %get-tuple-element.96, ...), kind=kLoop, calls=%fused_computation.9 | loop fusion | flops 22020096 | bytes 12730368 | tf_op jit(solution)/shard_map/jit(_where)/select_n | solution.py:30
  80.5 94.0 %all-to-all-done.1 = bf16[32,8,16384]{2,1,0:T(8,128)(2,1)} async-done(((bf16[32,8,16384]{2,1,0:T(8,128)(2,1)}), bf16[32,8,16384]{2,1,0:T(8,128)(2,1)}, u32[]{:S(2)}, u32[]{:S(2)}) %all-to-all-start.1) | async-done | bytes 8388640 | tf_op jit(solution)/shard_map/all_to_all | solution.py:139
  174.4 5.0 %all-to-all-start.3 = ((bf16[32,2,16384]{2,1,0:T(2,128)(2,1)}), bf16[32,2,16384]{2,1,0:T(2,128)(2,1)}, u32[]{:S(2)}, u32[]{:S(2)}) async-start(bf16[32,2,16384]{2,1,0:T(2,128)(2,1)} %reshape.365), calls=%async_computation.3 | async-start | bytes 4194304 | tf_op jit(solution)/shard_map/all_to_all | solution.py:146
  179.4 6.5 %pad_maximum_fusion = bf16[192,16384]{1,0:T(8,128)(2,1)} fusion(bf16[64,16384]{1,0:T(8,128)(2,1)} %get-tuple-element.85, bf16[64,16384]{1,0:T(8,128)(2,1)S(1)} %bitcast.39, bf16[64,16384]{1,0:T(8,128)(2,1)} %get-tuple-element.84), kind=kLoop, calls=%fused_computation.4 | loop fusion | flops 18874368 | bytes 12582912 | tf_op jit(solution)/shard_map/concatenate | solution.py:153
  185.9 5.9 %fusion.22 = (f32[256]{0:T(256)S(1)}, f32[256,192]{0,1:T(8,128)S(1)}, f32[256,192]{0,1:T(8,128)S(1)}) fusion(f32[256,64]{0,1:T(8,128)S(1)} %tile.17, f32[192]{0:T(256)S(1)} %sub.145, f32[256]{0:T(256)S(1)} %mul.66, bf16[256,16384]{1,0:T(8,128)(2,1)} %bitcast.2.x_ref, bf16[64,16384]{1,0:T(8,128)(2,1)S(1)} %copy-done.2, bf16[64,16384]{1,0:T(8,128)(2,1)S(1)} %bitcast.40, ...), kind=kOutput, calls=%fused_computation.74 | convolution fusion | flops 1629732608 | bytes 15141632 | tf_op jit(solution)/shard_map/dot_general | solution.py:161
  192.2 0.7 fusion.7
  193.0 0.4 multiply_reduce_fusion.1
  193.5 9.3 %shard_map.93.acc_ref = f32[64,16384]{1,0:T(8,128)} custom-call(bf16[192,256]{1,0:T(8,128)(2,1)} %get-tuple-element.83.w_ref, bf16[256,16384]{1,0:T(8,128)(2,1)} %bitcast.2.x_ref), custom_call_target="tpu_custom_call" | custom-call | flops 1610612736 | bytes 12681216 | tf_op jit(solution)/shard_map/pallas_call | solution.py:63
  202.8 6.4 %all-to-all-done.3 = bf16[32,2,16384]{2,1,0:T(2,128)(2,1)} async-done(((bf16[32,2,16384]{2,1,0:T(2,128)(2,1)}), bf16[32,2,16384]{2,1,0:T(2,128)(2,1)}, u32[]{:S(2)}, u32[]{:S(2)}) %all-to-all-start.3) | async-done | bytes 2097184 | tf_op jit(solution)/shard_map/all_to_all | solution.py:146
  209.2 2.7 %reshape.381 = bf16[64,16384,1]{1,0,2:T(8,128)(2,1)S(1)} reshape(bf16[32,2,16384]{2,1,0:T(2,128)(2,1)} %all-to-all-done.3) | data formatting | bytes 4194304 | tf_op jit(solution)/shard_map/reshape | solution.py:146
  212.0 4.6 %fusion.28 = (f32[64]{0:T(128)S(1)}, f32[64,3,64]{0,2,1:T(8,128)S(1)}) fusion(f32[64,64]{0,1:T(8,128)S(1)} %bitcast.44, f32[64]{0:T(128)S(1)} %div.41, bf16[64,16384,1]{1,0,2:T(8,128)(2,1)S(1)} %reshape.381, bf16[3,64,16384]{2,1,0:T(8,128)(2,1)} %bitcast.41, f32[64]{0:T(128)S(1)} %mul.76), kind=kOutput, calls=%fused_computation.80 | convolution fusion | flops 402714560 | bytes 8454912 | tf_op jit(solution)/shard_map/dot_general | solution.py:161
  216.8 0.8 fusion.15
  217.9 0.8 reshape.384
  218.7 3.8 %all-to-all-start.4 = ((f32[32,1,330]{2,1,0:T(1,128)}), f32[32,1,330]{2,1,0:T(1,128)S(1)}, u32[]{:S(2)}, u32[]{:S(2)}) async-start(f32[32,1,330]{2,1,0:T(1,128)} %reshape.384), calls=%async_computation.4 | async-start | bytes 98304 | tf_op jit(solution)/shard_map/all_to_all | solution.py:192
  222.6 1.3 fusion.20
  224.0 0.7 fusion.21
  224.9 4.1 %reshape.367.x_ref = bf16[64,16384]{1,0:T(8,128)(2,1)} reshape(bf16[32,2,16384]{2,1,0:T(2,128)(2,1)} %all-to-all-done.3) | data formatting | bytes 4194304 | tf_op jit(solution)/shard_map/reshape | solution.py:146
  229.0 8.5 %shard_map.94 = bf16[64,16512]{1,0:T(8,128)(2,1)} custom-call(bf16[192,64]{1,0:T(8,128)(2,1)} %bitcast.46, bf16[64,16384]{1,0:T(8,128)(2,1)} %reshape.367.x_ref, f32[64,16384]{1,0:T(8,128)} %shard_map.93.acc_ref, bf16[64,128]{1,0:T(8,128)(2,1)} %copy-done.6), custom_call_target="tpu_custom_call" | custom-call | flops 402653184 | bytes 8429568 | tf_op jit(solution)/shard_map/pallas_call | solution.py:85
  237.5 3.6 %all-to-all-start.5 = ((bf16[4,16,16512]{2,1,0:T(8,128)(2,1)}), bf16[4,16,16512]{2,1,0:T(8,128)(2,1)S(1)}, u32[]{:S(2)}, u32[]{:S(2)}) async-start(bf16[4,16,16512]{2,1,0:T(8,128)(2,1)} %bitcast.42), calls=%async_computation.5 | async-start | bytes 4227072 | tf_op jit(solution)/shard_map/all_to_all | solution.py:203
  241.2 0.5 broadcast.271
  241.7 0.8 reduce.34
  242.6 0.7 gather_fusion
  243.3 0.7 copy.50
  244.0 0.7 slice_reduce_fusion.1
  244.8 23.4 %all-to-all-done.5 = bf16[4,16,16512]{2,1,0:T(8,128)(2,1)S(1)} async-done(((bf16[4,16,16512]{2,1,0:T(8,128)(2,1)}), bf16[4,16,16512]{2,1,0:T(8,128)(2,1)S(1)}, u32[]{:S(2)}, u32[]{:S(2)}) %all-to-all-start.5) | async-done | bytes 2113568 | tf_op jit(solution)/shard_map/all_to_all | solution.py:203
  268.9 1.1 convert_element_type.125
  270.1 0.6 copy.51
  (72 shorter events, 4.3 us)
Async XLA Ops:
  4.7 22.9 %all-to-all-start = ((f32[32,2,10]{2,1,0:T(2,128)}), f32[32,2,10]{2,1,0:T(2,128)S(1)}, u32[]{:S(2)}, u32[]{:S(2)}) async-start(f32[32,2,10]{2,1,0:T(2,128)} %copy.43), calls=%async_computation | async-start | bytes 65536 | tf_op jit(solution)/shard_map/all_to_all | solution.py:138
  12.1 9.1 %copy-start = (bf16[256,16384]{1,0:T(8,128)(2,1)S(1)}, bf16[256,16384]{1,0:T(8,128)(2,1)}, u32[]{:S(2)}) copy-start(bf16[256,16384]{1,0:T(8,128)(2,1)} %param.12) | copy-start | bytes 25165828
  21.2 1.6 copy-start.5
  22.8 2.9 %copy-start.7 = (s32[2]{0:T(128)S(1)}, s32[2]{0:T(128)}, u32[]{:S(2)}) copy-start(s32[2]{0:T(128)} %param.17) | copy-start | bytes 28
  29.1 32.1 %all-to-all-start.2 = ((bf16[4,16,16384]{2,1,0:T(8,128)(2,1)}), bf16[4,16,16384]{2,1,0:T(8,128)(2,1)S(1)}, u32[]{:S(2)}, u32[]{:S(2)}) async-start(bf16[4,16,16384]{2,1,0:T(8,128)(2,1)} %broadcast_in_dim.35), calls=%async_computation.2 | async-start | bytes 4194304 | tf_op jit(solution)/shard_map/all_to_all | solution.py:150
  61.2 113.3 %all-to-all-start.1 = ((bf16[32,8,16384]{2,1,0:T(8,128)(2,1)}), bf16[32,8,16384]{2,1,0:T(8,128)(2,1)}, u32[]{:S(2)}, u32[]{:S(2)}) async-start(bf16[32,8,16384]{2,1,0:T(8,128)(2,1)} %fusion), calls=%async_computation.1 | async-start | bytes 16777216 | tf_op jit(solution)/shard_map/all_to_all | solution.py:139
  72.3 1.6 copy-start.3
  72.3 2.2 copy-start.4
  174.4 34.7 %all-to-all-start.3 = ((bf16[32,2,16384]{2,1,0:T(2,128)(2,1)}), bf16[32,2,16384]{2,1,0:T(2,128)(2,1)}, u32[]{:S(2)}, u32[]{:S(2)}) async-start(bf16[32,2,16384]{2,1,0:T(2,128)(2,1)} %reshape.365), calls=%async_computation.3 | async-start | bytes 4194304 | tf_op jit(solution)/shard_map/all_to_all | solution.py:146
  179.4 6.5 %copy-start.1 = (bf16[64,16384]{1,0:T(8,128)(2,1)S(1)}, bf16[64,16384]{1,0:T(8,128)(2,1)}, u32[]{:S(2)}) copy-start(bf16[64,16384]{1,0:T(8,128)(2,1)} %get-tuple-element.84) | copy-start | bytes 6291460
  179.4 6.5 %copy-start.2 = (bf16[64,16384]{1,0:T(8,128)(2,1)S(1)}, bf16[64,16384]{1,0:T(8,128)(2,1)}, u32[]{:S(2)}) copy-start(bf16[64,16384]{1,0:T(8,128)(2,1)} %get-tuple-element.85) | copy-start | bytes 6291460
  218.7 18.8 %all-to-all-start.4 = ((f32[32,1,330]{2,1,0:T(1,128)}), f32[32,1,330]{2,1,0:T(1,128)S(1)}, u32[]{:S(2)}, u32[]{:S(2)}) async-start(f32[32,1,330]{2,1,0:T(1,128)} %reshape.384), calls=%async_computation.4 | async-start | bytes 98304 | tf_op jit(solution)/shard_map/all_to_all | solution.py:192
  224.9 4.1 %copy-start.6 = (bf16[64,128]{1,0:T(8,128)(2,1)}, bf16[64,128]{1,0:T(8,128)(2,1)S(1)}, u32[]{:S(2)}) copy-start(bf16[64,128]{1,0:T(8,128)(2,1)S(1)} %scatter.14.tail_ref) | copy-start | bytes 49156
  237.5 30.7 %all-to-all-start.5 = ((bf16[4,16,16512]{2,1,0:T(8,128)(2,1)}), bf16[4,16,16512]{2,1,0:T(8,128)(2,1)S(1)}, u32[]{:S(2)}, u32[]{:S(2)}) async-start(bf16[4,16,16512]{2,1,0:T(8,128)(2,1)} %bitcast.42), calls=%async_computation.5 | async-start | bytes 4227072 | tf_op jit(solution)/shard_map/all_to_all | solution.py:203

commit v4 on v3

--- a/solution.py
+++ b/solution.py
@@ -109,6 +109,11 @@
     return [hi, mid, lo]
 
 
+def ahead(block, axis, distance):
+    size = lax.axis_size(axis)
+    return lax.ppermute(block, axis, [(i, (i + distance) % size) for i in range(size)])
+
+
 def shards(particles, noise_prec, prior_pose, owners, projections, pose_index):
     f32 = jnp.float32
     count_dom = lax.axis_size("dom")
@@ -146,8 +151,13 @@
         got_b = lax.all_to_all(send_b, "dom", 0, 0, tiled=True).reshape(count_dom * rows_b, pixels)
 
     own_proj = projections.reshape(-1, pixels)
-    spread = jnp.broadcast_to(own_proj[None], (count_ref,) + own_proj.shape)
-    all_proj = lax.all_to_all(spread, "ref", 0, 0, tiled=True).reshape(-1, pixels)
+    ref_here = lax.axis_index("ref")
+    blocks = jnp.zeros((count_ref,) + own_proj.shape, own_proj.dtype)
+    blocks = lax.dynamic_update_index_in_dim(blocks, own_proj, ref_here, 0)
+    for k in range(1, count_ref):
+        moved = ahead(own_proj, "ref", k)
+        blocks = lax.dynamic_update_index_in_dim(blocks, moved, (ref_here - k) % count_ref, 0)
+    all_proj = blocks.reshape(-1, pixels)
     rows = all_proj.shape[0]
     offsets = [u - SHIFTS // 2 for u in range(SHIFTS)]
     shifted = jnp.concatenate([translate(all_proj, -t) for t in offsets], axis=0)
@@ -200,7 +210,11 @@
         tail = tail.at[:, q].set(piece)
     image_sums = last_sums(low_b, got_b, sums_a, tail, offsets)
     partial = image_sums.reshape(count_ref, rows // count_ref, pixels + IMG)
-    got_partial = lax.all_to_all(partial, "ref", 0, 0, tiled=True).astype(f32)
+    pieces = [lax.dynamic_index_in_dim(partial, ref_here, 0, keepdims=False)]
+    for k in range(1, count_ref):
+        outgoing = lax.dynamic_index_in_dim(partial, (ref_here + k) % count_ref, 0, keepdims=False)
+        pieces.append(ahead(outgoing, "ref", k))
+    got_partial = jnp.stack(pieces).astype(f32)
     class_sums = jnp.sum(got_partial[:, :, :pixels], axis=0).astype(jnp.bfloat16)
     class_sums = class_sums.reshape(projections.shape)
     got_tot = got_partial[:, :, pixels] + got_partial[:, :, pixels + 1] + got_partial[:, :, pixels + 2]

time: 272 us -> 251 us (0.923)
  waiting for transfers between devices: 150 us -> 109 us
  local copies, waits for them, and re-layouts: 24.7 us -> 33.3 us
  matrix products: 21.1 us -> 25.7 us
  other arithmetic: 23.9 us -> 28.2 us
    all_to_all x2 -> x0, waiting for transfers between devices: 49.3 us -> none  [the longest x1 25.9 us: shards(): lax.all_to_all(spread, 'ref', 0, 0, tiled=True).reshape(-1, pixels)]
    ppermute x0 -> x6, starting transfers between devices: none -> 10.4 us  [ahead(): lax.ppermute(block, axis, [(i, (i + distance) % size) for i in range(size)])]
    all_to_all x2 -> x0, starting transfers between devices: 8.92 us -> none  [the longest x1 5.31 us: shards(): lax.all_to_all(spread, 'ref', 0, 0, tiled=True).reshape(-1, pixels)]
    all_to_all x1, waiting for transfers between devices: 0.01 us -> 7.43 us  [shards(): lax.all_to_all(back, 'dom', 0, 0, tiled=True)]
    dot_general x1, matrix products: 1.57 us -> 6.3 us  [shards(): jnp.dot(pick_b.astype(particles.dtype), particles, preferred_element_type...]
    ppermute x0 -> x6, waiting for transfers between devices: none -> 4.69 us  [ahead(): lax.ppermute(block, axis, [(i, (i + distance) % size) for i in range(size)])]
    all_to_all x1, waiting for transfers between devices: 94 us -> 89.8 us  [shards(): lax.all_to_all(send_a, 'dom', 0, 0, tiled=True)]
    dynamic_update_slice x0 -> x4, local copies, waits for them, and re-layouts: none -> 3.28 us  [the longest x3 3.24 us: shards(): lax.dynamic_update_index_in_dim(blocks, moved, (ref_here - k) % count_ref...]
  transfers between devices with their start and end apart: 6 -> 10, of which waited for: 4 -> 5; matrix products, arithmetic and copies ran while one was open for 19% -> 24% of each run, Pallas kernels for 7% -> 4%
where the time goes in v4:
time: 251 us; the launch traced here: 249 us
  waiting for transfers between devices  109 us (43%)
  starting transfers between devices  34 us (14%)
  local copies, waits for them, and re-layouts  33.3 us (13%)
  other arithmetic  28.2 us (11%)
  matrix products  25.7 us (10%)
  Pallas kernels  17.8 us (7%)
    all_to_all x1, waiting for transfers between devices, shards(): lax.all_to_all(send_a, 'dom', 0, 0, tiled=True)  89.8 us
    dot_general x2, matrix products, part(): lax.dot_general(images, shifted, (((1,), (1,)), ((), ())), preferred_elem...  10.5 us
    ppermute x6, starting transfers between devices, ahead(): lax.ppermute(block, axis, [(i, (i + distance) % size) for i in range(size)])  10.4 us
    pallas_call x1, Pallas kernels, first_sums(): pl.pallas_call(functools.partial(first_sums_kernel, tuple(offsets), rows)...  9.27 us
    dot_general x1, matrix products, shards(): jnp.dot(pick_a.astype(particles.dtype), particles, preferred_element_type...  8.93 us
    pallas_call x1, Pallas kernels, last_sums(): pl.pallas_call(functools.partial(last_sums_kernel, tuple(offsets), rows,...  8.53 us
    all_to_all x1, starting transfers between devices, shards(): lax.all_to_all(send_a, 'dom', 0, 0, tiled=True)  7.69 us
    all_to_all x1, waiting for transfers between devices, shards(): lax.all_to_all(back, 'dom', 0, 0, tiled=True)  7.43 us
  transfers between devices with their start and end apart: 10, of which 5 were waited for; matrix products, arithmetic and copies ran while one was open for 24% of the time, Pallas kernels for 4%

profile of v4, /device:TPU:0, one launch (start us, length us, event | category | flops | bytes accessed | tf_op | source)
XLA Modules:
  0.0 249.4 jit_solution(11409916388984693924)
XLA Ops:
  0.6 1.2 reshape.369
  1.9 2.1 collective-permute-start
  3.9 3.6 %collective-permute-start.1 = (bf16[16,16384]{1,0:T(8,128)(2,1)S(1)}, bf16[16,16384]{1,0:T(8,128)(2,1)}, u32[]{:S(2)}, u32[]{:S(2)}) collective-permute-start(bf16[16,16384]{1,0:T(8,128)(2,1)S(1)} %reshape.369), channel_id=1, source_target_pairs={{0,2},{1,3},{2,0},{3,1},{4,6},{5,7},{6,4},{7,5},{8,10},{9,11},{10,... | collective-permute-start | bytes 1572872 | tf_op jit(solution)/shard_map/ppermute | solution.py:114
  7.5 1.0 collective-permute-start.2
  8.5 0.9 convert_reduce_fusion
  9.5 0.7 compare_select_fusion
  10.2 0.7 convert_add_fusion.2
  12.6 7.3 %all-to-all-start = ((f32[32,2,10]{2,1,0:T(2,128)}), f32[32,2,10]{2,1,0:T(2,128)S(1)}, u32[]{:S(2)}, u32[]{:S(2)}) async-start(f32[32,2,10]{2,1,0:T(2,128)} %copy.43), calls=%async_computation | async-start | bytes 65536 | tf_op jit(solution)/shard_map/all_to_all | solution.py:143
  19.9 1.2 broadcast_in_dim.73
  21.3 8.9 %fusion = bf16[32,8,16384]{2,1,0:T(8,128)(2,1)} fusion(bf16[256,16384]{1,0:T(8,128)(2,1)} %param.12, s32[256]{0:T(256)S(1)} %get-tuple-element.95), kind=kOutput, calls=%fused_computation.2 | convolution fusion | flops 2151743488 | bytes 16778240 | tf_op jit(solution)/shard_map/dot_general | solution.py:135
  30.2 6.3 %convolution_convert_fusion.1 = bf16[64,16384]{1,0:T(8,128)(2,1)} fusion(pred[64,256]{1,0:T(32,128)(4,1)S(1)} %iota_compare_fusion.4, bf16[256,16384]{1,0:T(8,128)(2,1)} %param.12), kind=kOutput, calls=%fused_computation.3 | convolution fusion | flops 537919488 | bytes 10502144 | tf_op jit(solution)/shard_map/dot_general | solution.py:148
  36.7 4.4 %reshape.368 = bf16[32,2,16384]{2,1,0:T(2,128)(2,1)} reshape(bf16[64,16384]{1,0:T(8,128)(2,1)} %convolution_convert_fusion.1) | data formatting | bytes 4194304 | tf_op jit(solution)/shard_map/reshape | solution.py:149
  43.1 7.7 %all-to-all-start.1 = ((bf16[32,8,16384]{2,1,0:T(8,128)(2,1)}), bf16[32,8,16384]{2,1,0:T(8,128)(2,1)}, u32[]{:S(2)}, u32[]{:S(2)}) async-start(bf16[32,8,16384]{2,1,0:T(8,128)(2,1)} %fusion), calls=%async_computation.1 | async-start | bytes 16777216 | tf_op jit(solution)/shard_map/all_to_all | solution.py:144
  51.6 1.1 bitcast_dynamic-update-slice_fusion.2
  52.7 1.1 bitcast_dynamic-update-slice_fusion.1
  53.8 1.1 bitcast_dynamic-update-slice_fusion
  54.9 2.7 %fusion.23 = (bf16[64,16257]{1,0:T(8,128)(2,1)}, bf16[64,16257]{1,0:T(8,128)(2,1)}) fusion(bf16[64,16384]{1,0:T(8,128)(2,1)S(1)} %bitcast.50), kind=kLoop, calls=%fused_computation.84 | loop fusion | bytes 8323584 | tf_op jit(solution)/shard_map/jit(_roll_static)/slice | solution.py:24
  58.5 0.7 fusion.26
  59.2 0.9 copy-done.2
  60.7 6.0 %fusion.1 = (bf16[64,16384]{1,0:T(8,128)(2,1)}, bf16[64,16384]{1,0:T(8,128)(2,1)}) fusion(bf16[64,16383]{1,0:T(8,128)(2,1)S(1)} %get-tuple-element.84, bf16[64,1]{1,0:T(8,128)(2,1)S(1)} %get-tuple-element.82, bf16[64,127]{1,0:T(8,128)(2,1)S(1)} %get-tuple-element.80, bf16[64,16257]{1,0:T(8,128)(2,1)S(1)} %copy-done.2, s32[16384]{0:T(1024)S(1)} %get-tuple-element.100, ...), kind=kLoop, calls=%fused_computation.9 | loop fusion | flops 22020096 | bytes 12730368 | tf_op jit(solution)/shard_map/jit(_where)/select_n | solution.py:30
  66.7 89.8 %all-to-all-done.1 = bf16[32,8,16384]{2,1,0:T(8,128)(2,1)} async-done(((bf16[32,8,16384]{2,1,0:T(8,128)(2,1)}), bf16[32,8,16384]{2,1,0:T(8,128)(2,1)}, u32[]{:S(2)}, u32[]{:S(2)}) %all-to-all-start.1) | async-done | bytes 8388640 | tf_op jit(solution)/shard_map/all_to_all | solution.py:144
  156.5 4.8 %all-to-all-start.2 = ((bf16[32,2,16384]{2,1,0:T(2,128)(2,1)}), bf16[32,2,16384]{2,1,0:T(2,128)(2,1)}, u32[]{:S(2)}, u32[]{:S(2)}) async-start(bf16[32,2,16384]{2,1,0:T(2,128)(2,1)} %reshape.368), calls=%async_computation.2 | async-start | bytes 4194304 | tf_op jit(solution)/shard_map/all_to_all | solution.py:151
  161.3 6.5 %pad_maximum_fusion = bf16[192,16384]{1,0:T(8,128)(2,1)} fusion(bf16[64,16384]{1,0:T(8,128)(2,1)} %get-tuple-element.89, bf16[64,16384]{1,0:T(8,128)(2,1)S(1)} %bitcast.54, bf16[64,16384]{1,0:T(8,128)(2,1)} %get-tuple-element.88), kind=kLoop, calls=%fused_computation.4 | loop fusion | flops 18874368 | bytes 12582912 | tf_op jit(solution)/shard_map/concatenate | solution.py:163
  167.8 5.9 %fusion.22 = (f32[256]{0:T(256)S(1)}, f32[256,192]{0,1:T(8,128)S(1)}, f32[256,192]{0,1:T(8,128)S(1)}) fusion(f32[256,64]{0,1:T(8,128)S(1)} %tile.17, f32[192]{0:T(256)S(1)} %sub.157, f32[256]{0:T(256)S(1)} %mul.66, bf16[256,16384]{1,0:T(8,128)(2,1)} %bitcast.2.x_ref, bf16[64,16384]{1,0:T(8,128)(2,1)S(1)} %copy-done.1, bf16[64,16384]{1,0:T(8,128)(2,1)S(1)} %bitcast.55, ...), kind=kOutput, calls=%fused_computation.83 | convolution fusion | flops 1629732608 | bytes 15141632 | tf_op jit(solution)/shard_map/dot_general | solution.py:171
  173.8 0.7 fusion.7
  174.6 9.3 %shard_map.93.acc_ref = f32[64,16384]{1,0:T(8,128)} custom-call(bf16[192,256]{1,0:T(8,128)(2,1)} %get-tuple-element.87.w_ref, bf16[256,16384]{1,0:T(8,128)(2,1)} %bitcast.2.x_ref), custom_call_target="tpu_custom_call" | custom-call | flops 1610612736 | bytes 12681216 | tf_op jit(solution)/shard_map/pallas_call | solution.py:63
  183.8 7.4 %all-to-all-done.2 = bf16[32,2,16384]{2,1,0:T(2,128)(2,1)} async-done(((bf16[32,2,16384]{2,1,0:T(2,128)(2,1)}), bf16[32,2,16384]{2,1,0:T(2,128)(2,1)}, u32[]{:S(2)}, u32[]{:S(2)}) %all-to-all-start.2) | async-done | bytes 2097184 | tf_op jit(solution)/shard_map/all_to_all | solution.py:151
  191.2 2.7 %reshape.385 = bf16[64,16384,1]{1,0,2:T(8,128)(2,1)S(1)} reshape(bf16[32,2,16384]{2,1,0:T(2,128)(2,1)} %all-to-all-done.2) | data formatting | bytes 4194304 | tf_op jit(solution)/shard_map/reshape | solution.py:151
  194.0 4.6 %fusion.28 = (f32[64]{0:T(128)S(1)}, f32[64,3,64]{0,2,1:T(8,128)S(1)}) fusion(f32[64,64]{0,1:T(8,128)S(1)} %bitcast.65, f32[64]{0:T(128)S(1)} %div.41, bf16[64,16384,1]{1,0,2:T(8,128)(2,1)S(1)} %reshape.385, bf16[3,64,16384]{2,1,0:T(8,128)(2,1)} %bitcast.56, f32[64]{0:T(128)S(1)} %mul.76), kind=kOutput, calls=%fused_computation.89 | convolution fusion | flops 402714560 | bytes 8454912 | tf_op jit(solution)/shard_map/dot_general | solution.py:171
  198.6 0.8 fusion.15
  199.5 1.3 fusion.20
  201.0 0.7 fusion.21
  201.8 4.1 %reshape.371.x_ref = bf16[64,16384]{1,0:T(8,128)(2,1)} reshape(bf16[32,2,16384]{2,1,0:T(2,128)(2,1)} %all-to-all-done.2) | data formatting | bytes 4194304 | tf_op jit(solution)/shard_map/reshape | solution.py:151
  205.9 8.5 %shard_map.94 = bf16[64,16512]{1,0:T(8,128)(2,1)} custom-call(bf16[192,64]{1,0:T(8,128)(2,1)} %bitcast.67, bf16[64,16384]{1,0:T(8,128)(2,1)} %reshape.371.x_ref, f32[64,16384]{1,0:T(8,128)} %shard_map.93.acc_ref, bf16[64,128]{1,0:T(8,128)(2,1)} %copy-done.4), custom_call_target="tpu_custom_call" | custom-call | flops 402653184 | bytes 8429568 | tf_op jit(solution)/shard_map/pallas_call | solution.py:85
  214.5 2.7 %constant_dynamic-slice_fusion = (bf16[1,16,16512]{2,1,0:T(8,128)(2,1)S(1)}, bf16[16,16512]{1,0:T(8,128)(2,1)S(1)}, bf16[16,16512]{1,0:T(8,128)(2,1)}, bf16[16,16512]{1,0:T(8,128)(2,1)}) fusion(bf16[4,16,16512]{2,1,0:T(8,128)(2,1)} %bitcast.57, s32[]{:T(128)S(6)} %select_n.91, s32[]{:T(128)S(6)} %select_n.106, s32[]{:T(128)S(6)} %select_n.104, s32[]{:T(128)S(6)} %select_n.102), kind=kLoop, calls=%fused_computation.64 | loop fusion | bytes 4227088 | tf_op jit(solution)/shard_map/jit(dynamic_index_in_dim)/dynamic_slice | solution.py:213
  217.2 1.0 collective-permute-start.3
  218.6 2.2 collective-permute-start.5
  222.2 0.8 reshape.388
  223.0 3.9 %all-to-all-start.3 = ((f32[32,1,330]{2,1,0:T(1,128)}), f32[32,1,330]{2,1,0:T(1,128)S(1)}, u32[]{:S(2)}, u32[]{:S(2)}) async-start(f32[32,1,330]{2,1,0:T(1,128)} %reshape.388), calls=%async_computation.3 | async-start | bytes 98304 | tf_op jit(solution)/shard_map/all_to_all | solution.py:202
  226.9 7.4 %all-to-all-done.3 = f32[32,1,330]{2,1,0:T(1,128)S(1)} async-done(((f32[32,1,330]{2,1,0:T(1,128)}), f32[32,1,330]{2,1,0:T(1,128)S(1)}, u32[]{:S(2)}, u32[]{:S(2)}) %all-to-all-start.3) | async-done | bytes 42272 | tf_op jit(solution)/shard_map/all_to_all | solution.py:202
  234.8 0.8 reduce.34
  235.7 0.7 gather_fusion
  236.5 0.7 copy.50
  237.2 0.7 slice_reduce_fusion.1
  237.9 4.1 %collective-permute-done.3 = bf16[16,16512]{1,0:T(8,128)(2,1)S(1)} collective-permute-done((bf16[16,16512]{1,0:T(8,128)(2,1)}, bf16[16,16512]{1,0:T(8,128)(2,1)S(1)}, u32[]{:S(2)}, u32[]{:S(2)}) %collective-permute-start.3) | collective-permute-done | bytes 528416 | tf_op jit(solution)/shard_map/ppermute | solution.py:114
  242.8 2.3 maximum_convert_fusion
  245.8 2.5 slice_reduce_fusion
  248.3 1.1 convert_element_type.125
  (82 shorter events, 10.7 us)
Async XLA Ops:
  1.9 49.7 %collective-permute-start = (bf16[16,16384]{1,0:T(8,128)(2,1)S(1)}, bf16[16,16384]{1,0:T(8,128)(2,1)}, u32[]{:S(2)}, u32[]{:S(2)}) collective-permute-start(bf16[16,16384]{1,0:T(8,128)(2,1)S(1)} %reshape.369), channel_id=1, source_target_pairs={{0,1},{1,2},{2,3},{3,0},{4,5},{5,6},{6,7},{7,4},{8,9},{9,10},{10,1... | collective-permute-start | bytes 1572872 | tf_op jit(solution)/shard_map/ppermute | solution.py:114
  3.9 48.7 %collective-permute-start.1 = (bf16[16,16384]{1,0:T(8,128)(2,1)S(1)}, bf16[16,16384]{1,0:T(8,128)(2,1)}, u32[]{:S(2)}, u32[]{:S(2)}) collective-permute-start(bf16[16,16384]{1,0:T(8,128)(2,1)S(1)} %reshape.369), channel_id=1, source_target_pairs={{0,2},{1,3},{2,0},{3,1},{4,6},{5,7},{6,4},{7,5},{8,10},{9,11},{10,... | collective-permute-start | bytes 1572872 | tf_op jit(solution)/shard_map/ppermute | solution.py:114
  7.5 46.3 %collective-permute-start.2 = (bf16[16,16384]{1,0:T(8,128)(2,1)S(1)}, bf16[16,16384]{1,0:T(8,128)(2,1)}, u32[]{:S(2)}, u32[]{:S(2)}) collective-permute-start(bf16[16,16384]{1,0:T(8,128)(2,1)S(1)} %reshape.369), channel_id=1, source_target_pairs={{0,3},{1,0},{2,1},{3,2},{4,7},{5,4},{6,5},{7,6},{8,11},{9,8},{10,9... | collective-permute-start | bytes 1572872 | tf_op jit(solution)/shard_map/ppermute | solution.py:114
  12.6 30.5 %all-to-all-start = ((f32[32,2,10]{2,1,0:T(2,128)}), f32[32,2,10]{2,1,0:T(2,128)S(1)}, u32[]{:S(2)}, u32[]{:S(2)}) async-start(f32[32,2,10]{2,1,0:T(2,128)} %copy.43), calls=%async_computation | async-start | bytes 65536 | tf_op jit(solution)/shard_map/all_to_all | solution.py:143
  36.7 4.4 %copy-start.5 = (s32[2]{0:T(128)S(1)}, s32[2]{0:T(128)}, u32[]{:S(2)}) copy-start(s32[2]{0:T(128)} %param.17) | copy-start | bytes 28
  43.1 113.4 %all-to-all-start.1 = ((bf16[32,8,16384]{2,1,0:T(8,128)(2,1)}), bf16[32,8,16384]{2,1,0:T(8,128)(2,1)}, u32[]{:S(2)}, u32[]{:S(2)}) async-start(bf16[32,8,16384]{2,1,0:T(8,128)(2,1)} %fusion), calls=%async_computation.1 | async-start | bytes 16777216 | tf_op jit(solution)/shard_map/all_to_all | solution.py:144
  58.5 1.6 copy-start.2
  58.5 2.2 copy-start.3
  156.5 34.7 %all-to-all-start.2 = ((bf16[32,2,16384]{2,1,0:T(2,128)(2,1)}), bf16[32,2,16384]{2,1,0:T(2,128)(2,1)}, u32[]{:S(2)}, u32[]{:S(2)}) async-start(bf16[32,2,16384]{2,1,0:T(2,128)(2,1)} %reshape.368), calls=%async_computation.2 | async-start | bytes 4194304 | tf_op jit(solution)/shard_map/all_to_all | solution.py:151
  161.3 6.5 %copy-start = (bf16[64,16384]{1,0:T(8,128)(2,1)S(1)}, bf16[64,16384]{1,0:T(8,128)(2,1)}, u32[]{:S(2)}) copy-start(bf16[64,16384]{1,0:T(8,128)(2,1)} %get-tuple-element.88) | copy-start | bytes 6291460
  161.3 6.5 %copy-start.1 = (bf16[64,16384]{1,0:T(8,128)(2,1)S(1)}, bf16[64,16384]{1,0:T(8,128)(2,1)}, u32[]{:S(2)}) copy-start(bf16[64,16384]{1,0:T(8,128)(2,1)} %get-tuple-element.89) | copy-start | bytes 6291460
  201.8 4.1 %copy-start.4 = (bf16[64,128]{1,0:T(8,128)(2,1)}, bf16[64,128]{1,0:T(8,128)(2,1)S(1)}, u32[]{:S(2)}) copy-start(bf16[64,128]{1,0:T(8,128)(2,1)S(1)} %scatter.14.tail_ref) | copy-start | bytes 49156
  217.2 24.8 %collective-permute-start.3 = (bf16[16,16512]{1,0:T(8,128)(2,1)}, bf16[16,16512]{1,0:T(8,128)(2,1)S(1)}, u32[]{:S(2)}, u32[]{:S(2)}) collective-permute-start(bf16[16,16512]{1,0:T(8,128)(2,1)} %get-tuple-element.77), channel_id=1, source_target_pairs={{0,1},{1,2},{2,3},{3,0},{4,5},{5,6},{6,7},{7,4},{8,9},{9,10},{10,1... | collective-permute-start | bytes 1585160 | tf_op jit(solution)/shard_map/ppermute | solution.py:114
  218.2 23.8 %collective-permute-start.4 = (bf16[16,16512]{1,0:T(8,128)(2,1)}, bf16[16,16512]{1,0:T(8,128)(2,1)S(1)}, u32[]{:S(2)}, u32[]{:S(2)}) collective-permute-start(bf16[16,16512]{1,0:T(8,128)(2,1)} %get-tuple-element.76), channel_id=1, source_target_pairs={{0,2},{1,3},{2,0},{3,1},{4,6},{5,7},{6,4},{7,5},{8,10},{9,11},{10,... | collective-permute-start | bytes 1585160 | tf_op jit(solution)/shard_map/ppermute | solution.py:114
  218.6 23.9 %collective-permute-start.5 = (bf16[16,16512]{1,0:T(8,128)(2,1)S(1)}, bf16[16,16512]{1,0:T(8,128)(2,1)S(1)}, u32[]{:S(2)}, u32[]{:S(2)}) collective-permute-start(bf16[16,16512]{1,0:T(8,128)(2,1)S(1)} %get-tuple-element.75), channel_id=1, source_target_pairs={{0,3},{1,0},{2,1},{3,2},{4,7},{5,4},{6,5},{7,6},{8,11},{9,8},{10,9... | collective-permute-start | bytes 1585160 | tf_op jit(solution)/shard_map/ppermute | solution.py:114
  223.0 11.3 %all-to-all-start.3 = ((f32[32,1,330]{2,1,0:T(1,128)}), f32[32,1,330]{2,1,0:T(1,128)S(1)}, u32[]{:S(2)}, u32[]{:S(2)}) async-start(f32[32,1,330]{2,1,0:T(1,128)} %reshape.388), calls=%async_computation.3 | async-start | bytes 98304 | tf_op jit(solution)/shard_map/all_to_all | solution.py:202

commit v5 on v4

--- a/solution.py
+++ b/solution.py
@@ -46,12 +46,23 @@
         out_ref[:, j * IMG:(j + 1) * IMG] = rolled_sum(y, rows, offsets, j)
 
 
-def last_sums_kernel(offsets, rows, chunk, w_ref, x_ref, acc_ref, tail_ref, out_ref):
+def last_sums_kernel(offsets, rows, chunk, w_ref, x_ref, acc_ref, tail_ref, out_ref, moved_ref):
     k = pl.program_id(0)
-    y = jnp.dot(w_ref[...], x_ref[...], preferred_element_type=jnp.float32)
-    for j in range(chunk // IMG):
-        total = acc_ref[:, j * IMG:(j + 1) * IMG] + rolled_sum(y, rows, offsets, j)
-        out_ref[:, pl.ds(k * chunk + j * IMG, IMG)] = total.astype(out_ref.dtype)
+    x = x_ref[...].astype(jnp.float32)
+    total = acc_ref[...]
+    for u, t in enumerate(offsets):
+        if t % IMG:
+            for j in range(chunk // IMG):
+                piece = x[:, j * IMG:(j + 1) * IMG]
+                moved_ref[:, j * IMG:(j + 1) * IMG] = pltpu.roll(piece, shift=t % IMG, axis=1).astype(
+                    moved_ref.dtype
+                )
+            shifted_x = moved_ref[...]
+        else:
+            shifted_x = x_ref[...]
+        w = w_ref[u * rows:(u + 1) * rows, :]
+        total = total + jnp.dot(w, shifted_x, preferred_element_type=jnp.float32)
+    out_ref[:, pl.ds(k * chunk, chunk)] = total.astype(out_ref.dtype)
     pixels = out_ref.shape[1] - tail_ref.shape[1]
     out_ref[:, pixels:] = tail_ref[...]
 
@@ -93,6 +104,7 @@
         ],
         out_specs=pl.BlockSpec((rows, width), lambda k: (0, 0)),
         out_shape=jax.ShapeDtypeStruct((rows, width), jnp.bfloat16),
+        scratch_shapes=[pltpu.VMEM((x.shape[0], chunk), x.dtype)],
         cost_estimate=pl.CostEstimate(
             flops=2 * w.shape[0] * pixels * x.shape[0],
             transcendentals=0,
@@ -142,14 +154,6 @@
     )
     got_meta = lax.all_to_all(meta, "dom", 0, 0, tiled=True)
     got_a = lax.all_to_all(send_a, "dom", 0, 0, tiled=True).reshape(count_dom * rows_a, pixels)
-    if rows_b:
-        pick_b = pick(jnp.where(in_a, -1, owners * rows_b + slot_rank - rows_a), count_dom * rows_b)
-        send_a, pick_b = lax.optimization_barrier((send_a, pick_b))
-        send_b = jnp.dot(pick_b.astype(particles.dtype), particles, preferred_element_type=f32)
-        send_b = send_b.astype(particles.dtype).reshape(count_dom, rows_b, pixels)
-        got_a, send_b = lax.optimization_barrier((got_a, send_b))
-        got_b = lax.all_to_all(send_b, "dom", 0, 0, tiled=True).reshape(count_dom * rows_b, pixels)
-
     own_proj = projections.reshape(-1, pixels)
     ref_here = lax.axis_index("ref")
     blocks = jnp.zeros((count_ref,) + own_proj.shape, own_proj.dtype)
@@ -158,6 +162,14 @@
         moved = ahead(own_proj, "ref", k)
         blocks = lax.dynamic_update_index_in_dim(blocks, moved, (ref_here - k) % count_ref, 0)
     all_proj = blocks.reshape(-1, pixels)
+    if rows_b:
+        pick_b = pick(jnp.where(in_a, -1, owners * rows_b + slot_rank - rows_a), count_dom * rows_b)
+        all_proj, pick_b = lax.optimization_barrier((all_proj, pick_b))
+        send_b = jnp.dot(pick_b.astype(particles.dtype), particles, preferred_element_type=f32)
+        send_b = send_b.astype(particles.dtype).reshape(count_dom, rows_b, pixels)
+        got_a, send_b = lax.optimization_barrier((got_a, send_b))
+        got_b = lax.all_to_all(send_b, "dom", 0, 0, tiled=True).reshape(count_dom * rows_b, pixels)
+
     rows = all_proj.shape[0]
     offsets = [u - SHIFTS // 2 for u in range(SHIFTS)]
     shifted = jnp.concatenate([translate(all_proj, -t) for t in offsets], axis=0)

time: 251 us -> 240 us (0.956)
  waiting for transfers between devices: 109 us -> 98.7 us
    all_to_all x1, waiting for transfers between devices: 89.8 us -> 79.2 us  [shards(): lax.all_to_all(send_a, 'dom', 0, 0, tiled=True)]
  transfers between devices with their start and end apart: 10 -> 10, of which waited for: 5 -> 5; matrix products, arithmetic and copies ran while one was open for 24% -> 25% of each run, Pallas kernels for 4% -> 4%
where the time goes in v5:
time: 240 us; the launch traced here: 239 us
  waiting for transfers between devices  98.7 us (41%)
  starting transfers between devices  34 us (14%)
  local copies, waits for them, and re-layouts  33.6 us (14%)
  other arithmetic  28.2 us (12%)
  matrix products  25.7 us (11%)
  Pallas kernels  17.6 us (7%)
    all_to_all x1, waiting for transfers between devices, shards(): lax.all_to_all(send_a, 'dom', 0, 0, tiled=True)  79.2 us
    dot_general x2, matrix products, part(): lax.dot_general(images, shifted, (((1,), (1,)), ((), ())), preferred_elem...  10.5 us
    ppermute x6, starting transfers between devices, ahead(): lax.ppermute(block, axis, [(i, (i + distance) % size) for i in range(size)])  10.4 us
    pallas_call x1, Pallas kernels, first_sums(): pl.pallas_call(functools.partial(first_sums_kernel, tuple(offsets), rows)...  9.27 us
    dot_general x1, matrix products, shards(): jnp.dot(pick_a.astype(particles.dtype), particles, preferred_element_type...  8.94 us
    pallas_call x1, Pallas kernels, last_sums(): pl.pallas_call(functools.partial(last_sums_kernel, tuple(offsets), rows,...  8.38 us
    all_to_all x1, starting transfers between devices, shards(): lax.all_to_all(send_a, 'dom', 0, 0, tiled=True)  7.68 us
    all_to_all x1, waiting for transfers between devices, shards(): lax.all_to_all(back, 'dom', 0, 0, tiled=True)  7.43 us
  transfers between devices with their start and end apart: 10, of which 5 were waited for; matrix products, arithmetic and copies ran while one was open for 25% of the time, Pallas kernels for 4%

profile of v5, /device:TPU:0, one launch (start us, length us, event | category | flops | bytes accessed | tf_op | source)
XLA Modules:
  0.0 239.0 jit_solution(2032900649459559546)
XLA Ops:
  0.6 1.2 reshape.362
  1.9 2.1 collective-permute-start
  3.9 3.6 %collective-permute-start.1 = (bf16[16,16384]{1,0:T(8,128)(2,1)S(1)}, bf16[16,16384]{1,0:T(8,128)(2,1)}, u32[]{:S(2)}, u32[]{:S(2)}) collective-permute-start(bf16[16,16384]{1,0:T(8,128)(2,1)S(1)} %reshape.362), channel_id=1, source_target_pairs={{0,2},{1,3},{2,0},{3,1},{4,6},{5,7},{6,4},{7,5},{8,10},{9,11},{10,... | collective-permute-start | bytes 1572872 | tf_op jit(solution)/shard_map/ppermute | solution.py:126
  7.5 1.0 collective-permute-start.2
  8.5 0.9 convert_reduce_fusion
  9.5 0.7 compare_select_fusion
  10.2 0.7 convert_add_fusion.2
  12.6 7.3 %all-to-all-start = ((f32[32,2,10]{2,1,0:T(2,128)}), f32[32,2,10]{2,1,0:T(2,128)S(1)}, u32[]{:S(2)}, u32[]{:S(2)}) async-start(f32[32,2,10]{2,1,0:T(2,128)} %copy.43), calls=%async_computation | async-start | bytes 65536 | tf_op jit(solution)/shard_map/all_to_all | solution.py:155
  19.9 1.2 broadcast_in_dim.73
  21.3 8.9 %fusion = bf16[32,8,16384]{2,1,0:T(8,128)(2,1)} fusion(bf16[256,16384]{1,0:T(8,128)(2,1)} %param.12, s32[256]{0:T(256)S(1)} %get-tuple-element.97), kind=kOutput, calls=%fused_computation.2 | convolution fusion | flops 2151743488 | bytes 16778240 | tf_op jit(solution)/shard_map/dot_general | solution.py:147
  32.8 7.7 %all-to-all-start.1 = ((bf16[32,8,16384]{2,1,0:T(8,128)(2,1)}), bf16[32,8,16384]{2,1,0:T(8,128)(2,1)}, u32[]{:S(2)}, u32[]{:S(2)}) async-start(bf16[32,8,16384]{2,1,0:T(8,128)(2,1)} %fusion), calls=%async_computation.1 | async-start | bytes 16777216 | tf_op jit(solution)/shard_map/all_to_all | solution.py:156
  41.3 1.1 bitcast_dynamic-update-slice_fusion.2
  42.4 1.1 bitcast_dynamic-update-slice_fusion.1
  43.5 1.1 bitcast_dynamic-update-slice_fusion
  44.6 2.7 %fusion.23 = (bf16[64,16257]{1,0:T(8,128)(2,1)}, bf16[64,16257]{1,0:T(8,128)(2,1)}) fusion(bf16[64,16384]{1,0:T(8,128)(2,1)S(1)} %bitcast.50), kind=kLoop, calls=%fused_computation.84 | loop fusion | bytes 8323584 | tf_op jit(solution)/shard_map/jit(_roll_static)/slice | solution.py:24
  47.3 6.3 %convolution_convert_fusion.1 = bf16[64,16384]{1,0:T(8,128)(2,1)} fusion(pred[64,256]{1,0:T(32,128)(4,1)S(1)} %iota_compare_fusion.4, bf16[256,16384]{1,0:T(8,128)(2,1)} %param.12), kind=kOutput, calls=%fused_computation.3 | convolution fusion | flops 537919488 | bytes 10502144 | tf_op jit(solution)/shard_map/dot_general | solution.py:168
  54.1 4.4 %reshape.364 = bf16[32,2,16384]{2,1,0:T(2,128)(2,1)} reshape(bf16[64,16384]{1,0:T(8,128)(2,1)} %convolution_convert_fusion.1) | data formatting | bytes 4194304 | tf_op jit(solution)/shard_map/reshape | solution.py:169
  58.8 0.7 fusion.26
  59.5 0.9 copy-done.2
  61.0 6.0 %fusion.1 = (bf16[64,16384]{1,0:T(8,128)(2,1)}, bf16[64,16384]{1,0:T(8,128)(2,1)}) fusion(bf16[64,16383]{1,0:T(8,128)(2,1)S(1)} %get-tuple-element.86, bf16[64,1]{1,0:T(8,128)(2,1)S(1)} %get-tuple-element.84, bf16[64,127]{1,0:T(8,128)(2,1)S(1)} %get-tuple-element.82, bf16[64,16257]{1,0:T(8,128)(2,1)S(1)} %copy-done.2, s32[16384]{0:T(1024)S(1)} %get-tuple-element.102, ...), kind=kLoop, calls=%fused_computation.9 | loop fusion | flops 22020096 | bytes 12730368 | tf_op jit(solution)/shard_map/jit(_where)/select_n | solution.py:30
  67.0 79.2 %all-to-all-done.1 = bf16[32,8,16384]{2,1,0:T(8,128)(2,1)} async-done(((bf16[32,8,16384]{2,1,0:T(8,128)(2,1)}), bf16[32,8,16384]{2,1,0:T(8,128)(2,1)}, u32[]{:S(2)}, u32[]{:S(2)}) %all-to-all-start.1) | async-done | bytes 8388640 | tf_op jit(solution)/shard_map/all_to_all | solution.py:156
  146.2 4.8 %all-to-all-start.2 = ((bf16[32,2,16384]{2,1,0:T(2,128)(2,1)}), bf16[32,2,16384]{2,1,0:T(2,128)(2,1)}, u32[]{:S(2)}, u32[]{:S(2)}) async-start(bf16[32,2,16384]{2,1,0:T(2,128)(2,1)} %reshape.364), calls=%async_computation.2 | async-start | bytes 4194304 | tf_op jit(solution)/shard_map/all_to_all | solution.py:171
  151.0 6.5 %pad_maximum_fusion = bf16[192,16384]{1,0:T(8,128)(2,1)} fusion(bf16[64,16384]{1,0:T(8,128)(2,1)} %get-tuple-element.91, bf16[64,16384]{1,0:T(8,128)(2,1)S(1)} %bitcast.55, bf16[64,16384]{1,0:T(8,128)(2,1)} %get-tuple-element.90), kind=kLoop, calls=%fused_computation.4 | loop fusion | flops 18874368 | bytes 12582912 | tf_op jit(solution)/shard_map/concatenate | solution.py:175
  157.5 5.9 %fusion.22 = (f32[256]{0:T(256)S(1)}, f32[256,192]{0,1:T(8,128)S(1)}, f32[256,192]{0,1:T(8,128)S(1)}) fusion(f32[256,64]{0,1:T(8,128)S(1)} %tile.17, f32[192]{0:T(256)S(1)} %sub.157, f32[256]{0:T(256)S(1)} %mul.66, bf16[256,16384]{1,0:T(8,128)(2,1)} %bitcast.2.x_ref, bf16[64,16384]{1,0:T(8,128)(2,1)S(1)} %copy-done.1, bf16[64,16384]{1,0:T(8,128)(2,1)S(1)} %bitcast.56, ...), kind=kOutput, calls=%fused_computation.83 | convolution fusion | flops 1629732608 | bytes 15141632 | tf_op jit(solution)/shard_map/dot_general | solution.py:183
  163.5 0.7 fusion.7
  164.3 9.3 %shard_map.93.acc_ref = f32[64,16384]{1,0:T(8,128)} custom-call(bf16[192,256]{1,0:T(8,128)(2,1)} %get-tuple-element.89.w_ref, bf16[256,16384]{1,0:T(8,128)(2,1)} %bitcast.2.x_ref), custom_call_target="tpu_custom_call" | custom-call | flops 1610612736 | bytes 12681216 | tf_op jit(solution)/shard_map/pallas_call | solution.py:74
  173.6 7.4 %all-to-all-done.2 = bf16[32,2,16384]{2,1,0:T(2,128)(2,1)} async-done(((bf16[32,2,16384]{2,1,0:T(2,128)(2,1)}), bf16[32,2,16384]{2,1,0:T(2,128)(2,1)}, u32[]{:S(2)}, u32[]{:S(2)}) %all-to-all-start.2) | async-done | bytes 2097184 | tf_op jit(solution)/shard_map/all_to_all | solution.py:171
  180.9 2.7 %reshape.379 = bf16[64,16384,1]{1,0,2:T(8,128)(2,1)S(1)} reshape(bf16[32,2,16384]{2,1,0:T(2,128)(2,1)} %all-to-all-done.2) | data formatting | bytes 4194304 | tf_op jit(solution)/shard_map/reshape | solution.py:171
  183.7 4.6 %fusion.28 = (f32[64]{0:T(128)S(1)}, f32[64,3,64]{0,2,1:T(8,128)S(1)}) fusion(f32[64,64]{0,1:T(8,128)S(1)} %bitcast.66, f32[64]{0:T(128)S(1)} %broadcast_multiply_fusion, bf16[64,16384,1]{1,0,2:T(8,128)(2,1)S(1)} %reshape.379, bf16[3,64,16384]{2,1,0:T(8,128)(2,1)} %bitcast.57, f32[64]{0:T(128)S(1)} %mul.76), kind=kOutput, calls=%fused_computation.89 | convolution fusion | flops 402714560 | bytes 8454912 | tf_op jit(solution)/shard_map/dot_general | solution.py:183
  188.3 0.8 fusion.15
  189.2 1.3 fusion.20
  190.7 0.7 fusion.21
  191.5 4.1 %reshape.365.x_ref = bf16[64,16384]{1,0:T(8,128)(2,1)} reshape(bf16[32,2,16384]{2,1,0:T(2,128)(2,1)} %all-to-all-done.2) | data formatting | bytes 4194304 | tf_op jit(solution)/shard_map/reshape | solution.py:171
  195.7 8.4 %shard_map.94 = bf16[64,16512]{1,0:T(8,128)(2,1)} custom-call(bf16[192,64]{1,0:T(8,128)(2,1)} %bitcast.68, bf16[64,16384]{1,0:T(8,128)(2,1)} %reshape.365.x_ref, f32[64,16384]{1,0:T(8,128)} %shard_map.93.acc_ref, bf16[64,128]{1,0:T(8,128)(2,1)} %copy-done.4), custom_call_target="tpu_custom_call" | custom-call | flops 402653184 | bytes 8429568 | tf_op jit(solution)/shard_map/pallas_call | solution.py:96
  204.0 2.7 %constant_dynamic-slice_fusion = (bf16[1,16,16512]{2,1,0:T(8,128)(2,1)S(1)}, bf16[16,16512]{1,0:T(8,128)(2,1)S(1)}, bf16[16,16512]{1,0:T(8,128)(2,1)}, bf16[16,16512]{1,0:T(8,128)(2,1)}) fusion(bf16[4,16,16512]{2,1,0:T(8,128)(2,1)} %bitcast.58, s32[]{:T(128)S(6)} %select_n.89, s32[]{:T(128)S(6)} %select_n.106, s32[]{:T(128)S(6)} %select_n.104, s32[]{:T(128)S(6)} %select_n.102), kind=kLoop, calls=%fused_computation.64 | loop fusion | bytes 4227088 | tf_op jit(solution)/shard_map/jit(dynamic_index_in_dim)/dynamic_slice | solution.py:225
  206.8 1.0 collective-permute-start.3
  208.2 2.2 collective-permute-start.5
  211.8 0.8 reshape.382
  212.6 3.9 %all-to-all-start.3 = ((f32[32,1,330]{2,1,0:T(1,128)}), f32[32,1,330]{2,1,0:T(1,128)S(1)}, u32[]{:S(2)}, u32[]{:S(2)}) async-start(f32[32,1,330]{2,1,0:T(1,128)} %reshape.382), calls=%async_computation.3 | async-start | bytes 98304 | tf_op jit(solution)/shard_map/all_to_all | solution.py:214
  216.5 7.4 %all-to-all-done.3 = f32[32,1,330]{2,1,0:T(1,128)S(1)} async-done(((f32[32,1,330]{2,1,0:T(1,128)}), f32[32,1,330]{2,1,0:T(1,128)S(1)}, u32[]{:S(2)}, u32[]{:S(2)}) %all-to-all-start.3) | async-done | bytes 42272 | tf_op jit(solution)/shard_map/all_to_all | solution.py:214
  224.4 0.8 reduce.33
  225.3 0.7 gather_fusion
  226.1 0.7 copy.50
  226.7 0.7 slice_reduce_fusion.1
  227.5 4.0 %collective-permute-done.3 = bf16[16,16512]{1,0:T(8,128)(2,1)S(1)} collective-permute-done((bf16[16,16512]{1,0:T(8,128)(2,1)}, bf16[16,16512]{1,0:T(8,128)(2,1)S(1)}, u32[]{:S(2)}, u32[]{:S(2)}) %collective-permute-start.3) | collective-permute-done | bytes 528416 | tf_op jit(solution)/shard_map/ppermute | solution.py:126
  232.3 2.3 maximum_convert_fusion
  235.4 2.5 %slice_reduce_fusion = bf16[16,16384]{1,0:T(8,128)(2,1)S(1)} fusion(f32[4,16,16512]{2,1,0:T(8,128)} %maximum_convert_fusion), kind=kLoop, calls=%fused_computation.7 | loop fusion | flops 786432 | bytes 4718592 | tf_op jit(solution)/shard_map/reduce_sum | solution.py:230
  237.9 1.1 convert_element_type.124
  (81 shorter events, 11.0 us)
Async XLA Ops:
  1.9 39.4 %collective-permute-start = (bf16[16,16384]{1,0:T(8,128)(2,1)S(1)}, bf16[16,16384]{1,0:T(8,128)(2,1)}, u32[]{:S(2)}, u32[]{:S(2)}) collective-permute-start(bf16[16,16384]{1,0:T(8,128)(2,1)S(1)} %reshape.362), channel_id=1, source_target_pairs={{0,1},{1,2},{2,3},{3,0},{4,5},{5,6},{6,7},{7,4},{8,9},{9,10},{10,1... | collective-permute-start | bytes 1572872 | tf_op jit(solution)/shard_map/ppermute | solution.py:126
  3.9 38.5 %collective-permute-start.1 = (bf16[16,16384]{1,0:T(8,128)(2,1)S(1)}, bf16[16,16384]{1,0:T(8,128)(2,1)}, u32[]{:S(2)}, u32[]{:S(2)}) collective-permute-start(bf16[16,16384]{1,0:T(8,128)(2,1)S(1)} %reshape.362), channel_id=1, source_target_pairs={{0,2},{1,3},{2,0},{3,1},{4,6},{5,7},{6,4},{7,5},{8,10},{9,11},{10,... | collective-permute-start | bytes 1572872 | tf_op jit(solution)/shard_map/ppermute | solution.py:126
  7.5 36.0 %collective-permute-start.2 = (bf16[16,16384]{1,0:T(8,128)(2,1)S(1)}, bf16[16,16384]{1,0:T(8,128)(2,1)}, u32[]{:S(2)}, u32[]{:S(2)}) collective-permute-start(bf16[16,16384]{1,0:T(8,128)(2,1)S(1)} %reshape.362), channel_id=1, source_target_pairs={{0,3},{1,0},{2,1},{3,2},{4,7},{5,4},{6,5},{7,6},{8,11},{9,8},{10,9... | collective-permute-start | bytes 1572872 | tf_op jit(solution)/shard_map/ppermute | solution.py:126
  12.6 20.2 %all-to-all-start = ((f32[32,2,10]{2,1,0:T(2,128)}), f32[32,2,10]{2,1,0:T(2,128)S(1)}, u32[]{:S(2)}, u32[]{:S(2)}) async-start(f32[32,2,10]{2,1,0:T(2,128)} %copy.43), calls=%async_computation | async-start | bytes 65536 | tf_op jit(solution)/shard_map/all_to_all | solution.py:155
  30.2 0.7 copy-start.5
  32.8 113.4 %all-to-all-start.1 = ((bf16[32,8,16384]{2,1,0:T(8,128)(2,1)}), bf16[32,8,16384]{2,1,0:T(8,128)(2,1)}, u32[]{:S(2)}, u32[]{:S(2)}) async-start(bf16[32,8,16384]{2,1,0:T(8,128)(2,1)} %fusion), calls=%async_computation.1 | async-start | bytes 16777216 | tf_op jit(solution)/shard_map/all_to_all | solution.py:156
  58.7 1.6 copy-start.2
  58.8 2.2 copy-start.3
  146.2 34.7 %all-to-all-start.2 = ((bf16[32,2,16384]{2,1,0:T(2,128)(2,1)}), bf16[32,2,16384]{2,1,0:T(2,128)(2,1)}, u32[]{:S(2)}, u32[]{:S(2)}) async-start(bf16[32,2,16384]{2,1,0:T(2,128)(2,1)} %reshape.364), calls=%async_computation.2 | async-start | bytes 4194304 | tf_op jit(solution)/shard_map/all_to_all | solution.py:171
  151.0 6.5 %copy-start = (bf16[64,16384]{1,0:T(8,128)(2,1)S(1)}, bf16[64,16384]{1,0:T(8,128)(2,1)}, u32[]{:S(2)}) copy-start(bf16[64,16384]{1,0:T(8,128)(2,1)} %get-tuple-element.90) | copy-start | bytes 6291460
  151.0 6.5 %copy-start.1 = (bf16[64,16384]{1,0:T(8,128)(2,1)S(1)}, bf16[64,16384]{1,0:T(8,128)(2,1)}, u32[]{:S(2)}) copy-start(bf16[64,16384]{1,0:T(8,128)(2,1)} %get-tuple-element.91) | copy-start | bytes 6291460
  191.5 4.1 %copy-start.4 = (bf16[64,128]{1,0:T(8,128)(2,1)}, bf16[64,128]{1,0:T(8,128)(2,1)S(1)}, u32[]{:S(2)}) copy-start(bf16[64,128]{1,0:T(8,128)(2,1)S(1)} %scatter.14.tail_ref) | copy-start | bytes 49156
  206.8 24.8 %collective-permute-start.3 = (bf16[16,16512]{1,0:T(8,128)(2,1)}, bf16[16,16512]{1,0:T(8,128)(2,1)S(1)}, u32[]{:S(2)}, u32[]{:S(2)}) collective-permute-start(bf16[16,16512]{1,0:T(8,128)(2,1)} %get-tuple-element.79), channel_id=1, source_target_pairs={{0,1},{1,2},{2,3},{3,0},{4,5},{5,6},{6,7},{7,4},{8,9},{9,10},{10,1... | collective-permute-start | bytes 1585160 | tf_op jit(solution)/shard_map/ppermute | solution.py:126
  207.8 23.8 %collective-permute-start.4 = (bf16[16,16512]{1,0:T(8,128)(2,1)}, bf16[16,16512]{1,0:T(8,128)(2,1)S(1)}, u32[]{:S(2)}, u32[]{:S(2)}) collective-permute-start(bf16[16,16512]{1,0:T(8,128)(2,1)} %get-tuple-element.78), channel_id=1, source_target_pairs={{0,2},{1,3},{2,0},{3,1},{4,6},{5,7},{6,4},{7,5},{8,10},{9,11},{10,... | collective-permute-start | bytes 1585160 | tf_op jit(solution)/shard_map/ppermute | solution.py:126
  208.2 23.9 %collective-permute-start.5 = (bf16[16,16512]{1,0:T(8,128)(2,1)S(1)}, bf16[16,16512]{1,0:T(8,128)(2,1)S(1)}, u32[]{:S(2)}, u32[]{:S(2)}) collective-permute-start(bf16[16,16512]{1,0:T(8,128)(2,1)S(1)} %get-tuple-element.77), channel_id=1, source_target_pairs={{0,3},{1,0},{2,1},{3,2},{4,7},{5,4},{6,5},{7,6},{8,11},{9,8},{10,9... | collective-permute-start | bytes 1585160 | tf_op jit(solution)/shard_map/ppermute | solution.py:126
  212.6 11.3 %all-to-all-start.3 = ((f32[32,1,330]{2,1,0:T(1,128)}), f32[32,1,330]{2,1,0:T(1,128)S(1)}, u32[]{:S(2)}, u32[]{:S(2)}) async-start(f32[32,1,330]{2,1,0:T(1,128)} %reshape.382), calls=%async_computation.3 | async-start | bytes 98304 | tf_op jit(solution)/shard_map/all_to_all | solution.py:214

commit v6 on v5

--- a/solution.py
+++ b/solution.py
@@ -67,9 +67,8 @@
     out_ref[:, pixels:] = tail_ref[...]
 
 
-def first_sums(w, x, offsets):
+def first_sums(w, x, offsets, pixels):
     rows = w.shape[0] // len(offsets)
-    pixels = x.shape[1]
     chunk = min(CHUNK, pixels)
     return pl.pallas_call(
         functools.partial(first_sums_kernel, tuple(offsets), rows),
@@ -83,14 +82,13 @@
         cost_estimate=pl.CostEstimate(
             flops=2 * w.shape[0] * pixels * x.shape[0],
             transcendentals=0,
-            bytes_accessed=2 * (x.size + w.size) + 4 * rows * pixels,
+            bytes_accessed=2 * (x.shape[0] * pixels + w.size) + 4 * rows * pixels,
         ),
     )(w, x)
 
 
-def last_sums(w, x, acc, tail, offsets):
+def last_sums(w, x, acc, tail, offsets, pixels):
     rows = w.shape[0] // len(offsets)
-    pixels = x.shape[1]
     chunk = min(CHUNK, pixels)
     width = pixels + tail.shape[1]
     return pl.pallas_call(
@@ -108,7 +106,7 @@
         cost_estimate=pl.CostEstimate(
             flops=2 * w.shape[0] * pixels * x.shape[0],
             transcendentals=0,
-            bytes_accessed=2 * (x.size + w.size + rows * width) + 4 * rows * pixels,
+            bytes_accessed=2 * (x.shape[0] * pixels + w.size + rows * width) + 4 * rows * pixels,
         ),
     )(w, x, acc, tail)
 
@@ -143,17 +141,18 @@
     def pick(slot_of, count):
         return slot_of[None, :] == jnp.arange(count, dtype=jnp.int32)[:, None]
 
+    code = prior_pose + 1
+    lane = jnp.arange(IMG, dtype=jnp.int32)[None, :]
+    extra = jnp.where(lane == 0, noise_prec.astype(f32)[:, None], 0.0)
+    extra = jnp.where(lane == 1, (code // 64).astype(f32)[:, None], extra)
+    extra = jnp.where(lane == 2, (code % 64).astype(f32)[:, None], extra)
+    carried = jnp.concatenate([particles, extra.astype(particles.dtype)], axis=1)
+    width = pixels + IMG
+
     pick_a = pick(jnp.where(in_a, owners * rows_a + slot_rank, -1), count_dom * rows_a)
-    send_a = jnp.dot(pick_a.astype(particles.dtype), particles, preferred_element_type=f32)
-    send_a = send_a.astype(particles.dtype).reshape(count_dom, rows_a, pixels)
-    pick_all = pick(owners * capacity + slot_rank, count_dom * capacity)
-    send_prec = jnp.sum(jnp.where(pick_all, noise_prec.astype(f32)[None, :], 0.0), axis=1)
-    send_prior = jnp.sum(jnp.where(pick_all, prior_pose.astype(f32)[None, :] + 1.0, 0.0), axis=1) - 1.0
-    meta = jnp.stack(
-        [send_prec.reshape(count_dom, capacity), send_prior.reshape(count_dom, capacity)], axis=1
-    )
-    got_meta = lax.all_to_all(meta, "dom", 0, 0, tiled=True)
-    got_a = lax.all_to_all(send_a, "dom", 0, 0, tiled=True).reshape(count_dom * rows_a, pixels)
+    send_a = jnp.dot(pick_a.astype(particles.dtype), carried, preferred_element_type=f32)
+    send_a = send_a.astype(particles.dtype).reshape(count_dom, rows_a, width)
+    got_a = lax.all_to_all(send_a, "dom", 0, 0, tiled=True).reshape(count_dom * rows_a, width)
     own_proj = projections.reshape(-1, pixels)
     ref_here = lax.axis_index("ref")
     blocks = jnp.zeros((count_ref,) + own_proj.shape, own_proj.dtype)
@@ -165,10 +164,10 @@
     if rows_b:
         pick_b = pick(jnp.where(in_a, -1, owners * rows_b + slot_rank - rows_a), count_dom * rows_b)
         all_proj, pick_b = lax.optimization_barrier((all_proj, pick_b))
-        send_b = jnp.dot(pick_b.astype(particles.dtype), particles, preferred_element_type=f32)
-        send_b = send_b.astype(particles.dtype).reshape(count_dom, rows_b, pixels)
+        send_b = jnp.dot(pick_b.astype(particles.dtype), carried, preferred_element_type=f32)
+        send_b = send_b.astype(particles.dtype).reshape(count_dom, rows_b, width)
         got_a, send_b = lax.optimization_barrier((got_a, send_b))
-        got_b = lax.all_to_all(send_b, "dom", 0, 0, tiled=True).reshape(count_dom * rows_b, pixels)
+        got_b = lax.all_to_all(send_b, "dom", 0, 0, tiled=True).reshape(count_dom * rows_b, width)
 
     rows = all_proj.shape[0]
     offsets = [u - SHIFTS // 2 for u in range(SHIFTS)]
@@ -177,11 +176,13 @@
     per_class = projections.shape[1]
     pose_f = pose_index.astype(f32)
 
-    def part(images, precision, prior_ids):
-        n = images.shape[0]
+    def part(received):
+        n = received.shape[0]
+        precision = received[:, pixels].astype(f32)
+        prior_ids = received[:, pixels + 1].astype(f32) * 64.0 + received[:, pixels + 2].astype(f32) - 1.0
         live = (prior_ids >= 0).astype(f32)
         corr = lax.dot_general(
-            images, shifted, (((1,), (1,)), ((), ())), preferred_element_type=f32
+            received[:, :pixels], shifted, (((1,), (1,)), ((), ())), preferred_element_type=f32
         ).reshape(n, SHIFTS, rows)
         log_prior = -jnp.abs(pose_f[None, :] - prior_ids[:, None]) / PRIOR_WIDTH
         prior_rows = jnp.tile(log_prior, (1, rows // per_class))
@@ -196,18 +197,12 @@
         post = jnp.concatenate([class_post, loglike[:, None]], axis=1)
         return low, totals, post
 
-    meta_prec = got_meta[:, 0, :]
-    meta_prior = got_meta[:, 1, :]
-    low_a, tot_a, post_a = part(
-        got_a, meta_prec[:, :rows_a].reshape(-1), meta_prior[:, :rows_a].reshape(-1)
-    )
-    sums_a = first_sums(low_a, got_a, offsets)
+    low_a, tot_a, post_a = part(got_a)
+    sums_a = first_sums(low_a, got_a, offsets, pixels)
     post_width = post_a.shape[1]
     back = [post_a.reshape(count_dom, rows_a, post_width)]
     if rows_b:
-        low_b, tot_b, post_b = part(
-            got_b, meta_prec[:, rows_a:].reshape(-1), meta_prior[:, rows_a:].reshape(-1)
-        )
+        low_b, tot_b, post_b = part(got_b)
         tot_a = tot_a + tot_b
         back.append(post_b.reshape(count_dom, rows_b, post_width))
     back = jnp.concatenate(back, axis=1)
@@ -215,12 +210,12 @@
 
     if not rows_b:
         low_b = jnp.zeros((SHIFTS * rows, 8), jnp.bfloat16)
-        got_b = jnp.zeros((8, pixels), particles.dtype)
+        got_b = jnp.zeros((8, width), particles.dtype)
     pieces = split_bf16(tot_a)
     tail = jnp.zeros((rows, IMG), jnp.bfloat16)
     for q, piece in enumerate(pieces):
         tail = tail.at[:, q].set(piece)
-    image_sums = last_sums(low_b, got_b, sums_a, tail, offsets)
+    image_sums = last_sums(low_b, got_b, sums_a, tail, offsets, pixels)
     partial = image_sums.reshape(count_ref, rows // count_ref, pixels + IMG)
     pieces = [lax.dynamic_index_in_dim(partial, ref_here, 0, keepdims=False)]
     for k in range(1, count_ref):

time: 240 us -> 228 us (0.950)
  starting transfers between devices: 34 us -> 26.7 us
  local copies, waits for them, and re-layouts: 33.6 us -> 29.1 us
  other arithmetic: 28.2 us -> 25.2 us
    all_to_all x1 -> x0, starting transfers between devices: 7.32 us -> none  [shards(): got_meta = lax.all_to_all(meta, 'dom', 0, 0, tiled=True)]
    concatenate x1 -> x0, other arithmetic: 6.5 us -> none  [shards(): jnp.concatenate([translate(all_proj, -t) for t in offsets], axis=0)]
    all_to_all x1, waiting for transfers between devices: 79.2 us -> 84.7 us  [shards(): lax.all_to_all(send_a, 'dom', 0, 0, tiled=True)]
    all_to_all x1, waiting for transfers between devices: 7.37 us -> 3.61 us  [shards(): lax.all_to_all(send_b, 'dom', 0, 0, tiled=True)]
    reshape x2 -> x1, local copies, waits for them, and re-layouts: 6.86 us -> 4.12 us  [shards(): lax.all_to_all(send_b, 'dom', 0, 0, tiled=True)]
  transfers between devices with their start and end apart: 10 -> 9, of which waited for: 5 -> 5; matrix products, arithmetic and copies ran while one was open for 25% -> 25% of each run, Pallas kernels for 4% -> 4%
where the time goes in v6:
time: 228 us; the launch traced here: 226 us
  waiting for transfers between devices  100 us (44%)
  local copies, waits for them, and re-layouts  29.1 us (13%)
  starting transfers between devices  26.7 us (12%)
  matrix products  26.3 us (12%)
  other arithmetic  25.2 us (11%)
  Pallas kernels  17.6 us (8%)
    all_to_all x1, waiting for transfers between devices, shards(): lax.all_to_all(send_a, 'dom', 0, 0, tiled=True)  84.7 us
    dot_general x2, matrix products, part(): lax.dot_general(received[:, :pixels], shifted, (((1,), (1,)), ((), ())),...  10.9 us
    ppermute x6, starting transfers between devices, ahead(): lax.ppermute(block, axis, [(i, (i + distance) % size) for i in range(size)])  10.3 us
    pallas_call x1, Pallas kernels, first_sums(): pl.pallas_call(functools.partial(first_sums_kernel, tuple(offsets), rows)...  9.22 us
    dot_general x1, matrix products, shards(): jnp.dot(pick_a.astype(particles.dtype), carried, preferred_element_type=f32)  9.13 us
    pallas_call x1, Pallas kernels, last_sums(): pl.pallas_call(functools.partial(last_sums_kernel, tuple(offsets), rows,...  8.33 us
    select_n x1, other arithmetic, translate(): return jnp.where(keep, near, far)  7.86 us
    all_to_all x1, starting transfers between devices, shards(): lax.all_to_all(send_a, 'dom', 0, 0, tiled=True)  7.56 us
  transfers between devices with their start and end apart: 9, of which 5 were waited for; matrix products, arithmetic and copies ran while one was open for 25% of the time, Pallas kernels for 4%

profile of v6, /device:TPU:0, one launch (start us, length us, event | category | flops | bytes accessed | tf_op | source)
XLA Modules:
  0.0 226.3 jit_solution(3205514163043738478)
XLA Ops:
  0.6 1.2 reshape.415
  1.9 2.1 collective-permute-start
  3.9 3.6 %collective-permute-start.1 = (bf16[16,16384]{1,0:T(8,128)(2,1)S(1)}, bf16[16,16384]{1,0:T(8,128)(2,1)}, u32[]{:S(2)}, u32[]{:S(2)}) collective-permute-start(bf16[16,16384]{1,0:T(8,128)(2,1)S(1)} %reshape.415), channel_id=1, source_target_pairs={{0,2},{1,3},{2,0},{3,1},{4,6},{5,7},{6,4},{7,5},{8,10},{9,11},{10,... | collective-permute-start | bytes 1572872 | tf_op jit(solution)/shard_map/ppermute | solution.py:124
  7.5 1.0 collective-permute-start.2
  8.5 0.9 convert_reduce_fusion
  9.5 0.7 compare_select_fusion
  10.2 0.8 select_convert_fusion
  11.0 9.1 %fusion = bf16[32,8,16512]{2,1,0:T(8,128)(2,1)} fusion(bf16[256,128]{1,0:T(8,128)(2,1)S(1)} %select_convert_fusion, bf16[256,16384]{1,0:T(8,128)(2,1)} %param.12, s32[256]{0:T(256)S(1)} %get-tuple-element.102), kind=kOutput, calls=%fused_computation.2 | convolution fusion | flops 2185461760 | bytes 16909312 | tf_op jit(solution)/shard_map/dot_general | solution.py:153
  20.2 7.6 %all-to-all-start = ((bf16[32,8,16512]{2,1,0:T(8,128)(2,1)}), bf16[32,8,16512]{2,1,0:T(8,128)(2,1)}, u32[]{:S(2)}, u32[]{:S(2)}) async-start(bf16[32,8,16512]{2,1,0:T(8,128)(2,1)} %fusion), calls=%async_computation | async-start | bytes 16908288 | tf_op jit(solution)/shard_map/all_to_all | solution.py:155
  28.4 0.6 compare_reduce_fusion.1
  29.0 0.6 compare_reduce_fusion.2
  30.4 1.1 bitcast_dynamic-update-slice_fusion.2
  31.5 1.1 bitcast_dynamic-update-slice_fusion.1
  32.6 1.1 bitcast_dynamic-update-slice_fusion
  33.7 6.3 %convolution_convert_fusion.1 = bf16[64,16512]{1,0:T(8,128)(2,1)} fusion(pred[64,256]{1,0:T(32,128)(4,1)S(1)} %iota_compare_fusion.3, bf16[256,128]{1,0:T(8,128)(2,1)S(1)} %select_convert_fusion, bf16[256,16384]{1,0:T(8,128)(2,1)} %param.12), kind=kOutput, calls=%fused_computation.3 | convolution fusion | flops 559030272 | bytes 10584064 | tf_op jit(solution)/shard_map/dot_general | solution.py:167
  39.9 4.1 %reshape.417 = bf16[32,2,16512]{2,1,0:T(2,128)(2,1)} reshape(bf16[64,16512]{1,0:T(8,128)(2,1)} %convolution_convert_fusion.1) | data formatting | bytes 4227072 | tf_op jit(solution)/shard_map/reshape | solution.py:168
  44.2 2.8 %fusion.37 = (bf16[64,16257]{1,0:T(8,128)(2,1)}, bf16[64,16257]{1,0:T(8,128)(2,1)}) fusion(bf16[64,16384]{1,0:T(8,128)(2,1)S(1)} %bitcast.44), kind=kLoop, calls=%fused_computation.103 | loop fusion | bytes 8323584 | tf_op jit(solution)/shard_map/jit(_roll_static)/slice | solution.py:24
  47.0 2.8 %fusion.40 = (bf16[64,16383]{1,0:T(8,128)(2,1)}, bf16[64,16383]{1,0:T(8,128)(2,1)}) fusion(bf16[64,16384]{1,0:T(8,128)(2,1)S(1)} %bitcast.45), kind=kLoop, calls=%fused_computation.106 | loop fusion | bytes 8388096 | tf_op jit(solution)/shard_map/jit(_roll_static)/slice | solution.py:22
  49.8 84.7 %all-to-all-done = bf16[32,8,16512]{2,1,0:T(8,128)(2,1)} async-done(((bf16[32,8,16512]{2,1,0:T(8,128)(2,1)}), bf16[32,8,16512]{2,1,0:T(8,128)(2,1)}, u32[]{:S(2)}, u32[]{:S(2)}) %all-to-all-start) | async-done | bytes 8454176 | tf_op jit(solution)/shard_map/all_to_all | solution.py:155
  134.5 5.0 %all-to-all-start.1 = ((bf16[32,2,16512]{2,1,0:T(2,128)(2,1)}), bf16[32,2,16512]{2,1,0:T(2,128)(2,1)}, u32[]{:S(2)}, u32[]{:S(2)}) async-start(bf16[32,2,16512]{2,1,0:T(2,128)(2,1)} %reshape.417), calls=%async_computation.1 | async-start | bytes 4227072 | tf_op jit(solution)/shard_map/all_to_all | solution.py:170
  139.5 7.9 %fusion.3 = (bf16[64,16384]{1,0:T(8,128)(2,1)}, bf16[64,16384]{1,0:T(8,128)(2,1)}) fusion(bf16[64,16383]{1,0:T(8,128)(2,1)} %get-tuple-element.90, bf16[64,1]{1,0:T(8,128)(2,1)S(1)} %get-tuple-element.88, bf16[64,127]{1,0:T(8,128)(2,1)S(1)} %get-tuple-element.86, bf16[64,16257]{1,0:T(8,128)(2,1)} %get-tuple-element.84, s32[16384]{0:T(1024)S(1)} %get-tuple-element.111, ...), kind=kLoop, calls=%fused_computation.12 | loop fusion | flops 22020096 | bytes 12730368 | tf_op jit(solution)/shard_map/jit(_where)/select_n | solution.py:30
  148.1 1.1 convert_reduce_fusion.1
  149.4 6.3 %fusion.35 = (f32[256]{0:T(256)S(1)}, f32[256,192]{0,1:T(8,128)S(1)}, f32[256,192]{0,1:T(8,128)S(1)}) fusion(f32[256,64]{0,1:T(8,128)S(1)} %tile.17, f32[192]{0:T(256)S(1)} %sub.182, f32[256]{0:T(256)S(1)} %get-tuple-element.72, bf16[64,16384]{1,0:T(8,128)(2,1)} %get-tuple-element.95, bf16[64,16384]{1,0:T(8,128)(2,1)S(1)} %bitcast.47, ...), kind=kOutput, calls=%fused_computation.101 | convolution fusion | flops 1629732608 | bytes 15141632 | tf_op jit(solution)/shard_map/dot_general | solution.py:184
  155.7 0.7 fusion.14
  156.6 9.2 %shard_map.93.acc_ref = f32[64,16384]{1,0:T(8,128)} custom-call(bf16[192,256]{1,0:T(8,128)(2,1)} %get-tuple-element.93.w_ref, bf16[256,16512]{1,0:T(8,128)(2,1)} %bitcast.1.x_ref), custom_call_target="tpu_custom_call" | custom-call | flops 1610612736 | bytes 12681216 | tf_op jit(solution)/shard_map/pallas_call | solution.py:73
  165.9 3.6 %all-to-all-done.1 = bf16[32,2,16512]{2,1,0:T(2,128)(2,1)} async-done(((bf16[32,2,16512]{2,1,0:T(2,128)(2,1)}), bf16[32,2,16512]{2,1,0:T(2,128)(2,1)}, u32[]{:S(2)}, u32[]{:S(2)}) %all-to-all-start.1) | async-done | bytes 2113568 | tf_op jit(solution)/shard_map/all_to_all | solution.py:170
  169.5 4.1 %reshape.418.x_ref = bf16[64,16512]{1,0:T(8,128)(2,1)} reshape(bf16[32,2,16512]{2,1,0:T(2,128)(2,1)} %all-to-all-done.1) | data formatting | bytes 4227072 | tf_op jit(solution)/shard_map/reshape | solution.py:170
  173.6 1.0 convert_reduce_fusion.2
  174.7 4.6 %fusion.36 = (f32[64]{0:T(128)S(1)}, f32[64,192]{0,1:T(8,128)S(1)}, f32[64,192]{0,1:T(8,128)S(1)}) fusion(f32[64,64]{0,1:T(8,128)S(1)} %bitcast.59, f32[192]{0:T(256)S(1)} %sub.182, f32[64]{0:T(128)S(1)} %get-tuple-element.74, bf16[64,16384]{1,0:T(8,128)(2,1)} %get-tuple-element.95, bf16[64,16384]{1,0:T(8,128)(2,1)S(1)} %bitcast.48, ...), kind=kOutput, calls=%fused_computation.102 | convolution fusion | flops 421588928 | bytes 8504576 | tf_op jit(solution)/shard_map/dot_general | solution.py:184
  179.4 0.7 fusion.18
  180.3 1.3 fusion.27
  181.8 0.7 fusion.28
  183.2 8.3 %shard_map.94 = bf16[64,16512]{1,0:T(8,128)(2,1)} custom-call(bf16[192,64]{1,0:T(8,128)(2,1)} %get-tuple-element.97.w_ref, bf16[64,16512]{1,0:T(8,128)(2,1)} %reshape.418.x_ref, f32[64,16384]{1,0:T(8,128)} %shard_map.93.acc_ref, bf16[64,128]{1,0:T(8,128)(2,1)} %copy-done.1), custom_call_target="tpu_custom_call" | custom-call | flops 402653184 | bytes 8429568 | tf_op jit(solution)/shard_map/pallas_call | solution.py:94
  191.6 2.6 %constant_dynamic-slice_fusion = (bf16[1,16,16512]{2,1,0:T(8,128)(2,1)S(1)}, bf16[16,16512]{1,0:T(8,128)(2,1)S(1)}, bf16[16,16512]{1,0:T(8,128)(2,1)}, bf16[16,16512]{1,0:T(8,128)(2,1)}) fusion(bf16[4,16,16512]{2,1,0:T(8,128)(2,1)} %bitcast.49, s32[]{:T(128)S(6)} %select_n.107, s32[]{:T(128)S(6)} %select_n.124, s32[]{:T(128)S(6)} %select_n.122, s32[]{:T(128)S(6)} %select_n.120), kind=kLoop, calls=%fused_computation.69 | loop fusion | bytes 4227088 | tf_op jit(solution)/shard_map/jit(dynamic_index_in_dim)/dynamic_slice | solution.py:220
  194.2 1.0 collective-permute-start.3
  195.7 2.2 collective-permute-start.5
  199.2 0.8 reshape.438
  200.0 3.9 %all-to-all-start.2 = ((f32[32,1,330]{2,1,0:T(1,128)}), f32[32,1,330]{2,1,0:T(1,128)S(1)}, u32[]{:S(2)}, u32[]{:S(2)}) async-start(f32[32,1,330]{2,1,0:T(1,128)} %reshape.438), calls=%async_computation.2 | async-start | bytes 98304 | tf_op jit(solution)/shard_map/all_to_all | solution.py:209
  203.9 7.4 %all-to-all-done.2 = f32[32,1,330]{2,1,0:T(1,128)S(1)} async-done(((f32[32,1,330]{2,1,0:T(1,128)}), f32[32,1,330]{2,1,0:T(1,128)S(1)}, u32[]{:S(2)}, u32[]{:S(2)}) %all-to-all-start.2) | async-done | bytes 42272 | tf_op jit(solution)/shard_map/all_to_all | solution.py:209
  211.8 0.8 reduce.43
  212.7 0.7 gather_fusion
  213.5 0.7 copy.57
  214.2 0.7 slice_reduce_fusion.1
  214.9 3.9 %collective-permute-done.3 = bf16[16,16512]{1,0:T(8,128)(2,1)S(1)} collective-permute-done((bf16[16,16512]{1,0:T(8,128)(2,1)}, bf16[16,16512]{1,0:T(8,128)(2,1)S(1)}, u32[]{:S(2)}, u32[]{:S(2)}) %collective-permute-start.3) | collective-permute-done | bytes 528416 | tf_op jit(solution)/shard_map/ppermute | solution.py:124
  219.7 2.3 %maximum_convert_fusion = f32[4,16,16512]{2,1,0:T(8,128)} fusion(bf16[1,16,16512]{2,1,0:T(8,128)(2,1)S(1)} %bitcast.55, bf16[1,16,16512]{2,1,0:T(8,128)(2,1)S(1)} %bitcast.53, bf16[1,16,16512]{2,1,0:T(8,128)(2,1)S(1)} %bitcast.51, bf16[1,16,16512]{2,1,0:T(8,128)(2,1)S(1)} %get-tuple-element.80), kind=kLoop, calls=%fused_computation.15 | loop fusion | flops 4227072 | bytes 6340608 | tf_op jit(solution)/shard_map/convert_element_type | solution.py:224
  222.0 0.6 copy.58
  222.7 2.5 %slice_reduce_fusion = bf16[16,16384]{1,0:T(8,128)(2,1)S(1)} fusion(f32[4,16,16512]{2,1,0:T(8,128)} %maximum_convert_fusion), kind=kLoop, calls=%fused_computation.10 | loop fusion | flops 786432 | bytes 4718592 | tf_op jit(solution)/shard_map/reduce_sum | solution.py:225
  225.2 1.1 convert_element_type.197
  (63 shorter events, 7.0 us)
Async XLA Ops:
  1.9 28.5 %collective-permute-start = (bf16[16,16384]{1,0:T(8,128)(2,1)S(1)}, bf16[16,16384]{1,0:T(8,128)(2,1)}, u32[]{:S(2)}, u32[]{:S(2)}) collective-permute-start(bf16[16,16384]{1,0:T(8,128)(2,1)S(1)} %reshape.415), channel_id=1, source_target_pairs={{0,1},{1,2},{2,3},{3,0},{4,5},{5,6},{6,7},{7,4},{8,9},{9,10},{10,1... | collective-permute-start | bytes 1572872 | tf_op jit(solution)/shard_map/ppermute | solution.py:124
  3.9 27.5 %collective-permute-start.1 = (bf16[16,16384]{1,0:T(8,128)(2,1)S(1)}, bf16[16,16384]{1,0:T(8,128)(2,1)}, u32[]{:S(2)}, u32[]{:S(2)}) collective-permute-start(bf16[16,16384]{1,0:T(8,128)(2,1)S(1)} %reshape.415), channel_id=1, source_target_pairs={{0,2},{1,3},{2,0},{3,1},{4,6},{5,7},{6,4},{7,5},{8,10},{9,11},{10,... | collective-permute-start | bytes 1572872 | tf_op jit(solution)/shard_map/ppermute | solution.py:124
  7.5 25.0 %collective-permute-start.2 = (bf16[16,16384]{1,0:T(8,128)(2,1)S(1)}, bf16[16,16384]{1,0:T(8,128)(2,1)}, u32[]{:S(2)}, u32[]{:S(2)}) collective-permute-start(bf16[16,16384]{1,0:T(8,128)(2,1)S(1)} %reshape.415), channel_id=1, source_target_pairs={{0,3},{1,0},{2,1},{3,2},{4,7},{5,4},{6,5},{7,6},{8,11},{9,8},{10,9... | collective-permute-start | bytes 1572872 | tf_op jit(solution)/shard_map/ppermute | solution.py:124
  20.2 7.6 %copy-start = (bf16[8,2,16384]{2,1,0:T(2,128)(2,1)S(1)}, bf16[8,2,16384]{2,1,0:T(2,128)(2,1)}, u32[]{:S(2)}) copy-start(bf16[8,2,16384]{2,1,0:T(2,128)(2,1)} %param.16) | copy-start | bytes 1572868
  20.2 114.3 %all-to-all-start = ((bf16[32,8,16512]{2,1,0:T(8,128)(2,1)}), bf16[32,8,16512]{2,1,0:T(8,128)(2,1)}, u32[]{:S(2)}, u32[]{:S(2)}) async-start(bf16[32,8,16512]{2,1,0:T(8,128)(2,1)} %fusion), calls=%async_computation | async-start | bytes 16908288 | tf_op jit(solution)/shard_map/all_to_all | solution.py:155
  27.7 0.7 copy-start.2
  134.5 35.0 %all-to-all-start.1 = ((bf16[32,2,16512]{2,1,0:T(2,128)(2,1)}), bf16[32,2,16512]{2,1,0:T(2,128)(2,1)}, u32[]{:S(2)}, u32[]{:S(2)}) async-start(bf16[32,2,16512]{2,1,0:T(2,128)(2,1)} %reshape.417), calls=%async_computation.1 | async-start | bytes 4227072 | tf_op jit(solution)/shard_map/all_to_all | solution.py:170
  182.6 0.6 copy-start.1
  194.2 24.6 %collective-permute-start.3 = (bf16[16,16512]{1,0:T(8,128)(2,1)}, bf16[16,16512]{1,0:T(8,128)(2,1)S(1)}, u32[]{:S(2)}, u32[]{:S(2)}) collective-permute-start(bf16[16,16512]{1,0:T(8,128)(2,1)} %get-tuple-element.83), channel_id=1, source_target_pairs={{0,1},{1,2},{2,3},{3,0},{4,5},{5,6},{6,7},{7,4},{8,9},{9,10},{10,1... | collective-permute-start | bytes 1585160 | tf_op jit(solution)/shard_map/ppermute | solution.py:124
  195.2 23.6 %collective-permute-start.4 = (bf16[16,16512]{1,0:T(8,128)(2,1)}, bf16[16,16512]{1,0:T(8,128)(2,1)S(1)}, u32[]{:S(2)}, u32[]{:S(2)}) collective-permute-start(bf16[16,16512]{1,0:T(8,128)(2,1)} %get-tuple-element.82), channel_id=1, source_target_pairs={{0,2},{1,3},{2,0},{3,1},{4,6},{5,7},{6,4},{7,5},{8,10},{9,11},{10,... | collective-permute-start | bytes 1585160 | tf_op jit(solution)/shard_map/ppermute | solution.py:124
  195.7 23.8 %collective-permute-start.5 = (bf16[16,16512]{1,0:T(8,128)(2,1)S(1)}, bf16[16,16512]{1,0:T(8,128)(2,1)S(1)}, u32[]{:S(2)}, u32[]{:S(2)}) collective-permute-start(bf16[16,16512]{1,0:T(8,128)(2,1)S(1)} %get-tuple-element.81), channel_id=1, source_target_pairs={{0,3},{1,0},{2,1},{3,2},{4,7},{5,4},{6,5},{7,6},{8,11},{9,8},{10,9... | collective-permute-start | bytes 1585160 | tf_op jit(solution)/shard_map/ppermute | solution.py:124
  200.0 11.3 %all-to-all-start.2 = ((f32[32,1,330]{2,1,0:T(1,128)}), f32[32,1,330]{2,1,0:T(1,128)S(1)}, u32[]{:S(2)}, u32[]{:S(2)}) async-start(f32[32,1,330]{2,1,0:T(1,128)} %reshape.438), calls=%async_computation.2 | async-start | bytes 98304 | tf_op jit(solution)/shard_map/all_to_all | solution.py:209

commit v7 on v6

--- a/solution.py
+++ b/solution.py
@@ -48,20 +48,17 @@
 
 def last_sums_kernel(offsets, rows, chunk, w_ref, x_ref, acc_ref, tail_ref, out_ref, moved_ref):
     k = pl.program_id(0)
-    x = x_ref[...].astype(jnp.float32)
-    total = acc_ref[...]
+    n = x_ref.shape[0]
+    x = x_ref[:, pl.ds(k * chunk, chunk)]
+    wide = x.astype(jnp.float32)
     for u, t in enumerate(offsets):
         if t % IMG:
             for j in range(chunk // IMG):
-                piece = x[:, j * IMG:(j + 1) * IMG]
-                moved_ref[:, j * IMG:(j + 1) * IMG] = pltpu.roll(piece, shift=t % IMG, axis=1).astype(
-                    moved_ref.dtype
-                )
-            shifted_x = moved_ref[...]
+                piece = pltpu.roll(wide[:, j * IMG:(j + 1) * IMG], shift=t % IMG, axis=1)
+                moved_ref[u * n:(u + 1) * n, j * IMG:(j + 1) * IMG] = piece.astype(moved_ref.dtype)
         else:
-            shifted_x = x_ref[...]
-        w = w_ref[u * rows:(u + 1) * rows, :]
-        total = total + jnp.dot(w, shifted_x, preferred_element_type=jnp.float32)
+            moved_ref[u * n:(u + 1) * n, :] = x
+    total = acc_ref[...] + jnp.dot(w_ref[...], moved_ref[...], preferred_element_type=jnp.float32)
     out_ref[:, pl.ds(k * chunk, chunk)] = total.astype(out_ref.dtype)
     pixels = out_ref.shape[1] - tail_ref.shape[1]
     out_ref[:, pixels:] = tail_ref[...]
@@ -88,27 +85,29 @@
 
 
 def last_sums(w, x, acc, tail, offsets, pixels):
-    rows = w.shape[0] // len(offsets)
+    rows = acc.shape[0]
     chunk = min(CHUNK, pixels)
     width = pixels + tail.shape[1]
+    n = x.shape[0]
+    stacked_w = w.reshape(len(offsets), rows, n).transpose(1, 0, 2).reshape(rows, len(offsets) * n)
     return pl.pallas_call(
         functools.partial(last_sums_kernel, tuple(offsets), rows, chunk),
         grid=(pixels // chunk,),
         in_specs=[
-            pl.BlockSpec(w.shape, lambda k: (0, 0)),
-            pl.BlockSpec((x.shape[0], chunk), lambda k: (0, k)),
+            pl.BlockSpec(stacked_w.shape, lambda k: (0, 0)),
+            pl.BlockSpec(x.shape, lambda k: (0, 0)),
             pl.BlockSpec((rows, chunk), lambda k: (0, k)),
             pl.BlockSpec(tail.shape, lambda k: (0, 0)),
         ],
         out_specs=pl.BlockSpec((rows, width), lambda k: (0, 0)),
         out_shape=jax.ShapeDtypeStruct((rows, width), jnp.bfloat16),
-        scratch_shapes=[pltpu.VMEM((x.shape[0], chunk), x.dtype)],
+        scratch_shapes=[pltpu.VMEM((len(offsets) * n, chunk), x.dtype)],
         cost_estimate=pl.CostEstimate(
-            flops=2 * w.shape[0] * pixels * x.shape[0],
+            flops=2 * w.shape[0] * pixels * n,
             transcendentals=0,
-            bytes_accessed=2 * (x.shape[0] * pixels + w.size + rows * width) + 4 * rows * pixels,
+            bytes_accessed=2 * (n * width + w.size + rows * width) + 4 * rows * pixels,
         ),
-    )(w, x, acc, tail)
+    )(stacked_w, x, acc, tail)
 
 
 def split_bf16(values):
@@ -153,7 +152,7 @@
     send_a = jnp.dot(pick_a.astype(particles.dtype), carried, preferred_element_type=f32)
     send_a = send_a.astype(particles.dtype).reshape(count_dom, rows_a, width)
     got_a = lax.all_to_all(send_a, "dom", 0, 0, tiled=True).reshape(count_dom * rows_a, width)
-    own_proj = projections.reshape(-1, pixels)
+    _, own_proj = lax.optimization_barrier((send_a, projections.reshape(-1, pixels)))
     ref_here = lax.axis_index("ref")
     blocks = jnp.zeros((count_ref,) + own_proj.shape, own_proj.dtype)
     blocks = lax.dynamic_update_index_in_dim(blocks, own_proj, ref_here, 0)

time: 228 us -> 228 us (level)
    ppermute x6, waiting for transfers between devices: 4.56 us -> 15.3 us  [ahead(): lax.ppermute(block, axis, [(i, (i + distance) % size) for i in range(size)])]
    all_to_all x1, waiting for transfers between devices: 84.7 us -> 75 us  [shards(): lax.all_to_all(send_a, 'dom', 0, 0, tiled=True)]
  transfers between devices with their start and end apart: 9 -> 9, of which waited for: 5 -> 6; matrix products, arithmetic and copies ran while one was open for 25% -> 19% of each run, Pallas kernels for 4% -> 4%
where the time goes in v7:
time: 228 us; the launch traced here: 227 us
  waiting for transfers between devices  101 us (44%)
  local copies, waits for them, and re-layouts  28.6 us (13%)
  matrix products  26.8 us (12%)
  starting transfers between devices  26.5 us (12%)
  other arithmetic  24.8 us (11%)
  Pallas kernels  17.8 us (8%)
    all_to_all x1, waiting for transfers between devices, shards(): lax.all_to_all(send_a, 'dom', 0, 0, tiled=True)  75 us
    ppermute x6, waiting for transfers between devices, ahead(): lax.ppermute(block, axis, [(i, (i + distance) % size) for i in range(size)])  15.3 us
    dot_general x2, matrix products, part(): lax.dot_general(received[:, :pixels], shifted, (((1,), (1,)), ((), ())),...  11.4 us
    ppermute x6, starting transfers between devices, ahead(): lax.ppermute(block, axis, [(i, (i + distance) % size) for i in range(size)])  10.3 us
    pallas_call x1, Pallas kernels, first_sums(): pl.pallas_call(functools.partial(first_sums_kernel, tuple(offsets), rows)...  9.22 us
    dot_general x1, matrix products, shards(): jnp.dot(pick_a.astype(particles.dtype), carried, preferred_element_type=f32)  9.13 us
    pallas_call x1, Pallas kernels, last_sums(): pl.pallas_call(functools.partial(last_sums_kernel, tuple(offsets), rows,...  8.58 us
    select_n x1, other arithmetic, translate(): return jnp.where(keep, near, far)  7.86 us
  transfers between devices with their start and end apart: 9, of which 6 were waited for; matrix products, arithmetic and copies ran while one was open for 19% of the time, Pallas kernels for 4%

profile of v7, /device:TPU:0, one launch (start us, length us, event | category | flops | bytes accessed | tf_op | source)
XLA Modules:
  0.0 226.9 jit_solution(12561806159971638249)
XLA Ops:
  0.7 0.9 convert_reduce_fusion
  1.6 1.2 reshape.420
  2.8 0.7 compare_select_fusion
  3.5 0.8 select_convert_fusion
  4.4 9.1 %fusion = bf16[32,8,16512]{2,1,0:T(8,128)(2,1)} fusion(bf16[256,128]{1,0:T(8,128)(2,1)S(1)} %select_convert_fusion, bf16[256,16384]{1,0:T(8,128)(2,1)} %param.12, s32[256]{0:T(256)S(1)} %get-tuple-element.104), kind=kOutput, calls=%fused_computation.2 | convolution fusion | flops 2185461760 | bytes 16909312 | tf_op jit(solution)/shard_map/dot_general | solution.py:152
  13.5 2.0 collective-permute-start
  15.5 3.6 %collective-permute-start.1 = (bf16[16,16384]{1,0:T(8,128)(2,1)S(1)}, bf16[16,16384]{1,0:T(8,128)(2,1)}, u32[]{:S(2)}, u32[]{:S(2)}) collective-permute-start(bf16[16,16384]{1,0:T(8,128)(2,1)S(1)} %reshape.420), channel_id=1, source_target_pairs={{0,2},{1,3},{2,0},{3,1},{4,6},{5,7},{6,4},{7,5},{8,10},{9,11},{10,... | collective-permute-start | bytes 1572872 | tf_op jit(solution)/shard_map/ppermute | solution.py:123
  19.1 1.0 collective-permute-start.2
  20.1 7.4 %all-to-all-start = ((bf16[32,8,16512]{2,1,0:T(8,128)(2,1)}), bf16[32,8,16512]{2,1,0:T(8,128)(2,1)}, u32[]{:S(2)}, u32[]{:S(2)}) async-start(bf16[32,8,16512]{2,1,0:T(8,128)(2,1)} %fusion), calls=%async_computation | async-start | bytes 16908288 | tf_op jit(solution)/shard_map/all_to_all | solution.py:154
  28.2 0.6 compare_reduce_fusion.1
  28.8 0.6 compare_reduce_fusion.2
  30.2 1.1 bitcast_dynamic-update-slice_fusion.2
  31.3 10.8 %collective-permute-done.1 = bf16[16,16384]{1,0:T(8,128)(2,1)} collective-permute-done((bf16[16,16384]{1,0:T(8,128)(2,1)S(1)}, bf16[16,16384]{1,0:T(8,128)(2,1)}, u32[]{:S(2)}, u32[]{:S(2)}) %collective-permute-start.1) | collective-permute-done | bytes 524320 | tf_op jit(solution)/shard_map/ppermute | solution.py:123
  42.1 1.1 bitcast_dynamic-update-slice_fusion.1
  43.2 6.3 %convolution_convert_fusion.1 = bf16[64,16512]{1,0:T(8,128)(2,1)} fusion(pred[64,256]{1,0:T(32,128)(4,1)S(1)} %iota_compare_fusion.3, bf16[256,128]{1,0:T(8,128)(2,1)S(1)} %select_convert_fusion, bf16[256,16384]{1,0:T(8,128)(2,1)} %param.12), kind=kOutput, calls=%fused_computation.3 | convolution fusion | flops 559030272 | bytes 10584064 | tf_op jit(solution)/shard_map/dot_general | solution.py:166
  49.5 4.1 %reshape.422 = bf16[32,2,16512]{2,1,0:T(2,128)(2,1)} reshape(bf16[64,16512]{1,0:T(8,128)(2,1)} %convolution_convert_fusion.1) | data formatting | bytes 4227072 | tf_op jit(solution)/shard_map/reshape | solution.py:167
  53.8 2.8 %fusion.37 = (bf16[64,16257]{1,0:T(8,128)(2,1)}, bf16[64,16257]{1,0:T(8,128)(2,1)}) fusion(bf16[64,16384]{1,0:T(8,128)(2,1)S(1)} %bitcast.48), kind=kLoop, calls=%fused_computation.103 | loop fusion | bytes 8323584 | tf_op jit(solution)/shard_map/jit(_roll_static)/slice | solution.py:24
  56.6 2.8 %fusion.40 = (bf16[64,16383]{1,0:T(8,128)(2,1)}, bf16[64,16383]{1,0:T(8,128)(2,1)}) fusion(bf16[64,16384]{1,0:T(8,128)(2,1)S(1)} %bitcast.49), kind=kLoop, calls=%fused_computation.106 | loop fusion | bytes 8388096 | tf_op jit(solution)/shard_map/jit(_roll_static)/slice | solution.py:22
  59.3 75.0 %all-to-all-done = bf16[32,8,16512]{2,1,0:T(8,128)(2,1)} async-done(((bf16[32,8,16512]{2,1,0:T(8,128)(2,1)}), bf16[32,8,16512]{2,1,0:T(8,128)(2,1)}, u32[]{:S(2)}, u32[]{:S(2)}) %all-to-all-start) | async-done | bytes 8454176 | tf_op jit(solution)/shard_map/all_to_all | solution.py:154
  134.3 5.0 %all-to-all-start.1 = ((bf16[32,2,16512]{2,1,0:T(2,128)(2,1)}), bf16[32,2,16512]{2,1,0:T(2,128)(2,1)}, u32[]{:S(2)}, u32[]{:S(2)}) async-start(bf16[32,2,16512]{2,1,0:T(2,128)(2,1)} %reshape.422), calls=%async_computation.1 | async-start | bytes 4227072 | tf_op jit(solution)/shard_map/all_to_all | solution.py:169
  139.3 7.9 %fusion.3 = (bf16[64,16384]{1,0:T(8,128)(2,1)}, bf16[64,16384]{1,0:T(8,128)(2,1)}) fusion(bf16[64,16383]{1,0:T(8,128)(2,1)} %get-tuple-element.92, bf16[64,1]{1,0:T(8,128)(2,1)S(1)} %get-tuple-element.90, bf16[64,127]{1,0:T(8,128)(2,1)S(1)} %get-tuple-element.88, bf16[64,16257]{1,0:T(8,128)(2,1)} %get-tuple-element.86, s32[16384]{0:T(1024)S(1)} %get-tuple-element.113, ...), kind=kLoop, calls=%fused_computation.12 | loop fusion | flops 22020096 | bytes 12730368 | tf_op jit(solution)/shard_map/jit(_where)/select_n | solution.py:30
  147.9 1.1 convert_reduce_fusion.1
  149.2 6.3 %fusion.35 = (f32[256]{0:T(256)S(1)}, f32[256,192]{0,1:T(8,128)S(1)}, f32[256,192]{0,1:T(8,128)S(1)}) fusion(f32[256,64]{0,1:T(8,128)S(1)} %tile.17, f32[192]{0:T(256)S(1)} %sub.182, f32[256]{0:T(256)S(1)} %get-tuple-element.74, bf16[64,16384]{1,0:T(8,128)(2,1)} %get-tuple-element.97, bf16[64,16384]{1,0:T(8,128)(2,1)S(1)} %bitcast.51, ...), kind=kOutput, calls=%fused_computation.101 | convolution fusion | flops 1629732608 | bytes 15141632 | tf_op jit(solution)/shard_map/dot_general | solution.py:183
  155.6 0.7 fusion.14
  156.5 9.2 %shard_map.93.acc_ref = f32[64,16384]{1,0:T(8,128)} custom-call(bf16[192,256]{1,0:T(8,128)(2,1)} %get-tuple-element.95.w_ref, bf16[256,16512]{1,0:T(8,128)(2,1)} %bitcast.1.x_ref), custom_call_target="tpu_custom_call" | custom-call | flops 1610612736 | bytes 12681216 | tf_op jit(solution)/shard_map/pallas_call | solution.py:70
  165.7 3.6 %all-to-all-done.1 = bf16[32,2,16512]{2,1,0:T(2,128)(2,1)} async-done(((bf16[32,2,16512]{2,1,0:T(2,128)(2,1)}), bf16[32,2,16512]{2,1,0:T(2,128)(2,1)}, u32[]{:S(2)}, u32[]{:S(2)}) %all-to-all-start.1) | async-done | bytes 2113568 | tf_op jit(solution)/shard_map/all_to_all | solution.py:169
  169.3 4.1 %reshape.423.x_ref = bf16[64,16512]{1,0:T(8,128)(2,1)} reshape(bf16[32,2,16512]{2,1,0:T(2,128)(2,1)} %all-to-all-done.1) | data formatting | bytes 4227072 | tf_op jit(solution)/shard_map/reshape | solution.py:169
  173.4 1.0 convert_reduce_fusion.2
  174.6 5.1 %fusion.36 = (f32[64]{0:T(128)S(1)}, f32[64,192]{1,0:T(8,128)S(1)}, f32[64,192]{1,0:T(8,128)S(1)}) fusion(f32[64,192]{1,0:T(8,128)S(1)} %copy.69, f32[192]{0:T(256)S(1)} %sub.182, f32[64]{0:T(128)S(1)} %get-tuple-element.76, bf16[64,16384]{1,0:T(8,128)(2,1)} %get-tuple-element.97, bf16[64,16384]{1,0:T(8,128)(2,1)S(1)} %bitcast.52, ...), kind=kOutput, calls=%fused_computation.102 | convolution fusion | flops 421588928 | bytes 8537344 | tf_op jit(solution)/shard_map/dot_general | solution.py:183
  180.3 1.3 fusion.27
  181.7 0.7 fusion.28
  182.8 0.7 copy.76.w_ref
  183.6 8.6 %shard_map.94 = bf16[64,16512]{1,0:T(8,128)(2,1)} custom-call(bf16[64,192]{1,0:T(8,128)(2,1)} %copy.76.w_ref, bf16[64,16512]{1,0:T(8,128)(2,1)} %reshape.423.x_ref, f32[64,16384]{1,0:T(8,128)} %shard_map.93.acc_ref, bf16[64,128]{1,0:T(8,128)(2,1)} %copy-done), custom_call_target="tpu_custom_call" | custom-call | flops 402653184 | bytes 8445952 | tf_op jit(solution)/shard_map/pallas_call | solution.py:93
  192.1 2.6 %constant_dynamic-slice_fusion = (bf16[1,16,16512]{2,1,0:T(8,128)(2,1)S(1)}, bf16[16,16512]{1,0:T(8,128)(2,1)S(1)}, bf16[16,16512]{1,0:T(8,128)(2,1)}, bf16[16,16512]{1,0:T(8,128)(2,1)}) fusion(bf16[4,16,16512]{2,1,0:T(8,128)(2,1)} %bitcast.53, s32[]{:T(128)S(6)} %select_n.107, s32[]{:T(128)S(6)} %select_n.124, s32[]{:T(128)S(6)} %select_n.122, s32[]{:T(128)S(6)} %select_n.120), kind=kLoop, calls=%fused_computation.70 | loop fusion | bytes 4227088 | tf_op jit(solution)/shard_map/jit(dynamic_index_in_dim)/dynamic_slice | solution.py:219
  194.8 1.0 collective-permute-start.3
  196.2 2.2 collective-permute-start.5
  199.9 0.8 reshape.445
  200.7 3.9 %all-to-all-start.2 = ((f32[32,1,330]{2,1,0:T(1,128)}), f32[32,1,330]{2,1,0:T(1,128)S(1)}, u32[]{:S(2)}, u32[]{:S(2)}) async-start(f32[32,1,330]{2,1,0:T(1,128)} %reshape.445), calls=%async_computation.2 | async-start | bytes 98304 | tf_op jit(solution)/shard_map/all_to_all | solution.py:208
  204.5 7.4 %all-to-all-done.2 = f32[32,1,330]{2,1,0:T(1,128)S(1)} async-done(((f32[32,1,330]{2,1,0:T(1,128)}), f32[32,1,330]{2,1,0:T(1,128)S(1)}, u32[]{:S(2)}, u32[]{:S(2)}) %all-to-all-start.2) | async-done | bytes 42272 | tf_op jit(solution)/shard_map/all_to_all | solution.py:208
  212.5 0.8 reduce.43
  213.4 0.7 gather_fusion
  214.1 0.7 copy.77
  214.8 0.7 slice_reduce_fusion.1
  215.6 3.8 %collective-permute-done.3 = bf16[16,16512]{1,0:T(8,128)(2,1)S(1)} collective-permute-done((bf16[16,16512]{1,0:T(8,128)(2,1)}, bf16[16,16512]{1,0:T(8,128)(2,1)S(1)}, u32[]{:S(2)}, u32[]{:S(2)}) %collective-permute-start.3) | collective-permute-done | bytes 528416 | tf_op jit(solution)/shard_map/ppermute | solution.py:123
  220.2 2.3 %maximum_convert_fusion = f32[4,16,16512]{2,1,0:T(8,128)} fusion(bf16[1,16,16512]{2,1,0:T(8,128)(2,1)S(1)} %bitcast.59, bf16[1,16,16512]{2,1,0:T(8,128)(2,1)S(1)} %bitcast.57, bf16[1,16,16512]{2,1,0:T(8,128)(2,1)S(1)} %bitcast.55, bf16[1,16,16512]{2,1,0:T(8,128)(2,1)S(1)} %get-tuple-element.82), kind=kLoop, calls=%fused_computation.15 | loop fusion | flops 4227072 | bytes 6340608 | tf_op jit(solution)/shard_map/convert_element_type | solution.py:223
  222.6 0.6 copy.78
  223.3 2.5 %slice_reduce_fusion = bf16[16,16384]{1,0:T(8,128)(2,1)S(1)} fusion(f32[4,16,16512]{2,1,0:T(8,128)} %maximum_convert_fusion), kind=kLoop, calls=%fused_computation.10 | loop fusion | flops 786432 | bytes 4718592 | tf_op jit(solution)/shard_map/reduce_sum | solution.py:224
  225.7 1.1 convert_element_type.197
  (66 shorter events, 7.1 us)
Async XLA Ops:
  13.5 16.7 %collective-permute-start = (bf16[16,16384]{1,0:T(8,128)(2,1)S(1)}, bf16[16,16384]{1,0:T(8,128)(2,1)}, u32[]{:S(2)}, u32[]{:S(2)}) collective-permute-start(bf16[16,16384]{1,0:T(8,128)(2,1)S(1)} %reshape.420), channel_id=1, source_target_pairs={{0,1},{1,2},{2,3},{3,0},{4,5},{5,6},{6,7},{7,4},{8,9},{9,10},{10,1... | collective-permute-start | bytes 1572872 | tf_op jit(solution)/shard_map/ppermute | solution.py:123
  15.5 26.6 %collective-permute-start.1 = (bf16[16,16384]{1,0:T(8,128)(2,1)S(1)}, bf16[16,16384]{1,0:T(8,128)(2,1)}, u32[]{:S(2)}, u32[]{:S(2)}) collective-permute-start(bf16[16,16384]{1,0:T(8,128)(2,1)S(1)} %reshape.420), channel_id=1, source_target_pairs={{0,2},{1,3},{2,0},{3,1},{4,6},{5,7},{6,4},{7,5},{8,10},{9,11},{10,... | collective-permute-start | bytes 1572872 | tf_op jit(solution)/shard_map/ppermute | solution.py:123
  19.1 24.1 %collective-permute-start.2 = (bf16[16,16384]{1,0:T(8,128)(2,1)S(1)}, bf16[16,16384]{1,0:T(8,128)(2,1)S(1)}, u32[]{:S(2)}, u32[]{:S(2)}) collective-permute-start(bf16[16,16384]{1,0:T(8,128)(2,1)S(1)} %reshape.420), channel_id=1, source_target_pairs={{0,3},{1,0},{2,1},{3,2},{4,7},{5,4},{6,5},{7,6},{8,11},{9,8},{10,9... | collective-permute-start | bytes 1572872 | tf_op jit(solution)/shard_map/ppermute | solution.py:123
  20.1 114.2 %all-to-all-start = ((bf16[32,8,16512]{2,1,0:T(8,128)(2,1)}), bf16[32,8,16512]{2,1,0:T(8,128)(2,1)}, u32[]{:S(2)}, u32[]{:S(2)}) async-start(bf16[32,8,16512]{2,1,0:T(8,128)(2,1)} %fusion), calls=%async_computation | async-start | bytes 16908288 | tf_op jit(solution)/shard_map/all_to_all | solution.py:154
  27.5 0.7 copy-start.1
  134.3 35.0 %all-to-all-start.1 = ((bf16[32,2,16512]{2,1,0:T(2,128)(2,1)}), bf16[32,2,16512]{2,1,0:T(2,128)(2,1)}, u32[]{:S(2)}, u32[]{:S(2)}) async-start(bf16[32,2,16512]{2,1,0:T(2,128)(2,1)} %reshape.422), calls=%async_computation.1 | async-start | bytes 4227072 | tf_op jit(solution)/shard_map/all_to_all | solution.py:169
  182.6 1.0 copy-start
  194.8 24.6 %collective-permute-start.3 = (bf16[16,16512]{1,0:T(8,128)(2,1)}, bf16[16,16512]{1,0:T(8,128)(2,1)S(1)}, u32[]{:S(2)}, u32[]{:S(2)}) collective-permute-start(bf16[16,16512]{1,0:T(8,128)(2,1)} %get-tuple-element.85), channel_id=1, source_target_pairs={{0,1},{1,2},{2,3},{3,0},{4,5},{5,6},{6,7},{7,4},{8,9},{9,10},{10,1... | collective-permute-start | bytes 1585160 | tf_op jit(solution)/shard_map/ppermute | solution.py:123
  195.8 23.6 %collective-permute-start.4 = (bf16[16,16512]{1,0:T(8,128)(2,1)}, bf16[16,16512]{1,0:T(8,128)(2,1)S(1)}, u32[]{:S(2)}, u32[]{:S(2)}) collective-permute-start(bf16[16,16512]{1,0:T(8,128)(2,1)} %get-tuple-element.84), channel_id=1, source_target_pairs={{0,2},{1,3},{2,0},{3,1},{4,6},{5,7},{6,4},{7,5},{8,10},{9,11},{10,... | collective-permute-start | bytes 1585160 | tf_op jit(solution)/shard_map/ppermute | solution.py:123
  196.2 23.8 %collective-permute-start.5 = (bf16[16,16512]{1,0:T(8,128)(2,1)S(1)}, bf16[16,16512]{1,0:T(8,128)(2,1)S(1)}, u32[]{:S(2)}, u32[]{:S(2)}) collective-permute-start(bf16[16,16512]{1,0:T(8,128)(2,1)S(1)} %get-tuple-element.83), channel_id=1, source_target_pairs={{0,3},{1,0},{2,1},{3,2},{4,7},{5,4},{6,5},{7,6},{8,11},{9,8},{10,9... | collective-permute-start | bytes 1585160 | tf_op jit(solution)/shard_map/ppermute | solution.py:123
  200.7 11.3 %all-to-all-start.2 = ((f32[32,1,330]{2,1,0:T(1,128)}), f32[32,1,330]{2,1,0:T(1,128)S(1)}, u32[]{:S(2)}, u32[]{:S(2)}) async-start(f32[32,1,330]{2,1,0:T(1,128)} %reshape.445), calls=%async_computation.2 | async-start | bytes 98304 | tf_op jit(solution)/shard_map/all_to_all | solution.py:208

commit v8 on v7

--- a/solution.py
+++ b/solution.py
@@ -46,7 +46,8 @@
         out_ref[:, j * IMG:(j + 1) * IMG] = rolled_sum(y, rows, offsets, j)
 
 
-def last_sums_kernel(offsets, rows, chunk, w_ref, x_ref, acc_ref, tail_ref, out_ref, moved_ref):
+def last_sums_kernel(offsets, rows, chunk, w_ref, x_ref, acc_ref, tail_ref, *refs):
+    out_refs, moved_ref = refs[:-1], refs[-1]
     k = pl.program_id(0)
     n = x_ref.shape[0]
     x = x_ref[:, pl.ds(k * chunk, chunk)]
@@ -59,9 +60,11 @@
         else:
             moved_ref[u * n:(u + 1) * n, :] = x
     total = acc_ref[...] + jnp.dot(w_ref[...], moved_ref[...], preferred_element_type=jnp.float32)
-    out_ref[:, pl.ds(k * chunk, chunk)] = total.astype(out_ref.dtype)
-    pixels = out_ref.shape[1] - tail_ref.shape[1]
-    out_ref[:, pixels:] = tail_ref[...]
+    group = rows // len(out_refs)
+    for q, out_ref in enumerate(out_refs):
+        pixels = out_ref.shape[1] - tail_ref.shape[1]
+        out_ref[:, pl.ds(k * chunk, chunk)] = total[q * group:(q + 1) * group].astype(out_ref.dtype)
+        out_ref[:, pixels:] = tail_ref[q * group:(q + 1) * group]
 
 
 def first_sums(w, x, offsets, pixels):
@@ -84,8 +87,9 @@
     )(w, x)
 
 
-def last_sums(w, x, acc, tail, offsets, pixels):
+def last_sums(w, x, acc, tail, offsets, pixels, blocks):
     rows = acc.shape[0]
+    group = rows // blocks
     chunk = min(CHUNK, pixels)
     width = pixels + tail.shape[1]
     n = x.shape[0]
@@ -99,8 +103,8 @@
             pl.BlockSpec((rows, chunk), lambda k: (0, k)),
             pl.BlockSpec(tail.shape, lambda k: (0, 0)),
         ],
-        out_specs=pl.BlockSpec((rows, width), lambda k: (0, 0)),
-        out_shape=jax.ShapeDtypeStruct((rows, width), jnp.bfloat16),
+        out_specs=[pl.BlockSpec((group, width), lambda k: (0, 0)) for _ in range(blocks)],
+        out_shape=[jax.ShapeDtypeStruct((group, width), jnp.bfloat16) for _ in range(blocks)],
         scratch_shapes=[pltpu.VMEM((len(offsets) * n, chunk), x.dtype)],
         cost_estimate=pl.CostEstimate(
             flops=2 * w.shape[0] * pixels * n,
@@ -196,12 +200,21 @@
         post = jnp.concatenate([class_post, loglike[:, None]], axis=1)
         return low, totals, post
 
+    order = (ref_here + jnp.arange(count_ref, dtype=jnp.int32)) % count_ref
+
+    def rotate_rows(values, lead):
+        shape = values.shape
+        grouped = values.reshape((lead, count_ref, -1) + shape[1:])
+        return jnp.take(grouped, order, axis=1).reshape(shape)
+
     low_a, tot_a, post_a = part(got_a)
+    low_a = rotate_rows(low_a, SHIFTS)
     sums_a = first_sums(low_a, got_a, offsets, pixels)
     post_width = post_a.shape[1]
     back = [post_a.reshape(count_dom, rows_a, post_width)]
     if rows_b:
         low_b, tot_b, post_b = part(got_b)
+        low_b = rotate_rows(low_b, SHIFTS)
         tot_a = tot_a + tot_b
         back.append(post_b.reshape(count_dom, rows_b, post_width))
     back = jnp.concatenate(back, axis=1)
@@ -210,21 +223,18 @@
     if not rows_b:
         low_b = jnp.zeros((SHIFTS * rows, 8), jnp.bfloat16)
         got_b = jnp.zeros((8, width), particles.dtype)
-    pieces = split_bf16(tot_a)
+    tot_a = rotate_rows(tot_a, 1)
     tail = jnp.zeros((rows, IMG), jnp.bfloat16)
-    for q, piece in enumerate(pieces):
+    for q, piece in enumerate(split_bf16(tot_a)):
         tail = tail.at[:, q].set(piece)
-    image_sums = last_sums(low_b, got_b, sums_a, tail, offsets, pixels)
-    partial = image_sums.reshape(count_ref, rows // count_ref, pixels + IMG)
-    pieces = [lax.dynamic_index_in_dim(partial, ref_here, 0, keepdims=False)]
-    for k in range(1, count_ref):
-        outgoing = lax.dynamic_index_in_dim(partial, (ref_here + k) % count_ref, 0, keepdims=False)
-        pieces.append(ahead(outgoing, "ref", k))
-    got_partial = jnp.stack(pieces).astype(f32)
-    class_sums = jnp.sum(got_partial[:, :, :pixels], axis=0).astype(jnp.bfloat16)
-    class_sums = class_sums.reshape(projections.shape)
-    got_tot = got_partial[:, :, pixels] + got_partial[:, :, pixels + 1] + got_partial[:, :, pixels + 2]
-    weight_totals = jnp.sum(got_tot, axis=0).reshape(projections.shape[0], projections.shape[1])
+    outgoing = last_sums(low_b, got_b, sums_a, tail, offsets, pixels, count_ref)
+    pieces = [outgoing[0]] + [ahead(outgoing[k], "ref", k) for k in range(1, count_ref)]
+    class_sums = sum(piece[:, :pixels].reshape(projections.shape).astype(f32) for piece in pieces)
+    class_sums = class_sums.astype(jnp.bfloat16)
+    weight_totals = sum(
+        piece[:, pixels].astype(f32) + piece[:, pixels + 1].astype(f32) + piece[:, pixels + 2].astype(f32)
+        for piece in pieces
+    ).reshape(projections.shape[0], projections.shape[1])
 
     mine = got_back[owners * capacity + slot_rank]
     class_prob = mine[:, : post_width - 1]

time: 228 us -> 223 us (0.978)
  other arithmetic: 24.8 us -> 20.9 us
    reduce_sum x2 -> x0, other arithmetic: 2.68 us -> none  [the longest x1 2.49 us: shards(): jnp.sum(got_partial[:, :, :pixels], axis=0).astype(jnp.bfloat16)]
    dynamic_slice x1 -> x0, local copies, waits for them, and re-layouts: 2.65 us -> none  [shards(): pieces = [lax.dynamic_index_in_dim(partial, ref_here, 0, keepdims=False)]]
    convert_element_type x1 -> x0, other arithmetic: 2.31 us -> none  [shards(): got_partial = jnp.stack(pieces).astype(f32)]
  transfers between devices with their start and end apart: 9 -> 9, of which waited for: 6 -> 6; matrix products, arithmetic and copies ran while one was open for 19% -> 20% of each run, Pallas kernels for 4% -> 4%
where the time goes in v8:
time: 223 us; the launch traced here: 222 us
  waiting for transfers between devices  99.2 us (44%)
  local copies, waits for them, and re-layouts  28.4 us (13%)
  starting transfers between devices  27.3 us (12%)
  matrix products  26.8 us (12%)
  other arithmetic  20.9 us (9%)
  Pallas kernels  17.8 us (8%)
    all_to_all x1, waiting for transfers between devices, shards(): lax.all_to_all(send_a, 'dom', 0, 0, tiled=True)  75 us
    ppermute x6, waiting for transfers between devices, ahead(): lax.ppermute(block, axis, [(i, (i + distance) % size) for i in range(size)])  14.2 us
    dot_general x2, matrix products, part(): lax.dot_general(received[:, :pixels], shifted, (((1,), (1,)), ((), ())),...  11.4 us
    ppermute x6, starting transfers between devices, ahead(): lax.ppermute(block, axis, [(i, (i + distance) % size) for i in range(size)])  10.4 us
    pallas_call x1, Pallas kernels, first_sums(): pl.pallas_call(functools.partial(first_sums_kernel, tuple(offsets), rows)...  9.22 us
    dot_general x1, matrix products, shards(): jnp.dot(pick_a.astype(particles.dtype), carried, preferred_element_type=f32)  9.13 us
    pallas_call x1, Pallas kernels, last_sums(): pl.pallas_call(functools.partial(last_sums_kernel, tuple(offsets), rows,...  8.58 us
    select_n x1, other arithmetic, translate(): return jnp.where(keep, near, far)  7.89 us
  transfers between devices with their start and end apart: 9, of which 6 were waited for; matrix products, arithmetic and copies ran while one was open for 20% of the time, Pallas kernels for 4%

profile of v8, /device:TPU:0, one launch (start us, length us, event | category | flops | bytes accessed | tf_op | source)
XLA Modules:
  0.0 221.6 jit_solution(9448475474940926516)
XLA Ops:
  0.7 0.9 convert_reduce_fusion
  1.6 1.2 reshape.555
  2.8 0.7 compare_select_fusion
  3.5 0.8 select_convert_fusion
  4.4 9.1 %fusion = bf16[32,8,16512]{2,1,0:T(8,128)(2,1)} fusion(bf16[256,128]{1,0:T(8,128)(2,1)S(1)} %select_convert_fusion, bf16[256,16384]{1,0:T(8,128)(2,1)} %param.12, s32[256]{0:T(256)S(1)} %get-tuple-element.112), kind=kOutput, calls=%fused_computation.5 | convolution fusion | flops 2185461760 | bytes 16909312 | tf_op jit(solution)/shard_map/dot_general | solution.py:156
  13.5 2.0 collective-permute-start
  15.5 3.6 %collective-permute-start.1 = (bf16[16,16384]{1,0:T(8,128)(2,1)S(1)}, bf16[16,16384]{1,0:T(8,128)(2,1)}, u32[]{:S(2)}, u32[]{:S(2)}) collective-permute-start(bf16[16,16384]{1,0:T(8,128)(2,1)S(1)} %reshape.555), channel_id=1, source_target_pairs={{0,2},{1,3},{2,0},{3,1},{4,6},{5,7},{6,4},{7,5},{8,10},{9,11},{10,... | collective-permute-start | bytes 1572872 | tf_op jit(solution)/shard_map/ppermute | solution.py:127
  19.1 1.0 collective-permute-start.2
  20.1 7.4 %all-to-all-start = ((bf16[32,8,16512]{2,1,0:T(8,128)(2,1)}), bf16[32,8,16512]{2,1,0:T(8,128)(2,1)}, u32[]{:S(2)}, u32[]{:S(2)}) async-start(bf16[32,8,16512]{2,1,0:T(8,128)(2,1)} %fusion), calls=%async_computation | async-start | bytes 16908288 | tf_op jit(solution)/shard_map/all_to_all | solution.py:158
  27.7 0.6 compare_reduce_fusion.1
  28.3 0.6 compare_reduce_fusion.2
  28.9 0.7 compare_reduce_fusion
  30.4 1.1 bitcast_dynamic-update-slice_fusion.2
  31.5 10.5 %collective-permute-done.1 = bf16[16,16384]{1,0:T(8,128)(2,1)} collective-permute-done((bf16[16,16384]{1,0:T(8,128)(2,1)S(1)}, bf16[16,16384]{1,0:T(8,128)(2,1)}, u32[]{:S(2)}, u32[]{:S(2)}) %collective-permute-start.1) | collective-permute-done | bytes 524320 | tf_op jit(solution)/shard_map/ppermute | solution.py:127
  42.1 1.1 bitcast_dynamic-update-slice_fusion.1
  43.2 6.3 %convolution_convert_fusion.1 = bf16[64,16512]{1,0:T(8,128)(2,1)} fusion(pred[64,256]{1,0:T(32,128)(4,1)S(1)} %iota_compare_fusion.3, bf16[256,128]{1,0:T(8,128)(2,1)S(1)} %select_convert_fusion, bf16[256,16384]{1,0:T(8,128)(2,1)} %param.12), kind=kOutput, calls=%fused_computation.6 | convolution fusion | flops 559030272 | bytes 10584064 | tf_op jit(solution)/shard_map/dot_general | solution.py:170
  49.5 4.1 %reshape.557 = bf16[32,2,16512]{2,1,0:T(2,128)(2,1)} reshape(bf16[64,16512]{1,0:T(8,128)(2,1)} %convolution_convert_fusion.1) | data formatting | bytes 4227072 | tf_op jit(solution)/shard_map/reshape | solution.py:171
  53.8 2.8 %fusion.42 = (bf16[64,16383]{1,0:T(8,128)(2,1)}, bf16[64,16383]{1,0:T(8,128)(2,1)}) fusion(bf16[64,16384]{1,0:T(8,128)(2,1)S(1)} %bitcast.46), kind=kLoop, calls=%fused_computation.116 | loop fusion | bytes 8388096 | tf_op jit(solution)/shard_map/jit(_roll_static)/slice | solution.py:22
  56.6 2.7 %fusion.39 = (bf16[64,16257]{1,0:T(8,128)(2,1)}, bf16[64,16257]{1,0:T(8,128)(2,1)}) fusion(bf16[64,16384]{1,0:T(8,128)(2,1)S(1)} %bitcast.47), kind=kLoop, calls=%fused_computation.113 | loop fusion | bytes 8323584 | tf_op jit(solution)/shard_map/jit(_roll_static)/slice | solution.py:24
  59.3 75.0 %all-to-all-done = bf16[32,8,16512]{2,1,0:T(8,128)(2,1)} async-done(((bf16[32,8,16512]{2,1,0:T(8,128)(2,1)}), bf16[32,8,16512]{2,1,0:T(8,128)(2,1)}, u32[]{:S(2)}, u32[]{:S(2)}) %all-to-all-start) | async-done | bytes 8454176 | tf_op jit(solution)/shard_map/all_to_all | solution.py:158
  134.3 5.0 %all-to-all-start.1 = ((bf16[32,2,16512]{2,1,0:T(2,128)(2,1)}), bf16[32,2,16512]{2,1,0:T(2,128)(2,1)}, u32[]{:S(2)}, u32[]{:S(2)}) async-start(bf16[32,2,16512]{2,1,0:T(2,128)(2,1)} %reshape.557), calls=%async_computation.1 | async-start | bytes 4227072 | tf_op jit(solution)/shard_map/all_to_all | solution.py:173
  139.3 7.9 %fusion.3 = (bf16[64,16384]{1,0:T(8,128)(2,1)}, bf16[64,16384]{1,0:T(8,128)(2,1)}) fusion(bf16[64,16383]{1,0:T(8,128)(2,1)} %get-tuple-element.100, bf16[64,1]{1,0:T(8,128)(2,1)S(1)} %get-tuple-element.98, bf16[64,127]{1,0:T(8,128)(2,1)S(1)} %get-tuple-element.96, bf16[64,16257]{1,0:T(8,128)(2,1)} %get-tuple-element.94, s32[16384]{0:T(1024)S(1)} %get-tuple-element.121, ...), kind=kLoop, calls=%fused_computation.14 | loop fusion | flops 22020096 | bytes 12730368 | tf_op jit(solution)/shard_map/jit(_where)/select_n | solution.py:30
  147.9 1.4 convert_reduce_fusion.1
  149.4 6.3 %fusion.37 = (f32[256]{0:T(256)S(1)}, f32[256,192]{0,1:T(8,128)S(1)}, f32[256,192]{0,1:T(8,128)S(1)}) fusion(f32[256,64]{0,1:T(8,128)S(1)} %tile.17, f32[192]{0:T(256)S(1)} %sub.182, f32[256]{0:T(256)S(1)} %get-tuple-element.86, bf16[64,16384]{1,0:T(8,128)(2,1)} %get-tuple-element.105, bf16[64,16384]{1,0:T(8,128)(2,1)S(1)} %bitcast.49, ...), kind=kOutput, calls=%fused_computation.111 | convolution fusion | flops 1629732608 | bytes 15141632 | tf_op jit(solution)/shard_map/dot_general | solution.py:187
  156.7 0.7 bitcast_select_fusion.w_ref
  157.5 9.2 %shard_map.93.acc_ref = f32[64,16384]{1,0:T(8,128)} custom-call(bf16[192,256]{1,0:T(8,128)(2,1)} %bitcast_select_fusion.w_ref, bf16[256,16512]{1,0:T(8,128)(2,1)} %bitcast.1.x_ref), custom_call_target="tpu_custom_call" | custom-call | flops 1610612736 | bytes 12681216 | tf_op jit(solution)/shard_map/pallas_call | solution.py:73
  166.7 2.6 %all-to-all-done.1 = bf16[32,2,16512]{2,1,0:T(2,128)(2,1)} async-done(((bf16[32,2,16512]{2,1,0:T(2,128)(2,1)}), bf16[32,2,16512]{2,1,0:T(2,128)(2,1)}, u32[]{:S(2)}, u32[]{:S(2)}) %all-to-all-start.1) | async-done | bytes 2113568 | tf_op jit(solution)/shard_map/all_to_all | solution.py:173
  169.3 4.1 %reshape.558.x_ref = bf16[64,16512]{1,0:T(8,128)(2,1)} reshape(bf16[32,2,16512]{2,1,0:T(2,128)(2,1)} %all-to-all-done.1) | data formatting | bytes 4227072 | tf_op jit(solution)/shard_map/reshape | solution.py:173
  173.4 1.0 convert_reduce_fusion.2
  174.6 5.1 %fusion.38 = (f32[64]{0:T(128)S(1)}, f32[64,192]{1,0:T(8,128)S(1)}, f32[64,192]{1,0:T(8,128)S(1)}) fusion(f32[64,192]{1,0:T(8,128)S(1)} %copy.88, f32[192]{0:T(256)S(1)} %sub.182, f32[64]{0:T(128)S(1)} %get-tuple-element.88, bf16[64,16384]{1,0:T(8,128)(2,1)} %get-tuple-element.105, bf16[64,16384]{1,0:T(8,128)(2,1)S(1)} %bitcast.50, ...), kind=kOutput, calls=%fused_computation.112 | convolution fusion | flops 421588928 | bytes 8537344 | tf_op jit(solution)/shard_map/dot_general | solution.py:187
  180.9 1.3 fusion.26
  183.1 0.7 copy.97.w_ref
  184.0 0.8 fusion.27
  184.9 0.6 copy-done.1
  185.5 8.6 %shard_map.94 = (bf16[16,16512]{1,0:T(8,128)(2,1)}, bf16[16,16512]{1,0:T(8,128)(2,1)}, bf16[16,16512]{1,0:T(8,128)(2,1)}, bf16[16,16512]{1,0:T(8,128)(2,1)}) custom-call(bf16[64,192]{1,0:T(8,128)(2,1)} %copy.97.w_ref, bf16[64,16512]{1,0:T(8,128)(2,1)} %reshape.558.x_ref, f32[64,16384]{1,0:T(8,128)} %shard_map.93.acc_ref, bf16[64,128]{1,0:T(8,128)(2,1)} %copy-done.1), custom_call_target="tpu_custom_call" | custom-call | flops 402653184 | bytes 8445952 | tf_op jit(solution)/shard_map/pallas_call | solution.py:97
  194.1 1.0 collective-permute-start.3
  195.5 2.3 %collective-permute-start.5 = (bf16[16,16512]{1,0:T(8,128)(2,1)}, bf16[16,16512]{1,0:T(8,128)(2,1)S(1)}, u32[]{:S(2)}, u32[]{:S(2)}) collective-permute-start(bf16[16,16512]{1,0:T(8,128)(2,1)} %get-tuple-element.57), channel_id=1, source_target_pairs={{0,3},{1,0},{2,1},{3,2},{4,7},{5,4},{6,5},{7,6},{8,11},{9,8},{10,9... | collective-permute-start | bytes 1585160 | tf_op jit(solution)/shard_map/ppermute | solution.py:127
  199.3 0.8 reshape.610
  200.1 4.6 %all-to-all-start.2 = ((f32[32,1,330]{2,1,0:T(1,128)}), f32[32,1,330]{2,1,0:T(1,128)S(1)}, u32[]{:S(2)}, u32[]{:S(2)}) async-start(f32[32,1,330]{2,1,0:T(1,128)} %reshape.610), calls=%async_computation.2 | async-start | bytes 98304 | tf_op jit(solution)/shard_map/all_to_all | solution.py:221
  204.6 7.4 %all-to-all-done.2 = f32[32,1,330]{2,1,0:T(1,128)S(1)} async-done(((f32[32,1,330]{2,1,0:T(1,128)}), f32[32,1,330]{2,1,0:T(1,128)S(1)}, u32[]{:S(2)}, u32[]{:S(2)}) %all-to-all-start.2) | async-done | bytes 42272 | tf_op jit(solution)/shard_map/all_to_all | solution.py:221
  212.6 0.8 reduce.44
  213.5 0.7 gather_fusion
  214.2 0.7 copy.98
  214.9 0.7 slice_reduce_fusion
  215.7 3.0 %collective-permute-done.3 = bf16[16,16512]{1,0:T(8,128)(2,1)S(1)} collective-permute-done((bf16[16,16512]{1,0:T(8,128)(2,1)}, bf16[16,16512]{1,0:T(8,128)(2,1)S(1)}, u32[]{:S(2)}, u32[]{:S(2)}) %collective-permute-start.3) | collective-permute-done | bytes 528416 | tf_op jit(solution)/shard_map/ppermute | solution.py:127
  218.7 0.6 collective-permute-done.5
  219.6 0.7 copy.99
  220.5 1.1 add.366
  (83 shorter events, 8.3 us)
Async XLA Ops:
  13.5 16.1 %copy-start.2 = (s32[2]{0:T(128)S(1)}, s32[2]{0:T(128)}, u32[]{:S(2)}) copy-start(s32[2]{0:T(128)} %param.17) | copy-start | bytes 28
  13.5 16.9 %collective-permute-start = (bf16[16,16384]{1,0:T(8,128)(2,1)S(1)}, bf16[16,16384]{1,0:T(8,128)(2,1)}, u32[]{:S(2)}, u32[]{:S(2)}) collective-permute-start(bf16[16,16384]{1,0:T(8,128)(2,1)S(1)} %reshape.555), channel_id=1, source_target_pairs={{0,1},{1,2},{2,3},{3,0},{4,5},{5,6},{6,7},{7,4},{8,9},{9,10},{10,1... | collective-permute-start | bytes 1572872 | tf_op jit(solution)/shard_map/ppermute | solution.py:127
  15.5 26.6 %collective-permute-start.1 = (bf16[16,16384]{1,0:T(8,128)(2,1)S(1)}, bf16[16,16384]{1,0:T(8,128)(2,1)}, u32[]{:S(2)}, u32[]{:S(2)}) collective-permute-start(bf16[16,16384]{1,0:T(8,128)(2,1)S(1)} %reshape.555), channel_id=1, source_target_pairs={{0,2},{1,3},{2,0},{3,1},{4,6},{5,7},{6,4},{7,5},{8,10},{9,11},{10,... | collective-permute-start | bytes 1572872 | tf_op jit(solution)/shard_map/ppermute | solution.py:127
  19.1 24.1 %collective-permute-start.2 = (bf16[16,16384]{1,0:T(8,128)(2,1)S(1)}, bf16[16,16384]{1,0:T(8,128)(2,1)S(1)}, u32[]{:S(2)}, u32[]{:S(2)}) collective-permute-start(bf16[16,16384]{1,0:T(8,128)(2,1)S(1)} %reshape.555), channel_id=1, source_target_pairs={{0,3},{1,0},{2,1},{3,2},{4,7},{5,4},{6,5},{7,6},{8,11},{9,8},{10,9... | collective-permute-start | bytes 1572872 | tf_op jit(solution)/shard_map/ppermute | solution.py:127
  20.1 114.2 %all-to-all-start = ((bf16[32,8,16512]{2,1,0:T(8,128)(2,1)}), bf16[32,8,16512]{2,1,0:T(8,128)(2,1)}, u32[]{:S(2)}, u32[]{:S(2)}) async-start(bf16[32,8,16512]{2,1,0:T(8,128)(2,1)} %fusion), calls=%async_computation | async-start | bytes 16908288 | tf_op jit(solution)/shard_map/all_to_all | solution.py:158
  134.3 35.0 %all-to-all-start.1 = ((bf16[32,2,16512]{2,1,0:T(2,128)(2,1)}), bf16[32,2,16512]{2,1,0:T(2,128)(2,1)}, u32[]{:S(2)}, u32[]{:S(2)}) async-start(bf16[32,2,16512]{2,1,0:T(2,128)(2,1)} %reshape.557), calls=%async_computation.1 | async-start | bytes 4227072 | tf_op jit(solution)/shard_map/all_to_all | solution.py:173
  184.9 0.6 copy-start.1
  194.1 25.3 %copy-start = (bf16[16,16512]{1,0:T(8,128)(2,1)S(1)}, bf16[16,16512]{1,0:T(8,128)(2,1)}, u32[]{:S(2)}) copy-start(bf16[16,16512]{1,0:T(8,128)(2,1)} %get-tuple-element.54) | copy-start | bytes 1585156
  194.1 24.6 %collective-permute-start.3 = (bf16[16,16512]{1,0:T(8,128)(2,1)}, bf16[16,16512]{1,0:T(8,128)(2,1)S(1)}, u32[]{:S(2)}, u32[]{:S(2)}) collective-permute-start(bf16[16,16512]{1,0:T(8,128)(2,1)} %get-tuple-element.55), channel_id=1, source_target_pairs={{0,1},{1,2},{2,3},{3,0},{4,5},{5,6},{6,7},{7,4},{8,9},{9,10},{10,1... | collective-permute-start | bytes 1585160 | tf_op jit(solution)/shard_map/ppermute | solution.py:127
  195.1 23.6 %collective-permute-start.4 = (bf16[16,16512]{1,0:T(8,128)(2,1)}, bf16[16,16512]{1,0:T(8,128)(2,1)S(1)}, u32[]{:S(2)}, u32[]{:S(2)}) collective-permute-start(bf16[16,16512]{1,0:T(8,128)(2,1)} %get-tuple-element.56), channel_id=1, source_target_pairs={{0,2},{1,3},{2,0},{3,1},{4,6},{5,7},{6,4},{7,5},{8,10},{9,11},{10,... | collective-permute-start | bytes 1585160 | tf_op jit(solution)/shard_map/ppermute | solution.py:127
  195.5 23.8 %collective-permute-start.5 = (bf16[16,16512]{1,0:T(8,128)(2,1)}, bf16[16,16512]{1,0:T(8,128)(2,1)S(1)}, u32[]{:S(2)}, u32[]{:S(2)}) collective-permute-start(bf16[16,16512]{1,0:T(8,128)(2,1)} %get-tuple-element.57), channel_id=1, source_target_pairs={{0,3},{1,0},{2,1},{3,2},{4,7},{5,4},{6,5},{7,6},{8,11},{9,8},{10,9... | collective-permute-start | bytes 1585160 | tf_op jit(solution)/shard_map/ppermute | solution.py:127
  200.1 12.0 %all-to-all-start.2 = ((f32[32,1,330]{2,1,0:T(1,128)}), f32[32,1,330]{2,1,0:T(1,128)S(1)}, u32[]{:S(2)}, u32[]{:S(2)}) async-start(f32[32,1,330]{2,1,0:T(1,128)} %reshape.610), calls=%async_computation.2 | async-start | bytes 98304 | tf_op jit(solution)/shard_map/all_to_all | solution.py:221

commit v9 on v8

--- a/solution.py
+++ b/solution.py
@@ -50,7 +50,7 @@
     out_refs, moved_ref = refs[:-1], refs[-1]
     k = pl.program_id(0)
     n = x_ref.shape[0]
-    x = x_ref[:, pl.ds(k * chunk, chunk)]
+    x = x_ref[...]
     wide = x.astype(jnp.float32)
     for u, t in enumerate(offsets):
         if t % IMG:
@@ -99,7 +99,7 @@
         grid=(pixels // chunk,),
         in_specs=[
             pl.BlockSpec(stacked_w.shape, lambda k: (0, 0)),
-            pl.BlockSpec(x.shape, lambda k: (0, 0)),
+            pl.BlockSpec((n, chunk), lambda k: (0, k)),
             pl.BlockSpec((rows, chunk), lambda k: (0, k)),
             pl.BlockSpec(tail.shape, lambda k: (0, 0)),
         ],

time: 223 us -> 223 us (level)
  no operation moved by 1% of the time
where the time goes in v9:
time: 223 us; the launch traced here: 221 us
  waiting for transfers between devices  99.2 us (44%)
  local copies, waits for them, and re-layouts  28.4 us (13%)
  starting transfers between devices  27.3 us (12%)
  matrix products  26.8 us (12%)
  other arithmetic  20.9 us (9%)
  Pallas kernels  17.5 us (8%)
    all_to_all x1, waiting for transfers between devices, shards(): lax.all_to_all(send_a, 'dom', 0, 0, tiled=True)  75 us
    ppermute x6, waiting for transfers between devices, ahead(): lax.ppermute(block, axis, [(i, (i + distance) % size) for i in range(size)])  14.2 us
    dot_general x2, matrix products, part(): lax.dot_general(received[:, :pixels], shifted, (((1,), (1,)), ((), ())),...  11.4 us
    ppermute x6, starting transfers between devices, ahead(): lax.ppermute(block, axis, [(i, (i + distance) % size) for i in range(size)])  10.4 us
    pallas_call x1, Pallas kernels, first_sums(): pl.pallas_call(functools.partial(first_sums_kernel, tuple(offsets), rows)...  9.22 us
    dot_general x1, matrix products, shards(): jnp.dot(pick_a.astype(particles.dtype), carried, preferred_element_type=f32)  9.13 us
    pallas_call x1, Pallas kernels, last_sums(): pl.pallas_call(functools.partial(last_sums_kernel, tuple(offsets), rows,...  8.25 us
    select_n x1, other arithmetic, translate(): return jnp.where(keep, near, far)  7.89 us
  transfers between devices with their start and end apart: 9, of which 6 were waited for; matrix products, arithmetic and copies ran while one was open for 20% of the time, Pallas kernels for 4%

profile of v9, /device:TPU:0, one launch (start us, length us, event | category | flops | bytes accessed | tf_op | source)
XLA Modules:
  0.0 221.3 jit_solution(14662074291830547819)
XLA Ops:
  0.7 0.9 convert_reduce_fusion
  1.6 1.2 reshape.555
  2.8 0.7 compare_select_fusion
  3.5 0.8 select_convert_fusion
  4.4 9.1 %fusion = bf16[32,8,16512]{2,1,0:T(8,128)(2,1)} fusion(bf16[256,128]{1,0:T(8,128)(2,1)S(1)} %select_convert_fusion, bf16[256,16384]{1,0:T(8,128)(2,1)} %param.12, s32[256]{0:T(256)S(1)} %get-tuple-element.112), kind=kOutput, calls=%fused_computation.5 | convolution fusion | flops 2185461760 | bytes 16909312 | tf_op jit(solution)/shard_map/dot_general | solution.py:156
  13.5 2.0 collective-permute-start
  15.5 3.6 %collective-permute-start.1 = (bf16[16,16384]{1,0:T(8,128)(2,1)S(1)}, bf16[16,16384]{1,0:T(8,128)(2,1)}, u32[]{:S(2)}, u32[]{:S(2)}) collective-permute-start(bf16[16,16384]{1,0:T(8,128)(2,1)S(1)} %reshape.555), channel_id=1, source_target_pairs={{0,2},{1,3},{2,0},{3,1},{4,6},{5,7},{6,4},{7,5},{8,10},{9,11},{10,... | collective-permute-start | bytes 1572872 | tf_op jit(solution)/shard_map/ppermute | solution.py:127
  19.1 1.0 collective-permute-start.2
  20.1 7.4 %all-to-all-start = ((bf16[32,8,16512]{2,1,0:T(8,128)(2,1)}), bf16[32,8,16512]{2,1,0:T(8,128)(2,1)}, u32[]{:S(2)}, u32[]{:S(2)}) async-start(bf16[32,8,16512]{2,1,0:T(8,128)(2,1)} %fusion), calls=%async_computation | async-start | bytes 16908288 | tf_op jit(solution)/shard_map/all_to_all | solution.py:158
  27.7 0.6 compare_reduce_fusion.1
  28.3 0.6 compare_reduce_fusion.2
  28.9 0.7 compare_reduce_fusion
  30.4 1.1 bitcast_dynamic-update-slice_fusion.2
  31.5 10.5 %collective-permute-done.1 = bf16[16,16384]{1,0:T(8,128)(2,1)} collective-permute-done((bf16[16,16384]{1,0:T(8,128)(2,1)S(1)}, bf16[16,16384]{1,0:T(8,128)(2,1)}, u32[]{:S(2)}, u32[]{:S(2)}) %collective-permute-start.1) | collective-permute-done | bytes 524320 | tf_op jit(solution)/shard_map/ppermute | solution.py:127
  42.1 1.1 bitcast_dynamic-update-slice_fusion.1
  43.2 6.3 %convolution_convert_fusion.1 = bf16[64,16512]{1,0:T(8,128)(2,1)} fusion(pred[64,256]{1,0:T(32,128)(4,1)S(1)} %iota_compare_fusion.3, bf16[256,128]{1,0:T(8,128)(2,1)S(1)} %select_convert_fusion, bf16[256,16384]{1,0:T(8,128)(2,1)} %param.12), kind=kOutput, calls=%fused_computation.6 | convolution fusion | flops 559030272 | bytes 10584064 | tf_op jit(solution)/shard_map/dot_general | solution.py:170
  49.5 4.1 %reshape.557 = bf16[32,2,16512]{2,1,0:T(2,128)(2,1)} reshape(bf16[64,16512]{1,0:T(8,128)(2,1)} %convolution_convert_fusion.1) | data formatting | bytes 4227072 | tf_op jit(solution)/shard_map/reshape | solution.py:171
  53.8 2.8 %fusion.42 = (bf16[64,16383]{1,0:T(8,128)(2,1)}, bf16[64,16383]{1,0:T(8,128)(2,1)}) fusion(bf16[64,16384]{1,0:T(8,128)(2,1)S(1)} %bitcast.46), kind=kLoop, calls=%fused_computation.116 | loop fusion | bytes 8388096 | tf_op jit(solution)/shard_map/jit(_roll_static)/slice | solution.py:22
  56.6 2.7 %fusion.39 = (bf16[64,16257]{1,0:T(8,128)(2,1)}, bf16[64,16257]{1,0:T(8,128)(2,1)}) fusion(bf16[64,16384]{1,0:T(8,128)(2,1)S(1)} %bitcast.47), kind=kLoop, calls=%fused_computation.113 | loop fusion | bytes 8323584 | tf_op jit(solution)/shard_map/jit(_roll_static)/slice | solution.py:24
  59.3 75.0 %all-to-all-done = bf16[32,8,16512]{2,1,0:T(8,128)(2,1)} async-done(((bf16[32,8,16512]{2,1,0:T(8,128)(2,1)}), bf16[32,8,16512]{2,1,0:T(8,128)(2,1)}, u32[]{:S(2)}, u32[]{:S(2)}) %all-to-all-start) | async-done | bytes 8454176 | tf_op jit(solution)/shard_map/all_to_all | solution.py:158
  134.3 5.0 %all-to-all-start.1 = ((bf16[32,2,16512]{2,1,0:T(2,128)(2,1)}), bf16[32,2,16512]{2,1,0:T(2,128)(2,1)}, u32[]{:S(2)}, u32[]{:S(2)}) async-start(bf16[32,2,16512]{2,1,0:T(2,128)(2,1)} %reshape.557), calls=%async_computation.1 | async-start | bytes 4227072 | tf_op jit(solution)/shard_map/all_to_all | solution.py:173
  139.3 7.9 %fusion.3 = (bf16[64,16384]{1,0:T(8,128)(2,1)}, bf16[64,16384]{1,0:T(8,128)(2,1)}) fusion(bf16[64,16383]{1,0:T(8,128)(2,1)} %get-tuple-element.100, bf16[64,1]{1,0:T(8,128)(2,1)S(1)} %get-tuple-element.98, bf16[64,127]{1,0:T(8,128)(2,1)S(1)} %get-tuple-element.96, bf16[64,16257]{1,0:T(8,128)(2,1)} %get-tuple-element.94, s32[16384]{0:T(1024)S(1)} %get-tuple-element.121, ...), kind=kLoop, calls=%fused_computation.14 | loop fusion | flops 22020096 | bytes 12730368 | tf_op jit(solution)/shard_map/jit(_where)/select_n | solution.py:30
  147.9 1.4 convert_reduce_fusion.1
  149.4 6.3 %fusion.37 = (f32[256]{0:T(256)S(1)}, f32[256,192]{0,1:T(8,128)S(1)}, f32[256,192]{0,1:T(8,128)S(1)}) fusion(f32[256,64]{0,1:T(8,128)S(1)} %tile.17, f32[192]{0:T(256)S(1)} %sub.182, f32[256]{0:T(256)S(1)} %get-tuple-element.86, bf16[64,16384]{1,0:T(8,128)(2,1)} %get-tuple-element.105, bf16[64,16384]{1,0:T(8,128)(2,1)S(1)} %bitcast.49, ...), kind=kOutput, calls=%fused_computation.111 | convolution fusion | flops 1629732608 | bytes 15141632 | tf_op jit(solution)/shard_map/dot_general | solution.py:187
  156.7 0.7 bitcast_select_fusion.w_ref
  157.5 9.2 %shard_map.93.acc_ref = f32[64,16384]{1,0:T(8,128)} custom-call(bf16[192,256]{1,0:T(8,128)(2,1)} %bitcast_select_fusion.w_ref, bf16[256,16512]{1,0:T(8,128)(2,1)} %bitcast.1.x_ref), custom_call_target="tpu_custom_call" | custom-call | flops 1610612736 | bytes 12681216 | tf_op jit(solution)/shard_map/pallas_call | solution.py:73
  166.7 2.6 %all-to-all-done.1 = bf16[32,2,16512]{2,1,0:T(2,128)(2,1)} async-done(((bf16[32,2,16512]{2,1,0:T(2,128)(2,1)}), bf16[32,2,16512]{2,1,0:T(2,128)(2,1)}, u32[]{:S(2)}, u32[]{:S(2)}) %all-to-all-start.1) | async-done | bytes 2113568 | tf_op jit(solution)/shard_map/all_to_all | solution.py:173
  169.3 4.1 %reshape.558.x_ref = bf16[64,16512]{1,0:T(8,128)(2,1)} reshape(bf16[32,2,16512]{2,1,0:T(2,128)(2,1)} %all-to-all-done.1) | data formatting | bytes 4227072 | tf_op jit(solution)/shard_map/reshape | solution.py:173
  173.4 1.0 convert_reduce_fusion.2
  174.6 5.1 %fusion.38 = (f32[64]{0:T(128)S(1)}, f32[64,192]{1,0:T(8,128)S(1)}, f32[64,192]{1,0:T(8,128)S(1)}) fusion(f32[64,192]{1,0:T(8,128)S(1)} %copy.88, f32[192]{0:T(256)S(1)} %sub.182, f32[64]{0:T(128)S(1)} %get-tuple-element.88, bf16[64,16384]{1,0:T(8,128)(2,1)} %get-tuple-element.105, bf16[64,16384]{1,0:T(8,128)(2,1)S(1)} %bitcast.50, ...), kind=kOutput, calls=%fused_computation.112 | convolution fusion | flops 421588928 | bytes 8537344 | tf_op jit(solution)/shard_map/dot_general | solution.py:187
  180.9 1.3 fusion.26
  183.1 0.7 copy.97.w_ref
  184.0 0.8 fusion.27
  184.9 0.6 copy-done.1
  185.5 8.2 %shard_map.94 = (bf16[16,16512]{1,0:T(8,128)(2,1)}, bf16[16,16512]{1,0:T(8,128)(2,1)}, bf16[16,16512]{1,0:T(8,128)(2,1)}, bf16[16,16512]{1,0:T(8,128)(2,1)}) custom-call(bf16[64,192]{1,0:T(8,128)(2,1)} %copy.97.w_ref, bf16[64,16512]{1,0:T(8,128)(2,1)} %reshape.558.x_ref, f32[64,16384]{1,0:T(8,128)} %shard_map.93.acc_ref, bf16[64,128]{1,0:T(8,128)(2,1)} %copy-done.1), custom_call_target="tpu_custom_call" | custom-call | flops 402653184 | bytes 8445952 | tf_op jit(solution)/shard_map/pallas_call | solution.py:97
  193.7 1.0 collective-permute-start.3
  195.2 2.3 %collective-permute-start.5 = (bf16[16,16512]{1,0:T(8,128)(2,1)}, bf16[16,16512]{1,0:T(8,128)(2,1)S(1)}, u32[]{:S(2)}, u32[]{:S(2)}) collective-permute-start(bf16[16,16512]{1,0:T(8,128)(2,1)} %get-tuple-element.57), channel_id=1, source_target_pairs={{0,3},{1,0},{2,1},{3,2},{4,7},{5,4},{6,5},{7,6},{8,11},{9,8},{10,9... | collective-permute-start | bytes 1585160 | tf_op jit(solution)/shard_map/ppermute | solution.py:127
  198.9 0.8 reshape.610
  199.7 4.6 %all-to-all-start.2 = ((f32[32,1,330]{2,1,0:T(1,128)}), f32[32,1,330]{2,1,0:T(1,128)S(1)}, u32[]{:S(2)}, u32[]{:S(2)}) async-start(f32[32,1,330]{2,1,0:T(1,128)} %reshape.610), calls=%async_computation.2 | async-start | bytes 98304 | tf_op jit(solution)/shard_map/all_to_all | solution.py:221
  204.3 7.4 %all-to-all-done.2 = f32[32,1,330]{2,1,0:T(1,128)S(1)} async-done(((f32[32,1,330]{2,1,0:T(1,128)}), f32[32,1,330]{2,1,0:T(1,128)S(1)}, u32[]{:S(2)}, u32[]{:S(2)}) %all-to-all-start.2) | async-done | bytes 42272 | tf_op jit(solution)/shard_map/all_to_all | solution.py:221
  212.2 0.8 reduce.44
  213.2 0.7 gather_fusion
  213.9 0.7 copy.98
  214.6 0.7 slice_reduce_fusion
  215.3 3.0 %collective-permute-done.3 = bf16[16,16512]{1,0:T(8,128)(2,1)S(1)} collective-permute-done((bf16[16,16512]{1,0:T(8,128)(2,1)}, bf16[16,16512]{1,0:T(8,128)(2,1)S(1)}, u32[]{:S(2)}, u32[]{:S(2)}) %collective-permute-start.3) | collective-permute-done | bytes 528416 | tf_op jit(solution)/shard_map/ppermute | solution.py:127
  218.4 0.6 collective-permute-done.5
  219.3 0.7 copy.99
  220.2 1.1 add.366
  (83 shorter events, 8.3 us)
Async XLA Ops:
  13.5 16.1 %copy-start.2 = (s32[2]{0:T(128)S(1)}, s32[2]{0:T(128)}, u32[]{:S(2)}) copy-start(s32[2]{0:T(128)} %param.17) | copy-start | bytes 28
  13.5 16.9 %collective-permute-start = (bf16[16,16384]{1,0:T(8,128)(2,1)S(1)}, bf16[16,16384]{1,0:T(8,128)(2,1)}, u32[]{:S(2)}, u32[]{:S(2)}) collective-permute-start(bf16[16,16384]{1,0:T(8,128)(2,1)S(1)} %reshape.555), channel_id=1, source_target_pairs={{0,1},{1,2},{2,3},{3,0},{4,5},{5,6},{6,7},{7,4},{8,9},{9,10},{10,1... | collective-permute-start | bytes 1572872 | tf_op jit(solution)/shard_map/ppermute | solution.py:127
  15.5 26.6 %collective-permute-start.1 = (bf16[16,16384]{1,0:T(8,128)(2,1)S(1)}, bf16[16,16384]{1,0:T(8,128)(2,1)}, u32[]{:S(2)}, u32[]{:S(2)}) collective-permute-start(bf16[16,16384]{1,0:T(8,128)(2,1)S(1)} %reshape.555), channel_id=1, source_target_pairs={{0,2},{1,3},{2,0},{3,1},{4,6},{5,7},{6,4},{7,5},{8,10},{9,11},{10,... | collective-permute-start | bytes 1572872 | tf_op jit(solution)/shard_map/ppermute | solution.py:127
  19.1 24.1 %collective-permute-start.2 = (bf16[16,16384]{1,0:T(8,128)(2,1)S(1)}, bf16[16,16384]{1,0:T(8,128)(2,1)S(1)}, u32[]{:S(2)}, u32[]{:S(2)}) collective-permute-start(bf16[16,16384]{1,0:T(8,128)(2,1)S(1)} %reshape.555), channel_id=1, source_target_pairs={{0,3},{1,0},{2,1},{3,2},{4,7},{5,4},{6,5},{7,6},{8,11},{9,8},{10,9... | collective-permute-start | bytes 1572872 | tf_op jit(solution)/shard_map/ppermute | solution.py:127
  20.1 114.2 %all-to-all-start = ((bf16[32,8,16512]{2,1,0:T(8,128)(2,1)}), bf16[32,8,16512]{2,1,0:T(8,128)(2,1)}, u32[]{:S(2)}, u32[]{:S(2)}) async-start(bf16[32,8,16512]{2,1,0:T(8,128)(2,1)} %fusion), calls=%async_computation | async-start | bytes 16908288 | tf_op jit(solution)/shard_map/all_to_all | solution.py:158
  134.3 35.0 %all-to-all-start.1 = ((bf16[32,2,16512]{2,1,0:T(2,128)(2,1)}), bf16[32,2,16512]{2,1,0:T(2,128)(2,1)}, u32[]{:S(2)}, u32[]{:S(2)}) async-start(bf16[32,2,16512]{2,1,0:T(2,128)(2,1)} %reshape.557), calls=%async_computation.1 | async-start | bytes 4227072 | tf_op jit(solution)/shard_map/all_to_all | solution.py:173
  184.9 0.6 copy-start.1
  193.7 25.3 %copy-start = (bf16[16,16512]{1,0:T(8,128)(2,1)S(1)}, bf16[16,16512]{1,0:T(8,128)(2,1)}, u32[]{:S(2)}) copy-start(bf16[16,16512]{1,0:T(8,128)(2,1)} %get-tuple-element.54) | copy-start | bytes 1585156
  193.7 24.6 %collective-permute-start.3 = (bf16[16,16512]{1,0:T(8,128)(2,1)}, bf16[16,16512]{1,0:T(8,128)(2,1)S(1)}, u32[]{:S(2)}, u32[]{:S(2)}) collective-permute-start(bf16[16,16512]{1,0:T(8,128)(2,1)} %get-tuple-element.55), channel_id=1, source_target_pairs={{0,1},{1,2},{2,3},{3,0},{4,5},{5,6},{6,7},{7,4},{8,9},{9,10},{10,1... | collective-permute-start | bytes 1585160 | tf_op jit(solution)/shard_map/ppermute | solution.py:127
  194.8 23.6 %collective-permute-start.4 = (bf16[16,16512]{1,0:T(8,128)(2,1)}, bf16[16,16512]{1,0:T(8,128)(2,1)S(1)}, u32[]{:S(2)}, u32[]{:S(2)}) collective-permute-start(bf16[16,16512]{1,0:T(8,128)(2,1)} %get-tuple-element.56), channel_id=1, source_target_pairs={{0,2},{1,3},{2,0},{3,1},{4,6},{5,7},{6,4},{7,5},{8,10},{9,11},{10,... | collective-permute-start | bytes 1585160 | tf_op jit(solution)/shard_map/ppermute | solution.py:127
  195.2 23.8 %collective-permute-start.5 = (bf16[16,16512]{1,0:T(8,128)(2,1)}, bf16[16,16512]{1,0:T(8,128)(2,1)S(1)}, u32[]{:S(2)}, u32[]{:S(2)}) collective-permute-start(bf16[16,16512]{1,0:T(8,128)(2,1)} %get-tuple-element.57), channel_id=1, source_target_pairs={{0,3},{1,0},{2,1},{3,2},{4,7},{5,4},{6,5},{7,6},{8,11},{9,8},{10,9... | collective-permute-start | bytes 1585160 | tf_op jit(solution)/shard_map/ppermute | solution.py:127
  199.7 12.0 %all-to-all-start.2 = ((f32[32,1,330]{2,1,0:T(1,128)}), f32[32,1,330]{2,1,0:T(1,128)S(1)}, u32[]{:S(2)}, u32[]{:S(2)}) async-start(f32[32,1,330]{2,1,0:T(1,128)} %reshape.610), calls=%async_computation.2 | async-start | bytes 98304 | tf_op jit(solution)/shard_map/all_to_all | solution.py:221

commit v10 on v9

--- a/solution.py
+++ b/solution.py
@@ -46,24 +46,18 @@
         out_ref[:, j * IMG:(j + 1) * IMG] = rolled_sum(y, rows, offsets, j)
 
 
-def last_sums_kernel(offsets, rows, chunk, w_ref, x_ref, acc_ref, tail_ref, *refs):
-    out_refs, moved_ref = refs[:-1], refs[-1]
+def last_sums_kernel(offsets, rows, chunk, w_ref, x_ref, acc_ref, tail_ref, *out_refs):
     k = pl.program_id(0)
-    n = x_ref.shape[0]
-    x = x_ref[...]
-    wide = x.astype(jnp.float32)
-    for u, t in enumerate(offsets):
-        if t % IMG:
-            for j in range(chunk // IMG):
-                piece = pltpu.roll(wide[:, j * IMG:(j + 1) * IMG], shift=t % IMG, axis=1)
-                moved_ref[u * n:(u + 1) * n, j * IMG:(j + 1) * IMG] = piece.astype(moved_ref.dtype)
-        else:
-            moved_ref[u * n:(u + 1) * n, :] = x
-    total = acc_ref[...] + jnp.dot(w_ref[...], moved_ref[...], preferred_element_type=jnp.float32)
+    y = jnp.dot(w_ref[...], x_ref[...], preferred_element_type=jnp.float32)
     group = rows // len(out_refs)
+    for j in range(chunk // IMG):
+        total = acc_ref[:, j * IMG:(j + 1) * IMG] + rolled_sum(y, rows, offsets, j)
+        for q, out_ref in enumerate(out_refs):
+            out_ref[:, pl.ds(k * chunk + j * IMG, IMG)] = total[q * group:(q + 1) * group].astype(
+                out_ref.dtype
+            )
     for q, out_ref in enumerate(out_refs):
         pixels = out_ref.shape[1] - tail_ref.shape[1]
-        out_ref[:, pl.ds(k * chunk, chunk)] = total[q * group:(q + 1) * group].astype(out_ref.dtype)
         out_ref[:, pixels:] = tail_ref[q * group:(q + 1) * group]
 
 
@@ -93,25 +87,23 @@
     chunk = min(CHUNK, pixels)
     width = pixels + tail.shape[1]
     n = x.shape[0]
-    stacked_w = w.reshape(len(offsets), rows, n).transpose(1, 0, 2).reshape(rows, len(offsets) * n)
     return pl.pallas_call(
         functools.partial(last_sums_kernel, tuple(offsets), rows, chunk),
         grid=(pixels // chunk,),
         in_specs=[
-            pl.BlockSpec(stacked_w.shape, lambda k: (0, 0)),
+            pl.BlockSpec(w.shape, lambda k: (0, 0)),
             pl.BlockSpec((n, chunk), lambda k: (0, k)),
             pl.BlockSpec((rows, chunk), lambda k: (0, k)),
             pl.BlockSpec(tail.shape, lambda k: (0, 0)),
         ],
         out_specs=[pl.BlockSpec((group, width), lambda k: (0, 0)) for _ in range(blocks)],
         out_shape=[jax.ShapeDtypeStruct((group, width), jnp.bfloat16) for _ in range(blocks)],
-        scratch_shapes=[pltpu.VMEM((len(offsets) * n, chunk), x.dtype)],
         cost_estimate=pl.CostEstimate(
             flops=2 * w.shape[0] * pixels * n,
             transcendentals=0,
-            bytes_accessed=2 * (n * width + w.size + rows * width) + 4 * rows * pixels,
+            bytes_accessed=2 * (n * pixels + w.size + rows * width) + 4 * rows * pixels,
         ),
-    )(stacked_w, x, acc, tail)
+    )(w, x, acc, tail)
 
 
 def split_bf16(values):
@@ -133,7 +125,7 @@
     count_ref = lax.axis_size("ref")
     arrived, pixels = particles.shape
     capacity = (5 * arrived + 4 * count_dom - 1) // (4 * count_dom)
-    rows_a = min(FIRST_ROWS, capacity)
+    rows_a = min(FIRST_ROWS, capacity - 1)
     rows_b = capacity - rows_a
 
     earlier = jnp.arange(arrived)[:, None] > jnp.arange(arrived)[None, :]
@@ -152,11 +144,11 @@
     carried = jnp.concatenate([particles, extra.astype(particles.dtype)], axis=1)
     width = pixels + IMG
 
-    pick_a = pick(jnp.where(in_a, owners * rows_a + slot_rank, -1), count_dom * rows_a)
-    send_a = jnp.dot(pick_a.astype(particles.dtype), carried, preferred_element_type=f32)
-    send_a = send_a.astype(particles.dtype).reshape(count_dom, rows_a, width)
-    got_a = lax.all_to_all(send_a, "dom", 0, 0, tiled=True).reshape(count_dom * rows_a, width)
-    _, own_proj = lax.optimization_barrier((send_a, projections.reshape(-1, pixels)))
+    pick_b = pick(jnp.where(in_a, -1, owners * rows_b + slot_rank - rows_a), count_dom * rows_b)
+    send_b = jnp.dot(pick_b.astype(particles.dtype), carried, preferred_element_type=f32)
+    send_b = send_b.astype(particles.dtype).reshape(count_dom, rows_b, width)
+    got_b = lax.all_to_all(send_b, "dom", 0, 0, tiled=True).reshape(count_dom * rows_b, width)
+    _, own_proj = lax.optimization_barrier((send_b, projections.reshape(-1, pixels)))
     ref_here = lax.axis_index("ref")
     blocks = jnp.zeros((count_ref,) + own_proj.shape, own_proj.dtype)
     blocks = lax.dynamic_update_index_in_dim(blocks, own_proj, ref_here, 0)
@@ -164,13 +156,12 @@
         moved = ahead(own_proj, "ref", k)
         blocks = lax.dynamic_update_index_in_dim(blocks, moved, (ref_here - k) % count_ref, 0)
     all_proj = blocks.reshape(-1, pixels)
-    if rows_b:
-        pick_b = pick(jnp.where(in_a, -1, owners * rows_b + slot_rank - rows_a), count_dom * rows_b)
-        all_proj, pick_b = lax.optimization_barrier((all_proj, pick_b))
-        send_b = jnp.dot(pick_b.astype(particles.dtype), carried, preferred_element_type=f32)
-        send_b = send_b.astype(particles.dtype).reshape(count_dom, rows_b, width)
-        got_a, send_b = lax.optimization_barrier((got_a, send_b))
-        got_b = lax.all_to_all(send_b, "dom", 0, 0, tiled=True).reshape(count_dom * rows_b, width)
+    pick_a = pick(jnp.where(in_a, owners * rows_a + slot_rank, -1), count_dom * rows_a)
+    all_proj, pick_a = lax.optimization_barrier((all_proj, pick_a))
+    send_a = jnp.dot(pick_a.astype(particles.dtype), carried, preferred_element_type=f32)
+    send_a = send_a.astype(particles.dtype).reshape(count_dom, rows_a, width)
+    got_b, send_a = lax.optimization_barrier((got_b, send_a))
+    got_a = lax.all_to_all(send_a, "dom", 0, 0, tiled=True).reshape(count_dom * rows_a, width)
 
     rows = all_proj.shape[0]
     offsets = [u - SHIFTS // 2 for u in range(SHIFTS)]
@@ -207,27 +198,22 @@
         grouped = values.reshape((lead, count_ref, -1) + shape[1:])
         return jnp.take(grouped, order, axis=1).reshape(shape)
 
+    low_b, tot_b, post_b = part(got_b)
+    sums_b = first_sums(rotate_rows(low_b, SHIFTS), got_b, offsets, pixels)
     low_a, tot_a, post_a = part(got_a)
     low_a = rotate_rows(low_a, SHIFTS)
-    sums_a = first_sums(low_a, got_a, offsets, pixels)
     post_width = post_a.shape[1]
-    back = [post_a.reshape(count_dom, rows_a, post_width)]
-    if rows_b:
-        low_b, tot_b, post_b = part(got_b)
-        low_b = rotate_rows(low_b, SHIFTS)
-        tot_a = tot_a + tot_b
-        back.append(post_b.reshape(count_dom, rows_b, post_width))
-    back = jnp.concatenate(back, axis=1)
+    back = jnp.concatenate(
+        [post_a.reshape(count_dom, rows_a, post_width), post_b.reshape(count_dom, rows_b, post_width)],
+        axis=1,
+    )
     got_back = lax.all_to_all(back, "dom", 0, 0, tiled=True).reshape(count_dom * capacity, post_width)
 
-    if not rows_b:
-        low_b = jnp.zeros((SHIFTS * rows, 8), jnp.bfloat16)
-        got_b = jnp.zeros((8, width), particles.dtype)
-    tot_a = rotate_rows(tot_a, 1)
+    totals = rotate_rows(tot_a + tot_b, 1)
     tail = jnp.zeros((rows, IMG), jnp.bfloat16)
-    for q, piece in enumerate(split_bf16(tot_a)):
+    for q, piece in enumerate(split_bf16(totals)):
         tail = tail.at[:, q].set(piece)
-    outgoing = last_sums(low_b, got_b, sums_a, tail, offsets, pixels, count_ref)
+    outgoing = last_sums(low_a, got_a, sums_b, tail, offsets, pixels, count_ref)
     pieces = [outgoing[0]] + [ahead(outgoing[k], "ref", k) for k in range(1, count_ref)]
     class_sums = sum(piece[:, :pixels].reshape(projections.shape).astype(f32) for piece in pieces)
     class_sums = class_sums.astype(jnp.bfloat16)

time: 223 us -> 229 us (1.027)
  waiting for transfers between devices: 99.2 us -> 113 us
  local copies, waits for them, and re-layouts: 28.4 us -> 24 us
    ppermute x6, waiting for transfers between devices: 14.2 us -> 23.3 us  [ahead(): lax.ppermute(block, axis, [(i, (i + distance) % size) for i in range(size)])]
    all_to_all x1, waiting for transfers between devices: 75 us -> 82.4 us  [shards(): lax.all_to_all(send_a, 'dom', 0, 0, tiled=True)]
    all_to_all x1, waiting for transfers between devices: 2.6 us -> 0.01 us  [shards(): lax.all_to_all(send_b, 'dom', 0, 0, tiled=True)]
    all_to_all x1, starting transfers between devices: 4.97 us -> 7.52 us  [shards(): lax.all_to_all(send_b, 'dom', 0, 0, tiled=True)]
  transfers between devices with their start and end apart: 9 -> 9, of which waited for: 6 -> 5; matrix products, arithmetic and copies ran while one was open for 20% -> 17% of each run, Pallas kernels for 4% -> 3%
where the time goes in v10:
time: 229 us; the launch traced here: 228 us
  waiting for transfers between devices  113 us (49%)
  starting transfers between devices  27.5 us (12%)
  matrix products  25.3 us (11%)
  local copies, waits for them, and re-layouts  24 us (10%)
  other arithmetic  19.3 us (8%)
  Pallas kernels  17.6 us (8%)
    all_to_all x1, waiting for transfers between devices, shards(): lax.all_to_all(send_a, 'dom', 0, 0, tiled=True)  82.4 us
    ppermute x6, waiting for transfers between devices, ahead(): lax.ppermute(block, axis, [(i, (i + distance) % size) for i in range(size)])  23.3 us
    dot_general x2, matrix products, part(): lax.dot_general(received[:, :pixels], shifted, (((1,), (1,)), ((), ())),...  11.4 us
    pallas_call x1, Pallas kernels, last_sums(): pl.pallas_call(functools.partial(last_sums_kernel, tuple(offsets), rows,...  9.89 us
    dot_general x1, matrix products, shards(): jnp.dot(pick_a.astype(particles.dtype), carried, preferred_element_type=f32)  9.01 us
    ppermute x6, starting transfers between devices, ahead(): lax.ppermute(block, axis, [(i, (i + distance) % size) for i in range(size)])  8.6 us
    pallas_call x1, Pallas kernels, first_sums(): pl.pallas_call(functools.partial(first_sums_kernel, tuple(offsets), rows)...  7.73 us
    all_to_all x1, starting transfers between devices, shards(): lax.all_to_all(send_a, 'dom', 0, 0, tiled=True)  7.55 us
  transfers between devices with their start and end apart: 9, of which 5 were waited for; matrix products, arithmetic and copies ran while one was open for 17% of the time, Pallas kernels for 3%

profile of v10, /device:TPU:0, one launch (start us, length us, event | category | flops | bytes accessed | tf_op | source)
XLA Modules:
  0.0 228.0 jit_solution(9230584608944267544)
XLA Ops:
  0.7 0.9 convert_reduce_fusion
  1.6 0.7 compare_select_fusion
  2.3 0.8 select_convert_fusion
  3.1 5.0 %convolution_convert_fusion.1 = bf16[64,16512]{1,0:T(8,128)(2,1)S(1)} fusion(bf16[256,128]{1,0:T(8,128)(2,1)S(1)} %select_convert_fusion, bf16[256,16384]{1,0:T(8,128)(2,1)} %param.12, s32[256]{0:T(256)S(1)} %get-tuple-element.108), kind=kOutput, calls=%fused_computation.6 | convolution fusion | flops 559046656 | bytes 10568704 | tf_op jit(solution)/shard_map/dot_general | solution.py:148
  8.1 2.2 reshape.551
  10.4 7.5 %all-to-all-start = ((bf16[32,2,16512]{2,1,0:T(2,128)(2,1)}), bf16[32,2,16512]{2,1,0:T(2,128)(2,1)}, u32[]{:S(2)}, u32[]{:S(2)}) async-start(bf16[32,2,16512]{2,1,0:T(2,128)(2,1)} %reshape.551), calls=%async_computation | async-start | bytes 4227072 | tf_op jit(solution)/shard_map/all_to_all | solution.py:150
  18.1 4.1 %collective-permute-start.2 = (bf16[16,16384]{1,0:T(8,128)(2,1)S(1)}, bf16[16,16384]{1,0:T(8,128)(2,1)S(1)}, u32[]{:S(2)}, u32[]{:S(2)}) collective-permute-start(bf16[16,16384]{1,0:T(8,128)(2,1)S(1)} %reshape.553), channel_id=1, source_target_pairs={{0,3},{1,0},{2,1},{3,2},{4,7},{5,4},{6,5},{7,6},{8,11},{9,8},{10,9... | collective-permute-start | bytes 1572872 | tf_op jit(solution)/shard_map/ppermute | solution.py:119
  22.2 1.3 collective-permute-start
  23.5 0.6 compare_reduce_fusion.2
  24.1 0.6 compare_reduce_fusion.1
  24.8 0.6 compare_reduce_fusion
  26.1 22.4 %collective-permute-done = bf16[16,16384]{1,0:T(8,128)(2,1)} collective-permute-done((bf16[16,16384]{1,0:T(8,128)(2,1)S(1)}, bf16[16,16384]{1,0:T(8,128)(2,1)}, u32[]{:S(2)}, u32[]{:S(2)}) %collective-permute-start) | collective-permute-done | bytes 524320 | tf_op jit(solution)/shard_map/ppermute | solution.py:119
  48.5 1.1 bitcast_dynamic-update-slice_fusion.2
  49.6 1.1 bitcast_dynamic-update-slice_fusion.1
  50.8 2.7 %fusion.39 = (bf16[64,16257]{1,0:T(8,128)(2,1)}, bf16[64,16257]{1,0:T(8,128)(2,1)}) fusion(bf16[64,16384]{1,0:T(8,128)(2,1)S(1)} %bitcast.42), kind=kLoop, calls=%fused_computation.113 | loop fusion | bytes 8323584 | tf_op jit(solution)/shard_map/jit(_roll_static)/slice | solution.py:24
  54.3 9.0 %fusion = bf16[32,8,16512]{2,1,0:T(8,128)(2,1)} fusion(pred[256,256]{1,0:T(32,128)(4,1)S(1)} %iota_compare_fusion, bf16[256,128]{1,0:T(8,128)(2,1)S(1)} %select_convert_fusion, bf16[256,16384]{1,0:T(8,128)(2,1)} %param.12), kind=kOutput, calls=%fused_computation.5 | convolution fusion | flops 2185396224 | bytes 16973824 | tf_op jit(solution)/shard_map/dot_general | solution.py:161
  63.4 4.1 %reshape.552.x_ref = bf16[64,16512]{1,0:T(8,128)(2,1)} reshape(bf16[32,2,16512]{2,1,0:T(2,128)(2,1)} %all-to-all-done) | data formatting | bytes 4227072 | tf_op jit(solution)/shard_map/reshape | solution.py:150
  67.5 7.6 %all-to-all-start.1 = ((bf16[32,8,16512]{2,1,0:T(8,128)(2,1)}), bf16[32,8,16512]{2,1,0:T(8,128)(2,1)}, u32[]{:S(2)}, u32[]{:S(2)}) async-start(bf16[32,8,16512]{2,1,0:T(8,128)(2,1)} %fusion), calls=%async_computation.1 | async-start | bytes 16908288 | tf_op jit(solution)/shard_map/all_to_all | solution.py:164
  75.1 0.7 fusion.42
  75.8 0.8 copy-done
  76.6 0.6 copy-done.1
  77.3 6.0 %fusion.3 = (bf16[64,16384]{1,0:T(8,128)(2,1)}, bf16[64,16384]{1,0:T(8,128)(2,1)}) fusion(bf16[64,16383]{1,0:T(8,128)(2,1)S(1)} %get-tuple-element.96, bf16[64,1]{1,0:T(8,128)(2,1)S(1)} %get-tuple-element.94, bf16[64,127]{1,0:T(8,128)(2,1)S(1)} %get-tuple-element.92, bf16[64,16257]{1,0:T(8,128)(2,1)S(1)} %copy-done, s32[16384]{0:T(1024)S(1)} %get-tuple-element.117, ...), kind=kLoop, calls=%fused_computation.14 | loop fusion | flops 22020096 | bytes 12730368 | tf_op jit(solution)/shard_map/jit(_where)/select_n | solution.py:30
  83.2 1.1 convert_reduce_fusion.2
  84.5 5.1 %fusion.38 = (f32[64]{0:T(128)S(1)}, f32[64,192]{1,0:T(8,128)S(1)}, f32[64,192]{1,0:T(8,128)S(1)}) fusion(f32[64,192]{1,0:T(8,128)S(1)} %copy.68, f32[192]{0:T(256)S(1)} %sub.182, f32[64]{0:T(128)S(1)} %get-tuple-element.84, bf16[64,16384]{1,0:T(8,128)(2,1)} %get-tuple-element.101, bf16[64,16384]{1,0:T(8,128)(2,1)S(1)} %bitcast.47, ...), kind=kOutput, calls=%fused_computation.112 | convolution fusion | flops 421588928 | bytes 8537344 | tf_op jit(solution)/shard_map/dot_general | solution.py:178
  90.2 0.6 gather_fusion.2
  90.8 0.7 bitcast_select_fusion.1.w_ref
  91.5 7.7 %shard_map.93.acc_ref = f32[64,16384]{1,0:T(8,128)} custom-call(bf16[192,64]{1,0:T(8,128)(2,1)} %bitcast_select_fusion.1.w_ref, bf16[64,16512]{1,0:T(8,128)(2,1)} %reshape.552.x_ref), custom_call_target="tpu_custom_call" | custom-call | flops 402653184 | bytes 6316032 | tf_op jit(solution)/shard_map/pallas_call | solution.py:67
  99.3 82.4 %all-to-all-done.1 = bf16[32,8,16512]{2,1,0:T(8,128)(2,1)} async-done(((bf16[32,8,16512]{2,1,0:T(8,128)(2,1)}), bf16[32,8,16512]{2,1,0:T(8,128)(2,1)}, u32[]{:S(2)}, u32[]{:S(2)}) %all-to-all-start.1) | async-done | bytes 8454176 | tf_op jit(solution)/shard_map/all_to_all | solution.py:164
  181.6 1.1 convert_reduce_fusion.1
  183.0 6.3 %fusion.37 = (f32[256]{0:T(256)S(1)}, f32[256,192]{0,1:T(8,128)S(1)}, f32[256,192]{0,1:T(8,128)S(1)}) fusion(f32[256,64]{0,1:T(8,128)S(1)} %tile.17, f32[192]{0:T(256)S(1)} %sub.182, f32[256]{0:T(256)S(1)} %get-tuple-element.82, bf16[64,16384]{1,0:T(8,128)(2,1)} %get-tuple-element.101, bf16[64,16384]{1,0:T(8,128)(2,1)S(1)} %bitcast.48, ...), kind=kOutput, calls=%fused_computation.111 | convolution fusion | flops 1629732608 | bytes 15141632 | tf_op jit(solution)/shard_map/dot_general | solution.py:178
  190.0 0.7 bitcast_select_fusion.w_ref
  190.9 0.6 gather_fusion.3
  191.6 1.3 fusion.26
  193.1 0.7 fusion.27
  193.9 0.6 copy-done.4
  194.5 9.9 %shard_map.94 = (bf16[16,16512]{1,0:T(8,128)(2,1)}, bf16[16,16512]{1,0:T(8,128)(2,1)}, bf16[16,16512]{1,0:T(8,128)(2,1)}, bf16[16,16512]{1,0:T(8,128)(2,1)}) custom-call(bf16[192,256]{1,0:T(8,128)(2,1)} %bitcast_select_fusion.w_ref, bf16[256,16512]{1,0:T(8,128)(2,1)} %bitcast.6.x_ref, f32[64,16384]{1,0:T(8,128)} %shard_map.93.acc_ref, bf16[64,128]{1,0:T(8,128)(2,1)} %copy-done.4), custom_call_target="tpu_custom_call" | custom-call | flops 1610612736 | bytes 14794752 | tf_op jit(solution)/shard_map/pallas_call | solution.py:90
  204.4 2.3 %collective-permute-start.4 = (bf16[16,16512]{1,0:T(8,128)(2,1)}, bf16[16,16512]{1,0:T(8,128)(2,1)S(1)}, u32[]{:S(2)}, u32[]{:S(2)}) collective-permute-start(bf16[16,16512]{1,0:T(8,128)(2,1)} %get-tuple-element.56), channel_id=1, source_target_pairs={{0,2},{1,3},{2,0},{3,1},{4,6},{5,7},{6,4},{7,5},{8,10},{9,11},{10,... | collective-permute-start | bytes 1585160 | tf_op jit(solution)/shard_map/ppermute | solution.py:119
  206.8 0.9 collective-permute-start.5
  209.1 0.8 reshape.607
  209.9 3.9 %all-to-all-start.2 = ((f32[32,1,330]{2,1,0:T(1,128)}), f32[32,1,330]{2,1,0:T(1,128)S(1)}, u32[]{:S(2)}, u32[]{:S(2)}) async-start(f32[32,1,330]{2,1,0:T(1,128)} %reshape.607), calls=%async_computation.2 | async-start | bytes 98304 | tf_op jit(solution)/shard_map/all_to_all | solution.py:210
  213.8 7.4 %all-to-all-done.2 = f32[32,1,330]{2,1,0:T(1,128)S(1)} async-done(((f32[32,1,330]{2,1,0:T(1,128)}), f32[32,1,330]{2,1,0:T(1,128)S(1)}, u32[]{:S(2)}, u32[]{:S(2)}) %all-to-all-start.2) | async-done | bytes 42272 | tf_op jit(solution)/shard_map/all_to_all | solution.py:210
  221.7 0.8 reduce.44
  222.6 0.7 gather_fusion
  223.4 0.7 copy.76
  224.1 0.7 slice_reduce_fusion
  225.0 0.7 collective-permute-done.5
  226.0 1.1 add.366
  227.4 0.6 copy.77
  (85 shorter events, 6.8 us)
Async XLA Ops:
  8.1 9.8 %copy-start.3 = (bf16[8,2,16384]{2,1,0:T(2,128)(2,1)S(1)}, bf16[8,2,16384]{2,1,0:T(2,128)(2,1)}, u32[]{:S(2)}) copy-start(bf16[8,2,16384]{2,1,0:T(2,128)(2,1)} %param.16) | copy-start | bytes 1572868
  8.1 17.3 %copy-start.5 = (s32[2]{0:T(128)S(1)}, s32[2]{0:T(128)}, u32[]{:S(2)}) copy-start(s32[2]{0:T(128)} %param.17) | copy-start | bytes 28
  10.4 53.0 %all-to-all-start = ((bf16[32,2,16512]{2,1,0:T(2,128)(2,1)}), bf16[32,2,16512]{2,1,0:T(2,128)(2,1)}, u32[]{:S(2)}, u32[]{:S(2)}) async-start(bf16[32,2,16512]{2,1,0:T(2,128)(2,1)} %reshape.551), calls=%async_computation | async-start | bytes 4227072 | tf_op jit(solution)/shard_map/all_to_all | solution.py:150
  18.1 32.6 %collective-permute-start.2 = (bf16[16,16384]{1,0:T(8,128)(2,1)S(1)}, bf16[16,16384]{1,0:T(8,128)(2,1)S(1)}, u32[]{:S(2)}, u32[]{:S(2)}) collective-permute-start(bf16[16,16384]{1,0:T(8,128)(2,1)S(1)} %reshape.553), channel_id=1, source_target_pairs={{0,3},{1,0},{2,1},{3,2},{4,7},{5,4},{6,5},{7,6},{8,11},{9,8},{10,9... | collective-permute-start | bytes 1572872 | tf_op jit(solution)/shard_map/ppermute | solution.py:119
  22.2 27.4 %collective-permute-start.1 = (bf16[16,16384]{1,0:T(8,128)(2,1)S(1)}, bf16[16,16384]{1,0:T(8,128)(2,1)}, u32[]{:S(2)}, u32[]{:S(2)}) collective-permute-start(bf16[16,16384]{1,0:T(8,128)(2,1)S(1)} %reshape.553), channel_id=1, source_target_pairs={{0,2},{1,3},{2,0},{3,1},{4,6},{5,7},{6,4},{7,5},{8,10},{9,11},{10,... | collective-permute-start | bytes 1572872 | tf_op jit(solution)/shard_map/ppermute | solution.py:119
  22.2 26.3 %collective-permute-start = (bf16[16,16384]{1,0:T(8,128)(2,1)S(1)}, bf16[16,16384]{1,0:T(8,128)(2,1)}, u32[]{:S(2)}, u32[]{:S(2)}) collective-permute-start(bf16[16,16384]{1,0:T(8,128)(2,1)S(1)} %reshape.553), channel_id=1, source_target_pairs={{0,1},{1,2},{2,3},{3,0},{4,5},{5,6},{6,7},{7,4},{8,9},{9,10},{10,1... | collective-permute-start | bytes 1572872 | tf_op jit(solution)/shard_map/ppermute | solution.py:119
  67.5 114.2 %all-to-all-start.1 = ((bf16[32,8,16512]{2,1,0:T(8,128)(2,1)}), bf16[32,8,16512]{2,1,0:T(8,128)(2,1)}, u32[]{:S(2)}, u32[]{:S(2)}) async-start(bf16[32,8,16512]{2,1,0:T(8,128)(2,1)} %fusion), calls=%async_computation.1 | async-start | bytes 16908288 | tf_op jit(solution)/shard_map/all_to_all | solution.py:164
  75.0 1.6 copy-start
  75.0 2.2 copy-start.1
  193.9 0.6 copy-start.4
  204.4 21.3 %copy-start.2 = (bf16[16,16512]{1,0:T(8,128)(2,1)S(1)}, bf16[16,16512]{1,0:T(8,128)(2,1)}, u32[]{:S(2)}) copy-start(bf16[16,16512]{1,0:T(8,128)(2,1)} %get-tuple-element.54) | copy-start | bytes 1585156
  204.4 20.6 %collective-permute-start.3 = (bf16[16,16512]{1,0:T(8,128)(2,1)}, bf16[16,16512]{1,0:T(8,128)(2,1)S(1)}, u32[]{:S(2)}, u32[]{:S(2)}) collective-permute-start(bf16[16,16512]{1,0:T(8,128)(2,1)} %get-tuple-element.55), channel_id=1, source_target_pairs={{0,1},{1,2},{2,3},{3,0},{4,5},{5,6},{6,7},{7,4},{8,9},{9,10},{10,1... | collective-permute-start | bytes 1585160 | tf_op jit(solution)/shard_map/ppermute | solution.py:119
  204.4 20.6 %collective-permute-start.4 = (bf16[16,16512]{1,0:T(8,128)(2,1)}, bf16[16,16512]{1,0:T(8,128)(2,1)S(1)}, u32[]{:S(2)}, u32[]{:S(2)}) collective-permute-start(bf16[16,16512]{1,0:T(8,128)(2,1)} %get-tuple-element.56), channel_id=1, source_target_pairs={{0,2},{1,3},{2,0},{3,1},{4,6},{5,7},{6,4},{7,5},{8,10},{9,11},{10,... | collective-permute-start | bytes 1585160 | tf_op jit(solution)/shard_map/ppermute | solution.py:119
  206.8 18.9 %collective-permute-start.5 = (bf16[16,16512]{1,0:T(8,128)(2,1)}, bf16[16,16512]{1,0:T(8,128)(2,1)S(1)}, u32[]{:S(2)}, u32[]{:S(2)}) collective-permute-start(bf16[16,16512]{1,0:T(8,128)(2,1)} %get-tuple-element.57), channel_id=1, source_target_pairs={{0,3},{1,0},{2,1},{3,2},{4,7},{5,4},{6,5},{7,6},{8,11},{9,8},{10,9... | collective-permute-start | bytes 1585160 | tf_op jit(solution)/shard_map/ppermute | solution.py:119
  209.9 11.3 %all-to-all-start.2 = ((f32[32,1,330]{2,1,0:T(1,128)}), f32[32,1,330]{2,1,0:T(1,128)S(1)}, u32[]{:S(2)}, u32[]{:S(2)}) async-start(f32[32,1,330]{2,1,0:T(1,128)} %reshape.607), calls=%async_computation.2 | async-start | bytes 98304 | tf_op jit(solution)/shard_map/all_to_all | solution.py:210

commit v11 on v9

--- a/solution.py
+++ b/solution.py
@@ -11,7 +11,7 @@
 SHIFTS = 3
 PRIOR_WIDTH = 576
 FIRST_ROWS = 8
-CHUNK = 2048
+CHUNK = 4096
 
 
 def translate(images, offset):

time: 223 us -> 220 us (0.987)
  Pallas kernels: 17.5 us -> 13.6 us
  waiting for transfers between devices: 99.2 us -> 102 us
  transfers between devices with their start and end apart: 9 -> 9, of which waited for: 6 -> 6; matrix products, arithmetic and copies ran while one was open for 20% -> 20% of each run, Pallas kernels for 4% -> 3%
where the time goes in v11:
time: 220 us; the launch traced here: 219 us
  waiting for transfers between devices  102 us (46%)
  local copies, waits for them, and re-layouts  28.4 us (13%)
  matrix products  26.8 us (12%)
  starting transfers between devices  26.6 us (12%)
  other arithmetic  20.9 us (10%)
  Pallas kernels  13.6 us (6%)
    all_to_all x1, waiting for transfers between devices, shards(): lax.all_to_all(send_a, 'dom', 0, 0, tiled=True)  75 us
    ppermute x6, waiting for transfers between devices, ahead(): lax.ppermute(block, axis, [(i, (i + distance) % size) for i in range(size)])  14.9 us
    dot_general x2, matrix products, part(): lax.dot_general(received[:, :pixels], shifted, (((1,), (1,)), ((), ())),...  11.4 us
    ppermute x6, starting transfers between devices, ahead(): lax.ppermute(block, axis, [(i, (i + distance) % size) for i in range(size)])  10.4 us
    dot_general x1, matrix products, shards(): jnp.dot(pick_a.astype(particles.dtype), carried, preferred_element_type=f32)  9.13 us
    select_n x1, other arithmetic, translate(): return jnp.where(keep, near, far)  7.89 us
    pallas_call x1, Pallas kernels, first_sums(): pl.pallas_call(functools.partial(first_sums_kernel, tuple(offsets), rows)...  7.49 us
    all_to_all x1, starting transfers between devices, shards(): lax.all_to_all(send_a, 'dom', 0, 0, tiled=True)  7.43 us
  transfers between devices with their start and end apart: 9, of which 6 were waited for; matrix products, arithmetic and copies ran while one was open for 20% of the time, Pallas kernels for 3%

profile of v11, /device:TPU:0, one launch (start us, length us, event | category | flops | bytes accessed | tf_op | source)
XLA Modules:
  0.0 219.1 jit_solution(11649872997612245256)
XLA Ops:
  0.7 0.9 convert_reduce_fusion
  1.6 1.2 reshape.555
  2.8 0.7 compare_select_fusion
  3.5 0.8 select_convert_fusion
  4.4 9.1 %fusion = bf16[32,8,16512]{2,1,0:T(8,128)(2,1)} fusion(bf16[256,128]{1,0:T(8,128)(2,1)S(1)} %select_convert_fusion, bf16[256,16384]{1,0:T(8,128)(2,1)} %param.12, s32[256]{0:T(256)S(1)} %get-tuple-element.112), kind=kOutput, calls=%fused_computation.5 | convolution fusion | flops 2185461760 | bytes 16909312 | tf_op jit(solution)/shard_map/dot_general | solution.py:156
  13.5 2.0 collective-permute-start
  15.5 3.6 %collective-permute-start.1 = (bf16[16,16384]{1,0:T(8,128)(2,1)S(1)}, bf16[16,16384]{1,0:T(8,128)(2,1)}, u32[]{:S(2)}, u32[]{:S(2)}) collective-permute-start(bf16[16,16384]{1,0:T(8,128)(2,1)S(1)} %reshape.555), channel_id=1, source_target_pairs={{0,2},{1,3},{2,0},{3,1},{4,6},{5,7},{6,4},{7,5},{8,10},{9,11},{10,... | collective-permute-start | bytes 1572872 | tf_op jit(solution)/shard_map/ppermute | solution.py:127
  19.1 1.0 collective-permute-start.2
  20.1 7.4 %all-to-all-start = ((bf16[32,8,16512]{2,1,0:T(8,128)(2,1)}), bf16[32,8,16512]{2,1,0:T(8,128)(2,1)}, u32[]{:S(2)}, u32[]{:S(2)}) async-start(bf16[32,8,16512]{2,1,0:T(8,128)(2,1)} %fusion), calls=%async_computation | async-start | bytes 16908288 | tf_op jit(solution)/shard_map/all_to_all | solution.py:158
  27.7 0.6 compare_reduce_fusion.1
  28.3 0.6 compare_reduce_fusion.2
  28.9 0.7 compare_reduce_fusion
  30.4 1.1 bitcast_dynamic-update-slice_fusion.2
  31.5 10.5 %collective-permute-done.1 = bf16[16,16384]{1,0:T(8,128)(2,1)} collective-permute-done((bf16[16,16384]{1,0:T(8,128)(2,1)S(1)}, bf16[16,16384]{1,0:T(8,128)(2,1)}, u32[]{:S(2)}, u32[]{:S(2)}) %collective-permute-start.1) | collective-permute-done | bytes 524320 | tf_op jit(solution)/shard_map/ppermute | solution.py:127
  42.1 1.1 bitcast_dynamic-update-slice_fusion.1
  43.2 6.3 %convolution_convert_fusion.1 = bf16[64,16512]{1,0:T(8,128)(2,1)} fusion(pred[64,256]{1,0:T(32,128)(4,1)S(1)} %iota_compare_fusion.3, bf16[256,128]{1,0:T(8,128)(2,1)S(1)} %select_convert_fusion, bf16[256,16384]{1,0:T(8,128)(2,1)} %param.12), kind=kOutput, calls=%fused_computation.6 | convolution fusion | flops 559030272 | bytes 10584064 | tf_op jit(solution)/shard_map/dot_general | solution.py:170
  49.5 4.1 %reshape.557 = bf16[32,2,16512]{2,1,0:T(2,128)(2,1)} reshape(bf16[64,16512]{1,0:T(8,128)(2,1)} %convolution_convert_fusion.1) | data formatting | bytes 4227072 | tf_op jit(solution)/shard_map/reshape | solution.py:171
  53.8 2.8 %fusion.42 = (bf16[64,16383]{1,0:T(8,128)(2,1)}, bf16[64,16383]{1,0:T(8,128)(2,1)}) fusion(bf16[64,16384]{1,0:T(8,128)(2,1)S(1)} %bitcast.46), kind=kLoop, calls=%fused_computation.116 | loop fusion | bytes 8388096 | tf_op jit(solution)/shard_map/jit(_roll_static)/slice | solution.py:22
  56.6 2.7 %fusion.39 = (bf16[64,16257]{1,0:T(8,128)(2,1)}, bf16[64,16257]{1,0:T(8,128)(2,1)}) fusion(bf16[64,16384]{1,0:T(8,128)(2,1)S(1)} %bitcast.47), kind=kLoop, calls=%fused_computation.113 | loop fusion | bytes 8323584 | tf_op jit(solution)/shard_map/jit(_roll_static)/slice | solution.py:24
  59.3 75.0 %all-to-all-done = bf16[32,8,16512]{2,1,0:T(8,128)(2,1)} async-done(((bf16[32,8,16512]{2,1,0:T(8,128)(2,1)}), bf16[32,8,16512]{2,1,0:T(8,128)(2,1)}, u32[]{:S(2)}, u32[]{:S(2)}) %all-to-all-start) | async-done | bytes 8454176 | tf_op jit(solution)/shard_map/all_to_all | solution.py:158
  134.3 5.0 %all-to-all-start.1 = ((bf16[32,2,16512]{2,1,0:T(2,128)(2,1)}), bf16[32,2,16512]{2,1,0:T(2,128)(2,1)}, u32[]{:S(2)}, u32[]{:S(2)}) async-start(bf16[32,2,16512]{2,1,0:T(2,128)(2,1)} %reshape.557), calls=%async_computation.1 | async-start | bytes 4227072 | tf_op jit(solution)/shard_map/all_to_all | solution.py:173
  139.3 7.9 %fusion.3 = (bf16[64,16384]{1,0:T(8,128)(2,1)}, bf16[64,16384]{1,0:T(8,128)(2,1)}) fusion(bf16[64,16383]{1,0:T(8,128)(2,1)} %get-tuple-element.100, bf16[64,1]{1,0:T(8,128)(2,1)S(1)} %get-tuple-element.98, bf16[64,127]{1,0:T(8,128)(2,1)S(1)} %get-tuple-element.96, bf16[64,16257]{1,0:T(8,128)(2,1)} %get-tuple-element.94, s32[16384]{0:T(1024)S(1)} %get-tuple-element.121, ...), kind=kLoop, calls=%fused_computation.14 | loop fusion | flops 22020096 | bytes 12730368 | tf_op jit(solution)/shard_map/jit(_where)/select_n | solution.py:30
  147.9 1.4 convert_reduce_fusion.1
  149.4 6.3 %fusion.37 = (f32[256]{0:T(256)S(1)}, f32[256,192]{0,1:T(8,128)S(1)}, f32[256,192]{0,1:T(8,128)S(1)}) fusion(f32[256,64]{0,1:T(8,128)S(1)} %tile.17, f32[192]{0:T(256)S(1)} %sub.182, f32[256]{0:T(256)S(1)} %get-tuple-element.86, bf16[64,16384]{1,0:T(8,128)(2,1)} %get-tuple-element.105, bf16[64,16384]{1,0:T(8,128)(2,1)S(1)} %bitcast.49, ...), kind=kOutput, calls=%fused_computation.111 | convolution fusion | flops 1629732608 | bytes 15141632 | tf_op jit(solution)/shard_map/dot_general | solution.py:187
  156.7 0.7 bitcast_select_fusion.w_ref
  157.5 7.5 %shard_map.93.acc_ref = f32[64,16384]{1,0:T(8,128)} custom-call(bf16[192,256]{1,0:T(8,128)(2,1)} %bitcast_select_fusion.w_ref, bf16[256,16512]{1,0:T(8,128)(2,1)} %bitcast.1.x_ref), custom_call_target="tpu_custom_call" | custom-call | flops 1610612736 | bytes 12681216 | tf_op jit(solution)/shard_map/pallas_call | solution.py:73
  165.0 4.3 %all-to-all-done.1 = bf16[32,2,16512]{2,1,0:T(2,128)(2,1)} async-done(((bf16[32,2,16512]{2,1,0:T(2,128)(2,1)}), bf16[32,2,16512]{2,1,0:T(2,128)(2,1)}, u32[]{:S(2)}, u32[]{:S(2)}) %all-to-all-start.1) | async-done | bytes 2113568 | tf_op jit(solution)/shard_map/all_to_all | solution.py:173
  169.3 4.1 %reshape.558.x_ref = bf16[64,16512]{1,0:T(8,128)(2,1)} reshape(bf16[32,2,16512]{2,1,0:T(2,128)(2,1)} %all-to-all-done.1) | data formatting | bytes 4227072 | tf_op jit(solution)/shard_map/reshape | solution.py:173
  173.4 1.0 convert_reduce_fusion.2
  174.6 5.1 %fusion.38 = (f32[64]{0:T(128)S(1)}, f32[64,192]{1,0:T(8,128)S(1)}, f32[64,192]{1,0:T(8,128)S(1)}) fusion(f32[64,192]{1,0:T(8,128)S(1)} %copy.88, f32[192]{0:T(256)S(1)} %sub.182, f32[64]{0:T(128)S(1)} %get-tuple-element.88, bf16[64,16384]{1,0:T(8,128)(2,1)} %get-tuple-element.105, bf16[64,16384]{1,0:T(8,128)(2,1)S(1)} %bitcast.50, ...), kind=kOutput, calls=%fused_computation.112 | convolution fusion | flops 421588928 | bytes 8537344 | tf_op jit(solution)/shard_map/dot_general | solution.py:187
  180.9 1.3 fusion.26
  183.1 0.7 copy.97.w_ref
  184.0 0.8 fusion.27
  184.9 0.6 copy-done.1
  185.5 6.1 %shard_map.94 = (bf16[16,16512]{1,0:T(8,128)(2,1)}, bf16[16,16512]{1,0:T(8,128)(2,1)}, bf16[16,16512]{1,0:T(8,128)(2,1)}, bf16[16,16512]{1,0:T(8,128)(2,1)}) custom-call(bf16[64,192]{1,0:T(8,128)(2,1)} %copy.97.w_ref, bf16[64,16512]{1,0:T(8,128)(2,1)} %reshape.558.x_ref, f32[64,16384]{1,0:T(8,128)} %shard_map.93.acc_ref, bf16[64,128]{1,0:T(8,128)(2,1)} %copy-done.1), custom_call_target="tpu_custom_call" | custom-call | flops 402653184 | bytes 8445952 | tf_op jit(solution)/shard_map/pallas_call | solution.py:97
  191.6 1.0 collective-permute-start.3
  193.0 2.3 %collective-permute-start.5 = (bf16[16,16512]{1,0:T(8,128)(2,1)}, bf16[16,16512]{1,0:T(8,128)(2,1)S(1)}, u32[]{:S(2)}, u32[]{:S(2)}) collective-permute-start(bf16[16,16512]{1,0:T(8,128)(2,1)} %get-tuple-element.57), channel_id=1, source_target_pairs={{0,3},{1,0},{2,1},{3,2},{4,7},{5,4},{6,5},{7,6},{8,11},{9,8},{10,9... | collective-permute-start | bytes 1585160 | tf_op jit(solution)/shard_map/ppermute | solution.py:127
  196.8 0.8 reshape.610
  197.5 3.9 %all-to-all-start.2 = ((f32[32,1,330]{2,1,0:T(1,128)}), f32[32,1,330]{2,1,0:T(1,128)S(1)}, u32[]{:S(2)}, u32[]{:S(2)}) async-start(f32[32,1,330]{2,1,0:T(1,128)} %reshape.610), calls=%async_computation.2 | async-start | bytes 98304 | tf_op jit(solution)/shard_map/all_to_all | solution.py:221
  201.4 7.4 %all-to-all-done.2 = f32[32,1,330]{2,1,0:T(1,128)S(1)} async-done(((f32[32,1,330]{2,1,0:T(1,128)}), f32[32,1,330]{2,1,0:T(1,128)S(1)}, u32[]{:S(2)}, u32[]{:S(2)}) %all-to-all-start.2) | async-done | bytes 42272 | tf_op jit(solution)/shard_map/all_to_all | solution.py:221
  209.4 0.8 reduce.44
  210.3 0.7 gather_fusion
  211.0 0.7 copy.98
  211.7 0.7 slice_reduce_fusion
  212.5 3.7 %collective-permute-done.3 = bf16[16,16512]{1,0:T(8,128)(2,1)S(1)} collective-permute-done((bf16[16,16512]{1,0:T(8,128)(2,1)}, bf16[16,16512]{1,0:T(8,128)(2,1)S(1)}, u32[]{:S(2)}, u32[]{:S(2)}) %collective-permute-start.3) | collective-permute-done | bytes 528416 | tf_op jit(solution)/shard_map/ppermute | solution.py:127
  216.2 0.6 collective-permute-done.5
  217.1 0.7 copy.99
  218.0 1.1 add.366
  (83 shorter events, 8.3 us)
Async XLA Ops:
  13.5 16.1 %copy-start.2 = (s32[2]{0:T(128)S(1)}, s32[2]{0:T(128)}, u32[]{:S(2)}) copy-start(s32[2]{0:T(128)} %param.17) | copy-start | bytes 28
  13.5 16.9 %collective-permute-start = (bf16[16,16384]{1,0:T(8,128)(2,1)S(1)}, bf16[16,16384]{1,0:T(8,128)(2,1)}, u32[]{:S(2)}, u32[]{:S(2)}) collective-permute-start(bf16[16,16384]{1,0:T(8,128)(2,1)S(1)} %reshape.555), channel_id=1, source_target_pairs={{0,1},{1,2},{2,3},{3,0},{4,5},{5,6},{6,7},{7,4},{8,9},{9,10},{10,1... | collective-permute-start | bytes 1572872 | tf_op jit(solution)/shard_map/ppermute | solution.py:127
  15.5 26.6 %collective-permute-start.1 = (bf16[16,16384]{1,0:T(8,128)(2,1)S(1)}, bf16[16,16384]{1,0:T(8,128)(2,1)}, u32[]{:S(2)}, u32[]{:S(2)}) collective-permute-start(bf16[16,16384]{1,0:T(8,128)(2,1)S(1)} %reshape.555), channel_id=1, source_target_pairs={{0,2},{1,3},{2,0},{3,1},{4,6},{5,7},{6,4},{7,5},{8,10},{9,11},{10,... | collective-permute-start | bytes 1572872 | tf_op jit(solution)/shard_map/ppermute | solution.py:127
  19.1 24.1 %collective-permute-start.2 = (bf16[16,16384]{1,0:T(8,128)(2,1)S(1)}, bf16[16,16384]{1,0:T(8,128)(2,1)S(1)}, u32[]{:S(2)}, u32[]{:S(2)}) collective-permute-start(bf16[16,16384]{1,0:T(8,128)(2,1)S(1)} %reshape.555), channel_id=1, source_target_pairs={{0,3},{1,0},{2,1},{3,2},{4,7},{5,4},{6,5},{7,6},{8,11},{9,8},{10,9... | collective-permute-start | bytes 1572872 | tf_op jit(solution)/shard_map/ppermute | solution.py:127
  20.1 114.2 %all-to-all-start = ((bf16[32,8,16512]{2,1,0:T(8,128)(2,1)}), bf16[32,8,16512]{2,1,0:T(8,128)(2,1)}, u32[]{:S(2)}, u32[]{:S(2)}) async-start(bf16[32,8,16512]{2,1,0:T(8,128)(2,1)} %fusion), calls=%async_computation | async-start | bytes 16908288 | tf_op jit(solution)/shard_map/all_to_all | solution.py:158
  134.3 35.0 %all-to-all-start.1 = ((bf16[32,2,16512]{2,1,0:T(2,128)(2,1)}), bf16[32,2,16512]{2,1,0:T(2,128)(2,1)}, u32[]{:S(2)}, u32[]{:S(2)}) async-start(bf16[32,2,16512]{2,1,0:T(2,128)(2,1)} %reshape.557), calls=%async_computation.1 | async-start | bytes 4227072 | tf_op jit(solution)/shard_map/all_to_all | solution.py:173
  184.9 0.6 copy-start.1
  191.6 25.3 %copy-start = (bf16[16,16512]{1,0:T(8,128)(2,1)S(1)}, bf16[16,16512]{1,0:T(8,128)(2,1)}, u32[]{:S(2)}) copy-start(bf16[16,16512]{1,0:T(8,128)(2,1)} %get-tuple-element.54) | copy-start | bytes 1585156
  191.6 24.6 %collective-permute-start.3 = (bf16[16,16512]{1,0:T(8,128)(2,1)}, bf16[16,16512]{1,0:T(8,128)(2,1)S(1)}, u32[]{:S(2)}, u32[]{:S(2)}) collective-permute-start(bf16[16,16512]{1,0:T(8,128)(2,1)} %get-tuple-element.55), channel_id=1, source_target_pairs={{0,1},{1,2},{2,3},{3,0},{4,5},{5,6},{6,7},{7,4},{8,9},{9,10},{10,1... | collective-permute-start | bytes 1585160 | tf_op jit(solution)/shard_map/ppermute | solution.py:127
  192.6 23.6 %collective-permute-start.4 = (bf16[16,16512]{1,0:T(8,128)(2,1)}, bf16[16,16512]{1,0:T(8,128)(2,1)S(1)}, u32[]{:S(2)}, u32[]{:S(2)}) collective-permute-start(bf16[16,16512]{1,0:T(8,128)(2,1)} %get-tuple-element.56), channel_id=1, source_target_pairs={{0,2},{1,3},{2,0},{3,1},{4,6},{5,7},{6,4},{7,5},{8,10},{9,11},{10,... | collective-permute-start | bytes 1585160 | tf_op jit(solution)/shard_map/ppermute | solution.py:127
  193.0 23.8 %collective-permute-start.5 = (bf16[16,16512]{1,0:T(8,128)(2,1)}, bf16[16,16512]{1,0:T(8,128)(2,1)S(1)}, u32[]{:S(2)}, u32[]{:S(2)}) collective-permute-start(bf16[16,16512]{1,0:T(8,128)(2,1)} %get-tuple-element.57), channel_id=1, source_target_pairs={{0,3},{1,0},{2,1},{3,2},{4,7},{5,4},{6,5},{7,6},{8,11},{9,8},{10,9... | collective-permute-start | bytes 1585160 | tf_op jit(solution)/shard_map/ppermute | solution.py:127
  197.5 11.3 %all-to-all-start.2 = ((f32[32,1,330]{2,1,0:T(1,128)}), f32[32,1,330]{2,1,0:T(1,128)S(1)}, u32[]{:S(2)}, u32[]{:S(2)}) async-start(f32[32,1,330]{2,1,0:T(1,128)} %reshape.610), calls=%async_computation.2 | async-start | bytes 98304 | tf_op jit(solution)/shard_map/all_to_all | solution.py:221

commit v12 on v11

--- a/solution.py
+++ b/solution.py
@@ -11,7 +11,7 @@
 SHIFTS = 3
 PRIOR_WIDTH = 576
 FIRST_ROWS = 8
-CHUNK = 4096
+CHUNK = 8192
 
 
 def translate(images, offset):

time: 220 us -> 219 us (level)
  transfers between devices with their start and end apart: 9 -> 9, of which waited for: 6 -> 6; matrix products, arithmetic and copies ran while one was open for 20% -> 21% of each run, Pallas kernels for 3% -> 3%
where the time goes in v12:
time: 219 us; the launch traced here: 218 us
  waiting for transfers between devices  103 us (47%)
  local copies, waits for them, and re-layouts  28.4 us (13%)
  matrix products  26.8 us (12%)
  starting transfers between devices  26.6 us (12%)
  other arithmetic  20.9 us (10%)
  Pallas kernels  11.8 us (5%)
    all_to_all x1, waiting for transfers between devices, shards(): lax.all_to_all(send_a, 'dom', 0, 0, tiled=True)  75 us
    ppermute x6, waiting for transfers between devices, ahead(): lax.ppermute(block, axis, [(i, (i + distance) % size) for i in range(size)])  14.9 us
    dot_general x2, matrix products, part(): lax.dot_general(received[:, :pixels], shifted, (((1,), (1,)), ((), ())),...  11.4 us
    ppermute x6, starting transfers between devices, ahead(): lax.ppermute(block, axis, [(i, (i + distance) % size) for i in range(size)])  10.4 us
    dot_general x1, matrix products, shards(): jnp.dot(pick_a.astype(particles.dtype), carried, preferred_element_type=f32)  9.13 us
    select_n x1, other arithmetic, translate(): return jnp.where(keep, near, far)  7.89 us
    all_to_all x1, starting transfers between devices, shards(): lax.all_to_all(send_a, 'dom', 0, 0, tiled=True)  7.43 us
    all_to_all x1, waiting for transfers between devices, shards(): lax.all_to_all(back, 'dom', 0, 0, tiled=True)  7.43 us
  transfers between devices with their start and end apart: 9, of which 6 were waited for; matrix products, arithmetic and copies ran while one was open for 21% of the time, Pallas kernels for 3%

profile of v12, /device:TPU:0, one launch (start us, length us, event | category | flops | bytes accessed | tf_op | source)
XLA Modules:
  0.0 218.5 jit_solution(4954960427213889170)
XLA Ops:
  0.7 0.9 convert_reduce_fusion
  1.6 1.2 reshape.555
  2.8 0.7 compare_select_fusion
  3.5 0.8 select_convert_fusion
  4.4 9.1 %fusion = bf16[32,8,16512]{2,1,0:T(8,128)(2,1)} fusion(bf16[256,128]{1,0:T(8,128)(2,1)S(1)} %select_convert_fusion, bf16[256,16384]{1,0:T(8,128)(2,1)} %param.12, s32[256]{0:T(256)S(1)} %get-tuple-element.112), kind=kOutput, calls=%fused_computation.5 | convolution fusion | flops 2185461760 | bytes 16909312 | tf_op jit(solution)/shard_map/dot_general | solution.py:156
  13.5 2.0 collective-permute-start
  15.5 3.6 %collective-permute-start.1 = (bf16[16,16384]{1,0:T(8,128)(2,1)S(1)}, bf16[16,16384]{1,0:T(8,128)(2,1)}, u32[]{:S(2)}, u32[]{:S(2)}) collective-permute-start(bf16[16,16384]{1,0:T(8,128)(2,1)S(1)} %reshape.555), channel_id=1, source_target_pairs={{0,2},{1,3},{2,0},{3,1},{4,6},{5,7},{6,4},{7,5},{8,10},{9,11},{10,... | collective-permute-start | bytes 1572872 | tf_op jit(solution)/shard_map/ppermute | solution.py:127
  19.1 1.0 collective-permute-start.2
  20.1 7.4 %all-to-all-start = ((bf16[32,8,16512]{2,1,0:T(8,128)(2,1)}), bf16[32,8,16512]{2,1,0:T(8,128)(2,1)}, u32[]{:S(2)}, u32[]{:S(2)}) async-start(bf16[32,8,16512]{2,1,0:T(8,128)(2,1)} %fusion), calls=%async_computation | async-start | bytes 16908288 | tf_op jit(solution)/shard_map/all_to_all | solution.py:158
  27.7 0.6 compare_reduce_fusion.1
  28.3 0.6 compare_reduce_fusion.2
  28.9 0.7 compare_reduce_fusion
  30.4 1.1 bitcast_dynamic-update-slice_fusion.2
  31.5 10.5 %collective-permute-done.1 = bf16[16,16384]{1,0:T(8,128)(2,1)} collective-permute-done((bf16[16,16384]{1,0:T(8,128)(2,1)S(1)}, bf16[16,16384]{1,0:T(8,128)(2,1)}, u32[]{:S(2)}, u32[]{:S(2)}) %collective-permute-start.1) | collective-permute-done | bytes 524320 | tf_op jit(solution)/shard_map/ppermute | solution.py:127
  42.1 1.1 bitcast_dynamic-update-slice_fusion.1
  43.2 6.3 %convolution_convert_fusion.1 = bf16[64,16512]{1,0:T(8,128)(2,1)} fusion(pred[64,256]{1,0:T(32,128)(4,1)S(1)} %iota_compare_fusion.3, bf16[256,128]{1,0:T(8,128)(2,1)S(1)} %select_convert_fusion, bf16[256,16384]{1,0:T(8,128)(2,1)} %param.12), kind=kOutput, calls=%fused_computation.6 | convolution fusion | flops 559030272 | bytes 10584064 | tf_op jit(solution)/shard_map/dot_general | solution.py:170
  49.5 4.1 %reshape.557 = bf16[32,2,16512]{2,1,0:T(2,128)(2,1)} reshape(bf16[64,16512]{1,0:T(8,128)(2,1)} %convolution_convert_fusion.1) | data formatting | bytes 4227072 | tf_op jit(solution)/shard_map/reshape | solution.py:171
  53.8 2.8 %fusion.42 = (bf16[64,16383]{1,0:T(8,128)(2,1)}, bf16[64,16383]{1,0:T(8,128)(2,1)}) fusion(bf16[64,16384]{1,0:T(8,128)(2,1)S(1)} %bitcast.46), kind=kLoop, calls=%fused_computation.116 | loop fusion | bytes 8388096 | tf_op jit(solution)/shard_map/jit(_roll_static)/slice | solution.py:22
  56.6 2.7 %fusion.39 = (bf16[64,16257]{1,0:T(8,128)(2,1)}, bf16[64,16257]{1,0:T(8,128)(2,1)}) fusion(bf16[64,16384]{1,0:T(8,128)(2,1)S(1)} %bitcast.47), kind=kLoop, calls=%fused_computation.113 | loop fusion | bytes 8323584 | tf_op jit(solution)/shard_map/jit(_roll_static)/slice | solution.py:24
  59.3 75.0 %all-to-all-done = bf16[32,8,16512]{2,1,0:T(8,128)(2,1)} async-done(((bf16[32,8,16512]{2,1,0:T(8,128)(2,1)}), bf16[32,8,16512]{2,1,0:T(8,128)(2,1)}, u32[]{:S(2)}, u32[]{:S(2)}) %all-to-all-start) | async-done | bytes 8454176 | tf_op jit(solution)/shard_map/all_to_all | solution.py:158
  134.3 5.0 %all-to-all-start.1 = ((bf16[32,2,16512]{2,1,0:T(2,128)(2,1)}), bf16[32,2,16512]{2,1,0:T(2,128)(2,1)}, u32[]{:S(2)}, u32[]{:S(2)}) async-start(bf16[32,2,16512]{2,1,0:T(2,128)(2,1)} %reshape.557), calls=%async_computation.1 | async-start | bytes 4227072 | tf_op jit(solution)/shard_map/all_to_all | solution.py:173
  139.3 7.9 %fusion.3 = (bf16[64,16384]{1,0:T(8,128)(2,1)}, bf16[64,16384]{1,0:T(8,128)(2,1)}) fusion(bf16[64,16383]{1,0:T(8,128)(2,1)} %get-tuple-element.100, bf16[64,1]{1,0:T(8,128)(2,1)S(1)} %get-tuple-element.98, bf16[64,127]{1,0:T(8,128)(2,1)S(1)} %get-tuple-element.96, bf16[64,16257]{1,0:T(8,128)(2,1)} %get-tuple-element.94, s32[16384]{0:T(1024)S(1)} %get-tuple-element.121, ...), kind=kLoop, calls=%fused_computation.14 | loop fusion | flops 22020096 | bytes 12730368 | tf_op jit(solution)/shard_map/jit(_where)/select_n | solution.py:30
  147.9 1.4 convert_reduce_fusion.1
  149.4 6.3 %fusion.37 = (f32[256]{0:T(256)S(1)}, f32[256,192]{0,1:T(8,128)S(1)}, f32[256,192]{0,1:T(8,128)S(1)}) fusion(f32[256,64]{0,1:T(8,128)S(1)} %tile.17, f32[192]{0:T(256)S(1)} %sub.182, f32[256]{0:T(256)S(1)} %get-tuple-element.86, bf16[64,16384]{1,0:T(8,128)(2,1)} %get-tuple-element.105, bf16[64,16384]{1,0:T(8,128)(2,1)S(1)} %bitcast.49, ...), kind=kOutput, calls=%fused_computation.111 | convolution fusion | flops 1629732608 | bytes 15141632 | tf_op jit(solution)/shard_map/dot_general | solution.py:187
  156.7 0.7 bitcast_select_fusion.w_ref
  157.5 6.4 %shard_map.93.acc_ref = f32[64,16384]{1,0:T(8,128)} custom-call(bf16[192,256]{1,0:T(8,128)(2,1)} %bitcast_select_fusion.w_ref, bf16[256,16512]{1,0:T(8,128)(2,1)} %bitcast.1.x_ref), custom_call_target="tpu_custom_call" | custom-call | flops 1610612736 | bytes 12681216 | tf_op jit(solution)/shard_map/pallas_call | solution.py:73
  163.9 5.4 %all-to-all-done.1 = bf16[32,2,16512]{2,1,0:T(2,128)(2,1)} async-done(((bf16[32,2,16512]{2,1,0:T(2,128)(2,1)}), bf16[32,2,16512]{2,1,0:T(2,128)(2,1)}, u32[]{:S(2)}, u32[]{:S(2)}) %all-to-all-start.1) | async-done | bytes 2113568 | tf_op jit(solution)/shard_map/all_to_all | solution.py:173
  169.3 4.1 %reshape.558.x_ref = bf16[64,16512]{1,0:T(8,128)(2,1)} reshape(bf16[32,2,16512]{2,1,0:T(2,128)(2,1)} %all-to-all-done.1) | data formatting | bytes 4227072 | tf_op jit(solution)/shard_map/reshape | solution.py:173
  173.4 1.0 convert_reduce_fusion.2
  174.6 5.1 %fusion.38 = (f32[64]{0:T(128)S(1)}, f32[64,192]{1,0:T(8,128)S(1)}, f32[64,192]{1,0:T(8,128)S(1)}) fusion(f32[64,192]{1,0:T(8,128)S(1)} %copy.88, f32[192]{0:T(256)S(1)} %sub.182, f32[64]{0:T(128)S(1)} %get-tuple-element.88, bf16[64,16384]{1,0:T(8,128)(2,1)} %get-tuple-element.105, bf16[64,16384]{1,0:T(8,128)(2,1)S(1)} %bitcast.50, ...), kind=kOutput, calls=%fused_computation.112 | convolution fusion | flops 421588928 | bytes 8537344 | tf_op jit(solution)/shard_map/dot_general | solution.py:187
  180.9 1.3 fusion.26
  183.1 0.7 copy.97.w_ref
  184.0 0.8 fusion.27
  184.9 0.6 copy-done.1
  185.5 5.4 %shard_map.94 = (bf16[16,16512]{1,0:T(8,128)(2,1)}, bf16[16,16512]{1,0:T(8,128)(2,1)}, bf16[16,16512]{1,0:T(8,128)(2,1)}, bf16[16,16512]{1,0:T(8,128)(2,1)}) custom-call(bf16[64,192]{1,0:T(8,128)(2,1)} %copy.97.w_ref, bf16[64,16512]{1,0:T(8,128)(2,1)} %reshape.558.x_ref, f32[64,16384]{1,0:T(8,128)} %shard_map.93.acc_ref, bf16[64,128]{1,0:T(8,128)(2,1)} %copy-done.1), custom_call_target="tpu_custom_call" | custom-call | flops 402653184 | bytes 8445952 | tf_op jit(solution)/shard_map/pallas_call | solution.py:97
  190.9 1.0 collective-permute-start.3
  192.4 2.3 %collective-permute-start.5 = (bf16[16,16512]{1,0:T(8,128)(2,1)}, bf16[16,16512]{1,0:T(8,128)(2,1)S(1)}, u32[]{:S(2)}, u32[]{:S(2)}) collective-permute-start(bf16[16,16512]{1,0:T(8,128)(2,1)} %get-tuple-element.57), channel_id=1, source_target_pairs={{0,3},{1,0},{2,1},{3,2},{4,7},{5,4},{6,5},{7,6},{8,11},{9,8},{10,9... | collective-permute-start | bytes 1585160 | tf_op jit(solution)/shard_map/ppermute | solution.py:127
  196.1 0.8 reshape.610
  196.9 3.9 %all-to-all-start.2 = ((f32[32,1,330]{2,1,0:T(1,128)}), f32[32,1,330]{2,1,0:T(1,128)S(1)}, u32[]{:S(2)}, u32[]{:S(2)}) async-start(f32[32,1,330]{2,1,0:T(1,128)} %reshape.610), calls=%async_computation.2 | async-start | bytes 98304 | tf_op jit(solution)/shard_map/all_to_all | solution.py:221
  200.8 7.4 %all-to-all-done.2 = f32[32,1,330]{2,1,0:T(1,128)S(1)} async-done(((f32[32,1,330]{2,1,0:T(1,128)}), f32[32,1,330]{2,1,0:T(1,128)S(1)}, u32[]{:S(2)}, u32[]{:S(2)}) %all-to-all-start.2) | async-done | bytes 42272 | tf_op jit(solution)/shard_map/all_to_all | solution.py:221
  208.7 0.8 reduce.44
  209.6 0.7 gather_fusion
  210.4 0.7 copy.98
  211.1 0.7 slice_reduce_fusion
  211.8 3.7 %collective-permute-done.3 = bf16[16,16512]{1,0:T(8,128)(2,1)S(1)} collective-permute-done((bf16[16,16512]{1,0:T(8,128)(2,1)}, bf16[16,16512]{1,0:T(8,128)(2,1)S(1)}, u32[]{:S(2)}, u32[]{:S(2)}) %collective-permute-start.3) | collective-permute-done | bytes 528416 | tf_op jit(solution)/shard_map/ppermute | solution.py:127
  215.5 0.6 collective-permute-done.5
  216.4 0.7 copy.99
  217.3 1.1 add.366
  (83 shorter events, 8.3 us)
Async XLA Ops:
  13.5 16.1 %copy-start.2 = (s32[2]{0:T(128)S(1)}, s32[2]{0:T(128)}, u32[]{:S(2)}) copy-start(s32[2]{0:T(128)} %param.17) | copy-start | bytes 28
  13.5 16.9 %collective-permute-start = (bf16[16,16384]{1,0:T(8,128)(2,1)S(1)}, bf16[16,16384]{1,0:T(8,128)(2,1)}, u32[]{:S(2)}, u32[]{:S(2)}) collective-permute-start(bf16[16,16384]{1,0:T(8,128)(2,1)S(1)} %reshape.555), channel_id=1, source_target_pairs={{0,1},{1,2},{2,3},{3,0},{4,5},{5,6},{6,7},{7,4},{8,9},{9,10},{10,1... | collective-permute-start | bytes 1572872 | tf_op jit(solution)/shard_map/ppermute | solution.py:127
  15.5 26.6 %collective-permute-start.1 = (bf16[16,16384]{1,0:T(8,128)(2,1)S(1)}, bf16[16,16384]{1,0:T(8,128)(2,1)}, u32[]{:S(2)}, u32[]{:S(2)}) collective-permute-start(bf16[16,16384]{1,0:T(8,128)(2,1)S(1)} %reshape.555), channel_id=1, source_target_pairs={{0,2},{1,3},{2,0},{3,1},{4,6},{5,7},{6,4},{7,5},{8,10},{9,11},{10,... | collective-permute-start | bytes 1572872 | tf_op jit(solution)/shard_map/ppermute | solution.py:127
  19.1 24.1 %collective-permute-start.2 = (bf16[16,16384]{1,0:T(8,128)(2,1)S(1)}, bf16[16,16384]{1,0:T(8,128)(2,1)S(1)}, u32[]{:S(2)}, u32[]{:S(2)}) collective-permute-start(bf16[16,16384]{1,0:T(8,128)(2,1)S(1)} %reshape.555), channel_id=1, source_target_pairs={{0,3},{1,0},{2,1},{3,2},{4,7},{5,4},{6,5},{7,6},{8,11},{9,8},{10,9... | collective-permute-start | bytes 1572872 | tf_op jit(solution)/shard_map/ppermute | solution.py:127
  20.1 114.2 %all-to-all-start = ((bf16[32,8,16512]{2,1,0:T(8,128)(2,1)}), bf16[32,8,16512]{2,1,0:T(8,128)(2,1)}, u32[]{:S(2)}, u32[]{:S(2)}) async-start(bf16[32,8,16512]{2,1,0:T(8,128)(2,1)} %fusion), calls=%async_computation | async-start | bytes 16908288 | tf_op jit(solution)/shard_map/all_to_all | solution.py:158
  134.3 35.0 %all-to-all-start.1 = ((bf16[32,2,16512]{2,1,0:T(2,128)(2,1)}), bf16[32,2,16512]{2,1,0:T(2,128)(2,1)}, u32[]{:S(2)}, u32[]{:S(2)}) async-start(bf16[32,2,16512]{2,1,0:T(2,128)(2,1)} %reshape.557), calls=%async_computation.1 | async-start | bytes 4227072 | tf_op jit(solution)/shard_map/all_to_all | solution.py:173
  184.9 0.6 copy-start.1
  190.9 25.3 %copy-start = (bf16[16,16512]{1,0:T(8,128)(2,1)S(1)}, bf16[16,16512]{1,0:T(8,128)(2,1)}, u32[]{:S(2)}) copy-start(bf16[16,16512]{1,0:T(8,128)(2,1)} %get-tuple-element.54) | copy-start | bytes 1585156
  190.9 24.6 %collective-permute-start.3 = (bf16[16,16512]{1,0:T(8,128)(2,1)}, bf16[16,16512]{1,0:T(8,128)(2,1)S(1)}, u32[]{:S(2)}, u32[]{:S(2)}) collective-permute-start(bf16[16,16512]{1,0:T(8,128)(2,1)} %get-tuple-element.55), channel_id=1, source_target_pairs={{0,1},{1,2},{2,3},{3,0},{4,5},{5,6},{6,7},{7,4},{8,9},{9,10},{10,1... | collective-permute-start | bytes 1585160 | tf_op jit(solution)/shard_map/ppermute | solution.py:127
  191.9 23.6 %collective-permute-start.4 = (bf16[16,16512]{1,0:T(8,128)(2,1)}, bf16[16,16512]{1,0:T(8,128)(2,1)S(1)}, u32[]{:S(2)}, u32[]{:S(2)}) collective-permute-start(bf16[16,16512]{1,0:T(8,128)(2,1)} %get-tuple-element.56), channel_id=1, source_target_pairs={{0,2},{1,3},{2,0},{3,1},{4,6},{5,7},{6,4},{7,5},{8,10},{9,11},{10,... | collective-permute-start | bytes 1585160 | tf_op jit(solution)/shard_map/ppermute | solution.py:127
  192.4 23.8 %collective-permute-start.5 = (bf16[16,16512]{1,0:T(8,128)(2,1)}, bf16[16,16512]{1,0:T(8,128)(2,1)S(1)}, u32[]{:S(2)}, u32[]{:S(2)}) collective-permute-start(bf16[16,16512]{1,0:T(8,128)(2,1)} %get-tuple-element.57), channel_id=1, source_target_pairs={{0,3},{1,0},{2,1},{3,2},{4,7},{5,4},{6,5},{7,6},{8,11},{9,8},{10,9... | collective-permute-start | bytes 1585160 | tf_op jit(solution)/shard_map/ppermute | solution.py:127
  196.9 11.3 %all-to-all-start.2 = ((f32[32,1,330]{2,1,0:T(1,128)}), f32[32,1,330]{2,1,0:T(1,128)S(1)}, u32[]{:S(2)}, u32[]{:S(2)}) async-start(f32[32,1,330]{2,1,0:T(1,128)} %reshape.610), calls=%async_computation.2 | async-start | bytes 98304 | tf_op jit(solution)/shard_map/all_to_all | solution.py:221
